TPU v7x, 256 devices: a whole 4x4x8 slice. The times are simulated.
256 devices in a mesh: grp: 8 (over z), dev: 32 (over x, y, core).
Axes of the slice: x: 4, y: 4, z: 8, core: 2. Of those that a mesh axis runs over, the one named last changes fastest.
Arguments:
- particles: bfloat16 [8192, 16384], P(('grp', 'dev')), may hold values from -60 to 60
- particle_precision: bfloat16 [8192], P(('grp', 'dev')), may hold values from 0.5 to 4
- particle_class: int32 [8192, 1], P(('grp', 'dev')), may hold values from 0 to 31; in each aligned block of 32 rows (0 to 31, 32 to 63, ...) at most 2 rows name the same one
- class_owner: int32 [32], replicated, may hold values from 0 to 31, each once
- references: bfloat16 [32, 48, 16384], P('dev'), may hold values from -0.08984375 to 0.08984375
- insert_weights: float32 [256, 48], P('dev'), may hold values from -0.875 to 0.875
Outputs:
- volume: float32 [256, 256, 256], P('grp', 'dev')
- evidence: float32 [8192], P(('grp', 'dev'))
Inputs may be any that keep to these rules, and one draw needn't show every extreme that they name: `particle_class`: within the 32 particles of one device no class appears more than 2 times, and some class does exactly 2 times.
All inputs are finite; a program needn't handle non-finite values.
Results may differ from a plain program's by a relative error of at most 0.0026.
Values may be sent and summed in bfloat16 or wider, within the bound.
No kernel may reach another device: no remote copies, remote signals or barrier semaphores. Data moves between devices by JAX's collectives and lax.ppermute only.
A program may use at most 128 MiB of HBM per device.

v0:
```python
import functools

import jax
import jax.numpy as jnp
from jax import lax
from jax.experimental import pallas as pl
from jax.experimental.pallas import tpu as pltpu
from jax.sharding import PartitionSpec as P

IMG = 128
VOL = 256
SHIFTS = (-1, 0, 1)
TK = 2048
TN = 1024


def upsample_table(length, source):
    target = jnp.arange(length, dtype=jnp.int32)[:, None]
    anchor = jnp.arange(source, dtype=jnp.int32)[None, :]
    halves = target // 2
    lower = anchor == halves
    upper = anchor == (halves + 1) % source
    is_even = target % 2 == 0
    even_part = jnp.where(lower, 1.0, 0.0)
    odd_part = jnp.where(lower, 0.5, 0.0) + jnp.where(upper, 0.5, 0.0)
    return jnp.where(is_even, even_part, odd_part).astype(jnp.float32)


def local_table(rows, anchors):
    target = jnp.arange(rows, dtype=jnp.int32)[:, None]
    anchor = jnp.arange(anchors, dtype=jnp.int32)[None, :]
    halves = target // 2
    lower = anchor == halves
    upper = anchor == halves + 1
    is_even = target % 2 == 0
    even_part = jnp.where(lower, 1.0, 0.0)
    odd_part = jnp.where(lower, 0.5, 0.0) + jnp.where(upper, 0.5, 0.0)
    return jnp.where(is_even, even_part, odd_part).astype(jnp.float32)


def class_kernel(pix, rows_ref, ref_ref, scale_ref, energy_ref, sums_ref, evid_ref,
                 ext_ref, acc_ref, w_ref):
    chunks = pix // IMG

    def build(u, carry):
        off = pl.multiple_of(u * IMG, IMG)
        dst = pl.multiple_of(off + IMG, IMG)
        chunk = rows_ref[:, pl.ds(off, IMG)]
        wide = chunk.astype(jnp.float32)
        ext_ref[0, :, pl.ds(dst, IMG)] = pltpu.roll(wide, IMG - 1, 1).astype(jnp.bfloat16)
        ext_ref[1, :, pl.ds(dst, IMG)] = chunk
        ext_ref[2, :, pl.ds(dst, IMG)] = pltpu.roll(wide, 1, 1).astype(jnp.bfloat16)
        return carry

    lax.fori_loop(0, chunks, build, 0, unroll=8)
    ext_ref[:, :, 0:IMG] = ext_ref[:, :, pix:pix + IMG]
    ext_ref[:, :, pix + IMG:pix + 2 * IMG] = ext_ref[:, :, IMG:2 * IMG]

    acc_ref[...] = jnp.zeros_like(acc_ref)

    def products(j, carry):
        k0 = pl.multiple_of(j * TK, TK)
        tile = ref_ref[:, pl.ds(k0, TK)]
        for ai, a in enumerate(SHIFTS):
            start = pl.multiple_of(k0 + IMG * (1 - a), IMG)
            for bi in range(3):
                moved = ext_ref[bi, :, pl.ds(start, TK)]
                acc_ref[ai * 3 + bi] += lax.dot_general(
                    tile, moved, (((1,), (1,)), ((), ())), preferred_element_type=jnp.float32
                )
        return carry

    lax.fori_loop(0, pix // TK, products, 0)

    scale = scale_ref[...]
    half_energy = 0.5 * energy_ref[...]
    scores = [scale * (acc_ref[t] - half_energy) for t in range(9)]
    highest = jnp.max(scores[0], axis=0, keepdims=True)
    for t in range(1, 9):
        highest = jnp.maximum(highest, jnp.max(scores[t], axis=0, keepdims=True))
    total = jnp.sum(jnp.exp(scores[0] - highest), axis=0, keepdims=True)
    for t in range(1, 9):
        total = total + jnp.sum(jnp.exp(scores[t] - highest), axis=0, keepdims=True)
    evidence = highest + jnp.log(total)
    evid_ref[...] = evidence
    for t in range(9):
        w_ref[t] = jnp.exp(scores[t] - evidence).astype(jnp.bfloat16)

    def class_sums(j, carry):
        n0 = pl.multiple_of(j * TN, TN)
        summed = jnp.zeros(sums_ref[:, pl.ds(0, TN)].shape, jnp.float32)
        for ai, a in enumerate(SHIFTS):
            start = pl.multiple_of(n0 + IMG * (1 - a), IMG)
            for bi in range(3):
                summed = summed + jnp.dot(
                    w_ref[ai * 3 + bi], ext_ref[bi, :, pl.ds(start, TN)],
                    preferred_element_type=jnp.float32,
                )
        sums_ref[:, pl.ds(n0, TN)] = summed
        return carry

    lax.fori_loop(0, pix // TN, class_sums, 0)


def class_pass(rows_ext, templates, scale_row, energy_col, pix):
    rowcount = rows_ext.shape[0]
    refcount = templates.shape[0]
    vmem = pl.BlockSpec(memory_space=pltpu.VMEM)
    flops = 2 * 2 * 9 * refcount * rowcount * pix
    cost = pl.CostEstimate(
        flops=flops, transcendentals=10 * refcount * rowcount,
        bytes_accessed=rows_ext.size * 2 + templates.size * 2 + refcount * pix * 4,
    )
    return pl.pallas_call(
        functools.partial(class_kernel, pix),
        out_shape=(
            jax.ShapeDtypeStruct((refcount, pix), jnp.float32),
            jax.ShapeDtypeStruct((1, rowcount), jnp.float32),
        ),
        in_specs=[vmem] * 4,
        out_specs=(vmem, vmem),
        scratch_shapes=[
            pltpu.VMEM((3, rowcount, pix + 2 * IMG), jnp.bfloat16),
            pltpu.VMEM((9, refcount, rowcount), jnp.float32),
            pltpu.VMEM((9, refcount, rowcount), jnp.bfloat16),
        ],
        compiler_params=pltpu.CompilerParams(vmem_limit_bytes=48 * 1024 * 1024),
        cost_estimate=cost,
    )(rows_ext, templates, scale_row, energy_col)


def on_device(
    particles, particle_precision, particle_class, class_owner, references, insert_weights
):
    sources = lax.axis_size("dev")
    groups = lax.axis_size("grp")
    local_count, pix = particles.shape
    classes = class_owner.shape[0]
    owned_classes = references.shape[0]
    slot_depth = max(2, 2 * local_count // classes)
    labels = particle_class[:, 0]
    catalog = jnp.arange(classes, dtype=jnp.int32)
    position = jnp.sum(
        jnp.where(labels[:, None] == catalog[None, :], class_owner[None, :], 0), axis=1
    )
    ordinal = jnp.arange(local_count, dtype=jnp.int32)
    earlier = (labels[:, None] == labels[None, :]) & (ordinal[None, :] < ordinal[:, None])
    arrival = jnp.sum(earlier, axis=1)
    slot_index = position * slot_depth + arrival
    total_slots = classes * slot_depth
    placing = (jnp.arange(total_slots, dtype=jnp.int32)[:, None] == slot_index[None, :]).astype(
        jnp.bfloat16
    )
    extra = jnp.broadcast_to(particle_precision[:, None], (local_count, IMG))
    carried = jnp.concatenate([particles, extra], axis=1)
    width = pix + IMG
    outgoing = jnp.dot(placing, carried, preferred_element_type=jnp.float32).astype(jnp.bfloat16)
    outgoing = outgoing.reshape(sources, owned_classes * slot_depth, width)
    arrived = lax.all_to_all(outgoing, "dev", split_axis=0, concat_axis=0, tiled=True)
    rows_ext = arrived.reshape(sources * slot_depth, width)
    scale_row = rows_ext[:, pix].astype(jnp.float32).reshape(1, sources * slot_depth)
    templates = references[0]
    energy_col = jnp.sum(jnp.square(templates.astype(jnp.float32)), axis=1).reshape(-1, 1)
    summed, class_evidence = class_pass(rows_ext, templates, scale_row, energy_col, pix)
    stacked = class_evidence.reshape(sources, owned_classes * slot_depth)
    returned = lax.all_to_all(stacked, "dev", split_axis=0, concat_axis=0, tiled=True).reshape(
        total_slots
    )
    particle_evidence = jnp.take(returned, slot_index)
    planes = jnp.dot(
        insert_weights, summed, precision=lax.Precision.HIGHEST, preferred_element_type=jnp.float32
    )
    depth = planes.shape[0]
    planes = planes.reshape(depth, IMG, IMG)
    band = IMG // groups
    wrapped = jnp.concatenate([planes, planes[:, :1]], axis=1)
    windows = jnp.stack([wrapped[:, g * band:g * band + band + 1] for g in range(groups)], 0)
    mine = lax.psum_scatter(windows, "grp", scatter_dimension=0, tiled=True)[0]
    interp = upsample_table(VOL, IMG)
    across = jnp.einsum("zjv,xv->zjx", mine, interp, precision=lax.Precision.HIGHEST)
    rows_table = local_table(2 * band, band + 1)
    volume = jnp.einsum("yj,zjx->yzx", rows_table, across, precision=lax.Precision.HIGHEST)
    return (volume, particle_evidence)


def solution(mesh):
    placed = (
        P(("grp", "dev"), None),
        P(("grp", "dev")),
        P(("grp", "dev"), None),
        P(),
        P("dev", None, None),
        P("dev", None),
    )
    return jax.shard_map(
        on_device,
        mesh=mesh,
        in_specs=placed,
        out_specs=(P("grp", "dev", None), P(("grp", "dev"))),
        check_vma=False,
    )
```

profile of v0, /device:TPU:8, one launch (start us, length us, event | category | flops | bytes accessed | tf_op | source)
XLA Modules:
  0.0 120.6 jit_solution(3445368874612873297)
XLA Ops:
  7.2 0.0 copy-start
  7.2 0.9 select_reduce_fusion
  8.1 0.7 broadcast_in_dim.84
  8.8 1.9 %convolution_convert_fusion = bf16[64,16512]{1,0:T(8,128)(2,1)S(1)} fusion(bf16[32,128]{1,0:T(8,128)(2,1)S(1)} %broadcast_in_dim.84, bf16[32,16384]{1,0:T(8,128)(2,1)} %param.6, s32[32]{0:T(128)S(1)} %get-tuple-element.17), kind=kOutput, calls=%fused_computation.1 | convolution fusion | flops 70805504 | bytes 3170432 | tf_op jit(solution)/shard_map/dot_general | solution.py:157
  10.7 2.2 %reshape.209 = bf16[32,2,16512]{2,1,0:T(2,128)(2,1)} reshape(bf16[64,16512]{1,0:T(8,128)(2,1)S(1)} %convolution_convert_fusion) | data formatting | bytes 4227072 | tf_op jit(solution)/shard_map/reshape | solution.py:158
  13.0 0.0 copy-start.1
  13.0 7.7 %all-to-all-start = ((bf16[32,2,16512]{2,1,0:T(2,128)(2,1)}), bf16[32,2,16512]{2,1,0:T(2,128)(2,1)}, u32[]{:S(2)}, u32[]{:S(2)}) async-start(bf16[32,2,16512]{2,1,0:T(2,128)(2,1)} %reshape.209), calls=%async_computation | async-start | bytes 4227072 | tf_op jit(solution)/shard_map/all_to_all | solution.py:159
  20.7 0.0 reduce-scatter.4.cloned.1.call-start
  20.8 0.0 copy-done.1
  20.8 0.4 multiply_reduce_fusion
  21.2 0.1 copy.16.energy_ref
  21.3 26.6 %all-to-all-done = bf16[32,2,16512]{2,1,0:T(2,128)(2,1)} async-done(((bf16[32,2,16512]{2,1,0:T(2,128)(2,1)}), bf16[32,2,16512]{2,1,0:T(2,128)(2,1)}, u32[]{:S(2)}, u32[]{:S(2)}) %all-to-all-start) | async-done | bytes 2113568 | tf_op jit(solution)/shard_map/all_to_all | solution.py:159
  47.9 2.7 %reshape.210.rows_ref = bf16[64,16512]{1,0:T(8,128)(2,1)S(1)} reshape(bf16[32,2,16512]{2,1,0:T(2,128)(2,1)} %all-to-all-done) | data formatting | bytes 4227072 | tf_op jit(solution)/shard_map/reshape | solution.py:160
  50.6 0.1 convert_reduce_fusion
  50.7 0.0 copy-start.2
  50.7 1.4 %copy-done.2 = bf16[1,48,16384]{2,1,0:T(8,128)(2,1)S(1)} copy-done((bf16[1,48,16384]{2,1,0:T(8,128)(2,1)S(1)}, bf16[1,48,16384]{2,1,0:T(8,128)(2,1)}, u32[]{:S(2)}) %copy-start.2) | copy-done | bytes 1572888
  52.1 16.1 %shard_map.77 = (f32[48,16384]{1,0:T(8,128)}, f32[1,64]{1,0:T(1,128)S(1)}) custom-call(bf16[64,16512]{1,0:T(8,128)(2,1)S(1)} %reshape.210.rows_ref, bf16[48,16384]{1,0:T(8,128)(2,1)S(1)} %bitcast.57, f32[1,64]{1,0:T(1,128)S(1)} %bitcast.58, f32[48,1]{1,0:T(8,128)S(1)} %copy.16.energy_ref), custom_call_target="tpu_custom_call" | custom-call | flops 1811939328 | bytes 6832128 | tf_op jit(solution)/shard_map/pallas_call | solution.py:114
  68.3 0.0 copy-done
  68.3 3.6 %convolution_bitcast_fusion = f32[8,128,128]{2,0,1:T(8,128)S(1)} fusion(f32[48,16384]{1,0:T(8,128)} %get-tuple-element.4, f32[8,48]{1,0:T(8,128)S(1)} %copy-done), kind=kOutput, calls=%fused_computation.3 | convolution fusion | flops 75497472 | bytes 3671552 | tf_op jit(solution)/shard_map/dot_general | solution.py:170
  72.0 0.0 copy-start.3
  72.0 0.8 copy-done.3
  72.8 0.0 reduce-scatter.4.cloned.1.call-update
  72.9 0.5 broadcast.270
  73.4 0.7 reduce.8
  74.1 0.7 all_to_all.10
  74.8 5.8 %all-to-all-start.1 = ((f32[32,1,2]{2,1,0:T(1,128)}), f32[32,1,2]{2,1,0:T(1,128)S(1)}, u32[]{:S(2)}, u32[]{:S(2)}) async-start(f32[32,1,2]{2,1,0:T(1,128)} %bitcast.17), calls=%async_computation.1 | async-start | bytes 32768 | tf_op jit(solution)/shard_map/all_to_all | solution.py:166
  80.6 6.2 %all-to-all-done.1 = f32[32,1,2]{2,1,0:T(1,128)S(1)} async-done(((f32[32,1,2]{2,1,0:T(1,128)}), f32[32,1,2]{2,1,0:T(1,128)S(1)}, u32[]{:S(2)}, u32[]{:S(2)}) %all-to-all-start.1) | async-done | bytes 288 | tf_op jit(solution)/shard_map/all_to_all | solution.py:166
  86.7 0.7 reduce.9
  87.4 0.1 reshape.213
  87.5 0.7 gather_fusion
  88.2 0.5 and_select_fusion
  88.8 22.3 %reduce-scatter.4.cloned.1.call-done = f32[1,8,17,128]{3,1,2,0:T(8,128)} async-done(((f32[8,8,17,128]{3,1,2,0:T(8,128)}), f32[1,8,17,128]{3,1,2,0:T(8,128)}) %reduce-scatter.4.cloned.1.call-update) | async-done | bytes 69648
  111.1 1.3 %fusion.7 = f32[8,17,256]{2,1,0:T(8,128)S(1)} fusion(f32[8,17,128]{2,0,1:T(8,128)} %bitcast.61, s32[256]{0:T(256)S(1)} %get-tuple-element.18, s32[256]{0:T(256)S(1)} %get-tuple-element.19, pred[256]{0:T(512)(128)(4,1)S(1)} %fusion.47), kind=kOutput, calls=%fused_computation.13 | convolution fusion | flops 53706752 | bytes 211200 | tf_op jit(solution)/shard_map/zjv,xv->zjx/dot_general | solution.py:180
  112.5 0.4 fusion.34
  112.9 0.9 copy.19
  (15 shorter events, 0.1 us)
Async XLA Ops:
  7.2 61.1 %copy-start = (f32[8,48]{1,0:T(8,128)S(1)}, f32[8,48]{1,0:T(8,128)}, u32[]{:S(2)}) copy-start(f32[8,48]{1,0:T(8,128)} %param.11) | copy-start | bytes 4612
  13.0 7.8 %copy-start.1 = (bf16[1,48,16384]{2,1,0:T(8,128)(2,1)S(1)}, bf16[1,48,16384]{2,1,0:T(8,128)(2,1)}, u32[]{:S(2)}) copy-start(bf16[1,48,16384]{2,1,0:T(8,128)(2,1)} %param.10) | copy-start | bytes 4718596
  13.0 34.9 %all-to-all-start = ((bf16[32,2,16512]{2,1,0:T(2,128)(2,1)}), bf16[32,2,16512]{2,1,0:T(2,128)(2,1)}, u32[]{:S(2)}, u32[]{:S(2)}) async-start(bf16[32,2,16512]{2,1,0:T(2,128)(2,1)} %reshape.209), calls=%async_computation | async-start | bytes 4227072 | tf_op jit(solution)/shard_map/all_to_all | solution.py:159
  20.7 90.4 %reduce-scatter.4.cloned.1.call-start = ((), (), s32[]{:S(2)}) async-start(), calls=%async_computation.3 | async-start | bytes 626688
  50.7 1.4 %copy-start.2 = (bf16[1,48,16384]{2,1,0:T(8,128)(2,1)S(1)}, bf16[1,48,16384]{2,1,0:T(8,128)(2,1)}, u32[]{:S(2)}) copy-start(bf16[1,48,16384]{2,1,0:T(8,128)(2,1)} %param.10) | copy-start | bytes 4718596
  72.0 0.8 copy-start.3
  74.8 12.0 %all-to-all-start.1 = ((f32[32,1,2]{2,1,0:T(1,128)}), f32[32,1,2]{2,1,0:T(1,128)S(1)}, u32[]{:S(2)}, u32[]{:S(2)}) async-start(f32[32,1,2]{2,1,0:T(1,128)} %bitcast.17), calls=%async_computation.1 | async-start | bytes 32768 | tf_op jit(solution)/shard_map/all_to_all | solution.py:166
Sparse Core Ops, SparseCore 0:
  73.0 38.1 reduce-scatter.3
where the time goes:
time: 121 us
  waiting for transfers between devices  55.1 us (46%)
  Pallas kernels  16.1 us (13%)
  between operations  14.2 us (12%)
  starting transfers between devices  13.5 us (11%)
  local copies, waits for them, and re-layouts  11 us (9%)
  matrix products  7.3 us (6%)
  other arithmetic  3.34 us (3%)
    all_to_all x1, waiting for transfers between devices, on_device(): lax.all_to_all(outgoing, 'dev', split_axis=0, concat_axis=0, tiled=True)  26.6 us
    unnamed x2, waiting for transfers between devices  22.4 us
    pallas_call x1, Pallas kernels, class_pass(): pl.pallas_call(functools.partial(class_kernel, pix), out_shape=(jax.Shape...  16.1 us
    all_to_all x1, starting transfers between devices, on_device(): lax.all_to_all(outgoing, 'dev', split_axis=0, concat_axis=0, tiled=True)  7.72 us
    all_to_all x1, waiting for transfers between devices, on_device(): lax.all_to_all(stacked, 'dev', split_axis=0, concat_axis=0, tiled=True)  6.16 us
    all_to_all x1, starting transfers between devices, on_device(): lax.all_to_all(stacked, 'dev', split_axis=0, concat_axis=0, tiled=True)  5.78 us
    dot_general x1, matrix products, on_device(): jnp.dot(insert_weights, summed, precision=lax.Precision.HIGHEST, preferre...  3.63 us
    unnamed x16, local copies, waits for them, and re-layouts  3.11 us
  transfers between devices with their start and end apart: 3, of which 3 were waited for; matrix products, arithmetic and copies ran while one was open for 3% of the time, Pallas kernels for 0%

commit v1 on v0

--- a/solution.py
+++ b/solution.py
@@ -38,8 +38,8 @@
     return jnp.where(is_even, even_part, odd_part).astype(jnp.float32)
 
 
-def class_kernel(pix, rows_ref, ref_ref, scale_ref, energy_ref, sums_ref, evid_ref,
-                 ext_ref, acc_ref, w_ref):
+def class_kernel(pix, rows_ref, ref_ref, scale_ref, energy_ref, gain_ref, planes_ref, evid_ref,
+                 ext_ref, acc_ref, v_ref):
     chunks = pix // IMG
 
     def build(u, carry):
@@ -83,50 +83,61 @@
         total = total + jnp.sum(jnp.exp(scores[t] - highest), axis=0, keepdims=True)
     evidence = highest + jnp.log(total)
     evid_ref[...] = evidence
+    gain = gain_ref[...]
+    gain_hi = gain.astype(jnp.bfloat16)
+    gain_lo = (gain - gain_hi.astype(jnp.float32)).astype(jnp.bfloat16)
+    depth = gain.shape[0]
     for t in range(9):
-        w_ref[t] = jnp.exp(scores[t] - evidence).astype(jnp.bfloat16)
-
-    def class_sums(j, carry):
+        weights = jnp.exp(scores[t] - evidence).astype(jnp.bfloat16)
+        mixed = jnp.dot(gain_hi, weights, preferred_element_type=jnp.float32) + jnp.dot(
+            gain_lo, weights, preferred_element_type=jnp.float32
+        )
+        mixed_hi = mixed.astype(jnp.bfloat16).astype(jnp.float32)
+        v_ref[t, 0:depth] = mixed_hi
+        v_ref[t, depth:2 * depth] = mixed - mixed_hi
+
+    def plane_tiles(j, carry):
         n0 = pl.multiple_of(j * TN, TN)
-        summed = jnp.zeros(sums_ref[:, pl.ds(0, TN)].shape, jnp.float32)
+        summed = jnp.zeros((2 * depth, TN), jnp.float32)
         for ai, a in enumerate(SHIFTS):
             start = pl.multiple_of(n0 + IMG * (1 - a), IMG)
             for bi in range(3):
                 summed = summed + jnp.dot(
-                    w_ref[ai * 3 + bi], ext_ref[bi, :, pl.ds(start, TN)],
+                    v_ref[ai * 3 + bi].astype(jnp.bfloat16), ext_ref[bi, :, pl.ds(start, TN)],
                     preferred_element_type=jnp.float32,
                 )
-        sums_ref[:, pl.ds(n0, TN)] = summed
+        planes_ref[:, pl.ds(n0, TN)] = summed[0:depth] + summed[depth:2 * depth]
         return carry
 
-    lax.fori_loop(0, pix // TN, class_sums, 0)
-
-
-def class_pass(rows_ext, templates, scale_row, energy_col, pix):
+    lax.fori_loop(0, pix // TN, plane_tiles, 0)
+
+
+def class_pass(rows_ext, templates, scale_row, energy_col, gain, pix):
     rowcount = rows_ext.shape[0]
     refcount = templates.shape[0]
+    depth = gain.shape[0]
     vmem = pl.BlockSpec(memory_space=pltpu.VMEM)
-    flops = 2 * 2 * 9 * refcount * rowcount * pix
+    flops = 2 * 9 * (refcount + 2 * depth) * rowcount * pix
     cost = pl.CostEstimate(
         flops=flops, transcendentals=10 * refcount * rowcount,
-        bytes_accessed=rows_ext.size * 2 + templates.size * 2 + refcount * pix * 4,
+        bytes_accessed=rows_ext.size * 2 + templates.size * 2 + depth * pix * 4,
     )
     return pl.pallas_call(
         functools.partial(class_kernel, pix),
         out_shape=(
-            jax.ShapeDtypeStruct((refcount, pix), jnp.float32),
+            jax.ShapeDtypeStruct((depth, pix), jnp.float32),
             jax.ShapeDtypeStruct((1, rowcount), jnp.float32),
         ),
-        in_specs=[vmem] * 4,
+        in_specs=[vmem] * 5,
         out_specs=(vmem, vmem),
         scratch_shapes=[
             pltpu.VMEM((3, rowcount, pix + 2 * IMG), jnp.bfloat16),
             pltpu.VMEM((9, refcount, rowcount), jnp.float32),
-            pltpu.VMEM((9, refcount, rowcount), jnp.bfloat16),
+            pltpu.VMEM((9, 2 * depth, rowcount), jnp.float32),
         ],
         compiler_params=pltpu.CompilerParams(vmem_limit_bytes=48 * 1024 * 1024),
         cost_estimate=cost,
-    )(rows_ext, templates, scale_row, energy_col)
+    )(rows_ext, templates, scale_row, energy_col, gain)
 
 
 def on_device(
@@ -146,7 +157,7 @@
     ordinal = jnp.arange(local_count, dtype=jnp.int32)
     earlier = (labels[:, None] == labels[None, :]) & (ordinal[None, :] < ordinal[:, None])
     arrival = jnp.sum(earlier, axis=1)
-    slot_index = position * slot_depth + arrival
+    slot_index = arrival * classes + position
     total_slots = classes * slot_depth
     placing = (jnp.arange(total_slots, dtype=jnp.int32)[:, None] == slot_index[None, :]).astype(
         jnp.bfloat16
@@ -155,27 +166,26 @@
     carried = jnp.concatenate([particles, extra], axis=1)
     width = pix + IMG
     outgoing = jnp.dot(placing, carried, preferred_element_type=jnp.float32).astype(jnp.bfloat16)
-    outgoing = outgoing.reshape(sources, owned_classes * slot_depth, width)
-    arrived = lax.all_to_all(outgoing, "dev", split_axis=0, concat_axis=0, tiled=True)
-    rows_ext = arrived.reshape(sources * slot_depth, width)
-    scale_row = rows_ext[:, pix].astype(jnp.float32).reshape(1, sources * slot_depth)
+    outgoing = outgoing.reshape(slot_depth, sources, owned_classes * width)
+    arrived = lax.all_to_all(outgoing, "dev", split_axis=1, concat_axis=1, tiled=True)
+    rows_ext = arrived.reshape(slot_depth * sources, width)
+    scale_row = rows_ext[:, pix].astype(jnp.float32).reshape(1, slot_depth * sources)
     templates = references[0]
     energy_col = jnp.sum(jnp.square(templates.astype(jnp.float32)), axis=1).reshape(-1, 1)
-    summed, class_evidence = class_pass(rows_ext, templates, scale_row, energy_col, pix)
-    stacked = class_evidence.reshape(sources, owned_classes * slot_depth)
-    returned = lax.all_to_all(stacked, "dev", split_axis=0, concat_axis=0, tiled=True).reshape(
+    planes, class_evidence = class_pass(
+        rows_ext, templates, scale_row, energy_col, insert_weights, pix
+    )
+    stacked = class_evidence.reshape(slot_depth, sources)
+    returned = lax.all_to_all(stacked, "dev", split_axis=1, concat_axis=1, tiled=True).reshape(
         total_slots
     )
     particle_evidence = jnp.take(returned, slot_index)
-    planes = jnp.dot(
-        insert_weights, summed, precision=lax.Precision.HIGHEST, preferred_element_type=jnp.float32
-    )
     depth = planes.shape[0]
     planes = planes.reshape(depth, IMG, IMG)
     band = IMG // groups
     wrapped = jnp.concatenate([planes, planes[:, :1]], axis=1)
     windows = jnp.stack([wrapped[:, g * band:g * band + band + 1] for g in range(groups)], 0)
-    mine = lax.psum_scatter(windows, "grp", scatter_dimension=0, tiled=True)[0]
+    mine = jnp.sum(lax.all_to_all(windows, "grp", split_axis=0, concat_axis=0, tiled=True), 0)
     interp = upsample_table(VOL, IMG)
     across = jnp.einsum("zjv,xv->zjx", mine, interp, precision=lax.Precision.HIGHEST)
     rows_table = local_table(2 * band, band + 1)

time: 121 us -> 106 us (0.88)
  the two profiles are of different devices: /device:TPU:8 before, /device:TPU:1 now
where the time goes in v1:
time: 106 us
  waiting for transfers between devices  51.6 us (49%)
  starting transfers between devices  21.3 us (20%)
  Pallas kernels  13.1 us (12%)
  local copies, waits for them, and re-layouts  13 us (12%)
  other arithmetic  3.31 us (3%)
  matrix products  2.79 us (3%)
    all_to_all x1, waiting for transfers between devices, on_device(): lax.all_to_all(outgoing, 'dev', split_axis=1, concat_axis=1, tiled=True)  28 us
    all_to_all x1, waiting for transfers between devices, on_device(): lax.all_to_all(windows, 'grp', split_axis=0, concat_axis=0, tiled=True)  17.2 us
    pallas_call x1, Pallas kernels, class_pass(): pl.pallas_call(functools.partial(class_kernel, pix), out_shape=(jax.Shape...  13.1 us
    all_to_all x1, starting transfers between devices, on_device(): lax.all_to_all(outgoing, 'dev', split_axis=1, concat_axis=1, tiled=True)  8.77 us
    all_to_all x1, starting transfers between devices, on_device(): lax.all_to_all(windows, 'grp', split_axis=0, concat_axis=0, tiled=True)  8.18 us
    all_to_all x1, waiting for transfers between devices, on_device(): lax.all_to_all(stacked, 'dev', split_axis=1, concat_axis=1, tiled=True)  6.35 us
    unnamed x12, local copies, waits for them, and re-layouts  5.28 us
    all_to_all x1, starting transfers between devices, on_device(): lax.all_to_all(stacked, 'dev', split_axis=1, concat_axis=1, tiled=True)  4.36 us
  transfers between devices with their start and end apart: 3, of which 3 were waited for; matrix products, arithmetic and copies ran while one was open for 2% of the time, Pallas kernels for 0%

profile of v1, /device:TPU:1, one launch (start us, length us, event | category | flops | bytes accessed | tf_op | source)
XLA Modules:
  0.0 105.8 jit_solution(10966876019941614271)
XLA Ops:
  0.6 0.9 convert_reduce_fusion.1
  1.6 0.7 broadcast_in_dim.84
  2.3 1.9 %convolution_convert_fusion = bf16[64,16512]{1,0:T(8,128)(2,1)S(1)} fusion(bf16[32,128]{1,0:T(8,128)(2,1)S(1)} %broadcast_in_dim.84, bf16[32,16384]{1,0:T(8,128)(2,1)} %param.6, s32[32]{0:T(128)S(1)} %get-tuple-element.17), kind=kOutput, calls=%fused_computation.1 | convolution fusion | flops 70805504 | bytes 3170432 | tf_op jit(solution)/shard_map/dot_general | solution.py:168
  4.2 2.9 %copy.19 = bf16[2,32,16512]{2,0,1:T(2,128)(2,1)} copy(bf16[2,32,16512]{2,1,0:T(8,128)(2,1)S(1)} %bitcast.66) | data formatting | bytes 4227072 | tf_op jit(solution)/shard_map/reshape | solution.py:169
  7.1 0.0 copy-start
  7.1 8.8 %all-to-all-start = ((bf16[2,32,16512]{2,0,1:T(2,128)(2,1)}), bf16[2,32,16512]{2,0,1:T(2,128)(2,1)}, u32[]{:S(2)}, u32[]{:S(2)}) async-start(bf16[2,32,16512]{2,0,1:T(2,128)(2,1)} %copy.19), calls=%async_computation | async-start | bytes 4227072 | tf_op jit(solution)/shard_map/all_to_all | solution.py:170
  15.9 0.0 copy-done
  15.9 0.4 multiply_reduce_fusion
  16.3 0.1 copy.21.energy_ref
  16.4 0.0 copy-start.1
  16.4 28.0 %all-to-all-done = bf16[2,32,16512]{2,0,1:T(2,128)(2,1)} async-done(((bf16[2,32,16512]{2,0,1:T(2,128)(2,1)}), bf16[2,32,16512]{2,0,1:T(2,128)(2,1)}, u32[]{:S(2)}, u32[]{:S(2)}) %all-to-all-start) | async-done | bytes 2113568 | tf_op jit(solution)/shard_map/all_to_all | solution.py:170
  44.4 1.8 %copy.20 = bf16[2,32,16512]{2,1,0:T(8,128)(2,1)S(1)} copy(bf16[2,32,16512]{2,0,1:T(2,128)(2,1)} %all-to-all-done) | data formatting | bytes 4227072 | tf_op jit(solution)/shard_map/all_to_all | solution.py:170
  46.2 0.1 convert_reduce_fusion
  46.4 0.0 copy-done.1
  46.4 13.1 %shard_map.77 = (f32[8,16384]{1,0:T(8,128)S(1)}, f32[1,64]{1,0:T(1,128)S(1)}) custom-call(bf16[64,16512]{1,0:T(8,128)(2,1)S(1)} %bitcast.54, bf16[48,16384]{1,0:T(8,128)(2,1)S(1)} %bitcast.64, f32[1,64]{1,0:T(1,128)S(1)} %bitcast.65, f32[48,1]{1,0:T(8,128)S(1)} %copy.21.energy_ref, f32[8,48]{1,0:T(8,128)S(1)} %copy-done.1), custom_call_target="tpu_custom_call" | custom-call | flops 1207959552 | bytes 4210688 | tf_op jit(solution)/shard_map/pallas_call | solution.py:125
  59.5 0.6 fusion.21
  60.1 0.6 fusion.20
  60.8 0.6 fusion.19
  61.4 0.6 fusion.18
  62.0 0.6 fusion.17
  62.7 0.6 fusion.16
  63.3 0.6 fusion.15
  63.9 0.5 broadcast.267
  64.4 0.7 reduce.5
  65.1 0.1 all_to_all.14
  65.2 0.7 copy.23
  65.9 4.4 %all-to-all-start.2 = ((f32[2,32,1]{0,2,1:T(1,128)}), f32[2,32,1]{0,2,1:T(1,128)S(1)}, u32[]{:S(2)}, u32[]{:S(2)}) async-start(f32[2,32,1]{0,2,1:T(1,128)} %copy.23), calls=%async_computation.2 | async-start | bytes 32768 | tf_op jit(solution)/shard_map/all_to_all | solution.py:179
  70.2 0.6 fusion.14
  70.9 6.3 %all-to-all-done.2 = f32[2,32,1]{0,2,1:T(1,128)S(1)} async-done(((f32[2,32,1]{0,2,1:T(1,128)}), f32[2,32,1]{0,2,1:T(1,128)S(1)}, u32[]{:S(2)}, u32[]{:S(2)}) %all-to-all-start.2) | async-done | bytes 288 | tf_op jit(solution)/shard_map/all_to_all | solution.py:179
  77.2 8.2 %all-to-all-start.1 = ((f32[8,8,17,128]{3,1,2,0:T(8,128)}), f32[8,8,17,128]{3,1,2,0:T(8,128)S(1)}, u32[]{:S(2)}, u32[]{:S(2)}) async-start(f32[8,8,17,128]{3,1,2,0:T(8,128)} %fusion.14), calls=%async_computation.1 | async-start | bytes 1114112 | tf_op jit(solution)/shard_map/all_to_all | solution.py:188
  85.4 0.1 copy.24
  85.5 0.1 reshape.213
  85.6 0.7 gather_fusion
  86.3 0.5 and_select_fusion
  86.8 17.2 %all-to-all-done.1 = f32[8,8,17,128]{3,1,2,0:T(8,128)S(1)} async-done(((f32[8,8,17,128]{3,1,2,0:T(8,128)}), f32[8,8,17,128]{3,1,2,0:T(8,128)S(1)}, u32[]{:S(2)}, u32[]{:S(2)}) %all-to-all-start.1) | async-done | bytes 557088 | tf_op jit(solution)/shard_map/all_to_all | solution.py:188
  104.1 0.5 fusion.7
  104.5 0.4 fusion.34
  105.0 0.9 copy.25
  (8 shorter events, 0.1 us)
Async XLA Ops:
  7.1 8.8 %copy-start = (bf16[1,48,16384]{2,1,0:T(8,128)(2,1)S(1)}, bf16[1,48,16384]{2,1,0:T(8,128)(2,1)}, u32[]{:S(2)}) copy-start(bf16[1,48,16384]{2,1,0:T(8,128)(2,1)} %param.10) | copy-start | bytes 4718596
  7.1 37.3 %all-to-all-start = ((bf16[2,32,16512]{2,0,1:T(2,128)(2,1)}), bf16[2,32,16512]{2,0,1:T(2,128)(2,1)}, u32[]{:S(2)}, u32[]{:S(2)}) async-start(bf16[2,32,16512]{2,0,1:T(2,128)(2,1)} %copy.19), calls=%async_computation | async-start | bytes 4227072 | tf_op jit(solution)/shard_map/all_to_all | solution.py:170
  16.4 29.9 %copy-start.1 = (f32[8,48]{1,0:T(8,128)S(1)}, f32[8,48]{1,0:T(8,128)}, u32[]{:S(2)}) copy-start(f32[8,48]{1,0:T(8,128)} %gain_ref.1) | copy-start | bytes 4612
  65.9 11.3 %all-to-all-start.2 = ((f32[2,32,1]{0,2,1:T(1,128)}), f32[2,32,1]{0,2,1:T(1,128)S(1)}, u32[]{:S(2)}, u32[]{:S(2)}) async-start(f32[2,32,1]{0,2,1:T(1,128)} %copy.23), calls=%async_computation.2 | async-start | bytes 32768 | tf_op jit(solution)/shard_map/all_to_all | solution.py:179
  77.2 26.8 %all-to-all-start.1 = ((f32[8,8,17,128]{3,1,2,0:T(8,128)}), f32[8,8,17,128]{3,1,2,0:T(8,128)S(1)}, u32[]{:S(2)}, u32[]{:S(2)}) async-start(f32[8,8,17,128]{3,1,2,0:T(8,128)} %fusion.14), calls=%async_computation.1 | async-start | bytes 1114112 | tf_op jit(solution)/shard_map/all_to_all | solution.py:188

commit v2 on v1

--- a/solution.py
+++ b/solution.py
@@ -38,7 +38,7 @@
     return jnp.where(is_even, even_part, odd_part).astype(jnp.float32)
 
 
-def class_kernel(pix, rows_ref, ref_ref, scale_ref, energy_ref, gain_ref, planes_ref, evid_ref,
+def class_kernel(pix, groups, rows_ref, ref_ref, scale_ref, energy_ref, gain_ref, planes_ref, evid_ref,
                  ext_ref, acc_ref, v_ref):
     chunks = pix // IMG
 
@@ -96,23 +96,33 @@
         v_ref[t, 0:depth] = mixed_hi
         v_ref[t, depth:2 * depth] = mixed - mixed_hi
 
+    band = pix // groups
+    width = band // IMG
+
     def plane_tiles(j, carry):
-        n0 = pl.multiple_of(j * TN, TN)
-        summed = jnp.zeros((2 * depth, TN), jnp.float32)
+        n0 = pl.multiple_of(j * band, band)
+        summed = jnp.zeros((2 * depth, band), jnp.float32)
         for ai, a in enumerate(SHIFTS):
             start = pl.multiple_of(n0 + IMG * (1 - a), IMG)
             for bi in range(3):
                 summed = summed + jnp.dot(
-                    v_ref[ai * 3 + bi].astype(jnp.bfloat16), ext_ref[bi, :, pl.ds(start, TN)],
+                    v_ref[ai * 3 + bi].astype(jnp.bfloat16), ext_ref[bi, :, pl.ds(start, band)],
                     preferred_element_type=jnp.float32,
                 )
-        planes_ref[:, pl.ds(n0, TN)] = summed[0:depth] + summed[depth:2 * depth]
+        plane = summed[0:depth] + summed[depth:2 * depth]
+        before = lax.rem(j + groups - 1, groups)
+        for z in range(depth):
+            for u in range(width):
+                row = z * (width + 1) + u
+                planes_ref[j, pl.ds(row, 1), :] = plane[z:z + 1, u * IMG:(u + 1) * IMG]
+            row = z * (width + 1) + width
+            planes_ref[before, pl.ds(row, 1), :] = plane[z:z + 1, 0:IMG]
         return carry
 
-    lax.fori_loop(0, pix // TN, plane_tiles, 0)
-
-
-def class_pass(rows_ext, templates, scale_row, energy_col, gain, pix):
+    lax.fori_loop(0, groups, plane_tiles, 0)
+
+
+def class_pass(rows_ext, templates, scale_row, energy_col, gain, pix, groups):
     rowcount = rows_ext.shape[0]
     refcount = templates.shape[0]
     depth = gain.shape[0]
@@ -123,9 +133,9 @@
         bytes_accessed=rows_ext.size * 2 + templates.size * 2 + depth * pix * 4,
     )
     return pl.pallas_call(
-        functools.partial(class_kernel, pix),
+        functools.partial(class_kernel, pix, groups),
         out_shape=(
-            jax.ShapeDtypeStruct((depth, pix), jnp.float32),
+            jax.ShapeDtypeStruct((groups, depth * (pix // groups // IMG + 1), IMG), jnp.float32),
             jax.ShapeDtypeStruct((1, rowcount), jnp.float32),
         ),
         in_specs=[vmem] * 5,
@@ -172,20 +182,18 @@
     scale_row = rows_ext[:, pix].astype(jnp.float32).reshape(1, slot_depth * sources)
     templates = references[0]
     energy_col = jnp.sum(jnp.square(templates.astype(jnp.float32)), axis=1).reshape(-1, 1)
-    planes, class_evidence = class_pass(
-        rows_ext, templates, scale_row, energy_col, insert_weights, pix
+    windows, class_evidence = class_pass(
+        rows_ext, templates, scale_row, energy_col, insert_weights, pix, groups
     )
     stacked = class_evidence.reshape(slot_depth, sources)
     returned = lax.all_to_all(stacked, "dev", split_axis=1, concat_axis=1, tiled=True).reshape(
         total_slots
     )
     particle_evidence = jnp.take(returned, slot_index)
-    depth = planes.shape[0]
-    planes = planes.reshape(depth, IMG, IMG)
+    depth = insert_weights.shape[0]
     band = IMG // groups
-    wrapped = jnp.concatenate([planes, planes[:, :1]], axis=1)
-    windows = jnp.stack([wrapped[:, g * band:g * band + band + 1] for g in range(groups)], 0)
     mine = jnp.sum(lax.all_to_all(windows, "grp", split_axis=0, concat_axis=0, tiled=True), 0)
+    mine = mine.reshape(depth, band + 1, IMG)
     interp = upsample_table(VOL, IMG)
     across = jnp.einsum("zjv,xv->zjx", mine, interp, precision=lax.Precision.HIGHEST)
     rows_table = local_table(2 * band, band + 1)

time: 106 us -> 101 us (0.953)
  blocking collectives: 0 us -> 10.6 us
  waiting for transfers between devices: 51.6 us -> 45.2 us
  local copies, waits for them, and re-layouts: 13 us -> 7.99 us
  starting transfers between devices: 21.3 us -> 17 us
    all_to_all x0 -> x1, blocking collectives: none -> 10.6 us  [on_device(): lax.all_to_all(stacked, 'dev', split_axis=1, concat_axis=1, tiled=True)]
    all_to_all x1 -> x0, waiting for transfers between devices: 6.35 us -> none  [on_device(): lax.all_to_all(stacked, 'dev', split_axis=1, concat_axis=1, tiled=True)]
    unnamed x12 -> x5, local copies, waits for them, and re-layouts: 5.28 us -> 0.87 us
    all_to_all x1 -> x0, starting transfers between devices: 4.36 us -> none  [on_device(): lax.all_to_all(stacked, 'dev', split_axis=1, concat_axis=1, tiled=True)]
  transfers between devices with their start and end apart: 3 -> 2, of which waited for: 3 -> 2; matrix products, arithmetic and copies ran while one was open for 2% -> 2% of each run, Pallas kernels for 0% -> 0%
where the time goes in v2:
time: 101 us; the launch traced here: 100 us
  waiting for transfers between devices  45.2 us (45%)
  starting transfers between devices  17 us (17%)
  Pallas kernels  13.3 us (13%)
  blocking collectives  10.6 us (10%)
  local copies, waits for them, and re-layouts  7.99 us (8%)
  matrix products  2.79 us (3%)
  other arithmetic  2.68 us (3%)
    all_to_all x1, waiting for transfers between devices, on_device(): lax.all_to_all(outgoing, 'dev', split_axis=1, concat_axis=1, tiled=True)  28 us
    all_to_all x1, waiting for transfers between devices, on_device(): lax.all_to_all(windows, 'grp', split_axis=0, concat_axis=0, tiled=True)  17.2 us
    pallas_call x1, Pallas kernels, class_pass(): pl.pallas_call(functools.partial(class_kernel, pix, groups), out_shape=(j...  13.3 us
    all_to_all x1, blocking collectives, on_device(): lax.all_to_all(stacked, 'dev', split_axis=1, concat_axis=1, tiled=True)  10.6 us
    all_to_all x1, starting transfers between devices, on_device(): lax.all_to_all(outgoing, 'dev', split_axis=1, concat_axis=1, tiled=True)  8.77 us
    all_to_all x1, starting transfers between devices, on_device(): lax.all_to_all(windows, 'grp', split_axis=0, concat_axis=0, tiled=True)  8.2 us
    reshape x1, local copies, waits for them, and re-layouts, on_device(): outgoing = outgoing.reshape(slot_depth, sources, owned_classes * width)  2.94 us
  transfers between devices with their start and end apart: 2, of which 2 were waited for; matrix products, arithmetic and copies ran while one was open for 2% of the time, Pallas kernels for 0%

profile of v2, /device:TPU:1, one launch (start us, length us, event | category | flops | bytes accessed | tf_op | source)
XLA Modules:
  0.0 100.2 jit_solution(5553892943138361133)
XLA Ops:
  0.6 0.9 convert_reduce_fusion.1
  1.6 0.7 broadcast_in_dim.84
  2.3 1.9 %convolution_convert_fusion = bf16[64,16512]{1,0:T(8,128)(2,1)S(1)} fusion(bf16[32,128]{1,0:T(8,128)(2,1)S(1)} %broadcast_in_dim.84, bf16[32,16384]{1,0:T(8,128)(2,1)} %param.6, s32[32]{0:T(128)S(1)} %get-tuple-element.17), kind=kOutput, calls=%fused_computation.1 | convolution fusion | flops 70805504 | bytes 3170432 | tf_op jit(solution)/shard_map/dot_general | solution.py:178
  4.2 2.9 %copy.18 = bf16[2,32,16512]{2,0,1:T(2,128)(2,1)} copy(bf16[2,32,16512]{2,1,0:T(8,128)(2,1)S(1)} %bitcast.25) | data formatting | bytes 4227072 | tf_op jit(solution)/shard_map/reshape | solution.py:179
  7.1 0.0 copy-start
  7.1 8.8 %all-to-all-start = ((bf16[2,32,16512]{2,0,1:T(2,128)(2,1)}), bf16[2,32,16512]{2,0,1:T(2,128)(2,1)}, u32[]{:S(2)}, u32[]{:S(2)}) async-start(bf16[2,32,16512]{2,0,1:T(2,128)(2,1)} %copy.18), calls=%async_computation | async-start | bytes 4227072 | tf_op jit(solution)/shard_map/all_to_all | solution.py:180
  15.9 0.0 copy-done
  15.9 0.4 multiply_reduce_fusion
  16.3 0.1 copy.20.energy_ref
  16.4 0.0 copy-start.1
  16.4 28.0 %all-to-all-done = bf16[2,32,16512]{2,0,1:T(2,128)(2,1)} async-done(((bf16[2,32,16512]{2,0,1:T(2,128)(2,1)}), bf16[2,32,16512]{2,0,1:T(2,128)(2,1)}, u32[]{:S(2)}, u32[]{:S(2)}) %all-to-all-start) | async-done | bytes 2113568 | tf_op jit(solution)/shard_map/all_to_all | solution.py:180
  44.4 1.8 %copy.19 = bf16[2,32,16512]{2,1,0:T(8,128)(2,1)S(1)} copy(bf16[2,32,16512]{2,0,1:T(2,128)(2,1)} %all-to-all-done) | data formatting | bytes 4227072 | tf_op jit(solution)/shard_map/all_to_all | solution.py:180
  46.2 0.1 convert_reduce_fusion
  46.4 0.0 copy-done.1
  46.4 13.3 %shard_map.77 = (f32[8,136,128]{2,1,0:T(8,128)}, f32[1,64]{1,0:T(1,128)S(1)}) custom-call(bf16[64,16512]{1,0:T(8,128)(2,1)S(1)} %bitcast.22, bf16[48,16384]{1,0:T(8,128)(2,1)S(1)} %bitcast.23, f32[1,64]{1,0:T(1,128)S(1)} %bitcast.24, f32[48,1]{1,0:T(8,128)S(1)} %copy.20.energy_ref, f32[8,48]{1,0:T(8,128)S(1)} %copy-done.1), custom_call_target="tpu_custom_call" | custom-call | flops 1207959552 | bytes 4210688 | tf_op jit(solution)/shard_map/pallas_call | solution.py:135
  59.6 0.5 broadcast.267
  60.1 0.7 reduce.5
  60.8 0.1 all_to_all.14
  60.9 0.1 copy.21
  61.0 10.6 %all_to_all.19 = f32[2,32,1]{0,2,1:T(1,128)S(1)} all-to-all(f32[2,32,1]{0,2,1:T(1,128)S(1)} %copy.21), channel_id=1, replica_groups=mesh['grp'=8,'dev'=32] {'dev'}, dimensions={1} | all-to-all | bytes 512 | tf_op jit(solution)/shard_map/all_to_all | solution.py:189
  71.6 8.2 %all-to-all-start.1 = ((f32[8,136,128]{2,1,0:T(8,128)}), f32[8,136,128]{2,1,0:T(8,128)S(1)}, u32[]{:S(2)}, u32[]{:S(2)}) async-start(f32[8,136,128]{2,1,0:T(8,128)} %get-tuple-element.4), calls=%async_computation.1 | async-start | bytes 1114112 | tf_op jit(solution)/shard_map/all_to_all | solution.py:195
  79.8 0.1 copy.22
  79.9 0.1 reshape.213
  80.0 0.7 gather_fusion
  80.7 0.5 and_select_fusion
  81.2 17.2 %all-to-all-done.1 = f32[8,136,128]{2,1,0:T(8,128)S(1)} async-done(((f32[8,136,128]{2,1,0:T(8,128)}), f32[8,136,128]{2,1,0:T(8,128)S(1)}, u32[]{:S(2)}, u32[]{:S(2)}) %all-to-all-start.1) | async-done | bytes 557088 | tf_op jit(solution)/shard_map/all_to_all | solution.py:195
  98.5 0.5 fusion.7
  98.9 0.4 fusion.24
  99.4 0.9 copy.23
  (8 shorter events, 0.1 us)
Async XLA Ops:
  7.1 8.8 %copy-start = (bf16[1,48,16384]{2,1,0:T(8,128)(2,1)S(1)}, bf16[1,48,16384]{2,1,0:T(8,128)(2,1)}, u32[]{:S(2)}) copy-start(bf16[1,48,16384]{2,1,0:T(8,128)(2,1)} %param.10) | copy-start | bytes 4718596
  7.1 37.3 %all-to-all-start = ((bf16[2,32,16512]{2,0,1:T(2,128)(2,1)}), bf16[2,32,16512]{2,0,1:T(2,128)(2,1)}, u32[]{:S(2)}, u32[]{:S(2)}) async-start(bf16[2,32,16512]{2,0,1:T(2,128)(2,1)} %copy.18), calls=%async_computation | async-start | bytes 4227072 | tf_op jit(solution)/shard_map/all_to_all | solution.py:180
  16.4 29.9 %copy-start.1 = (f32[8,48]{1,0:T(8,128)S(1)}, f32[8,48]{1,0:T(8,128)}, u32[]{:S(2)}) copy-start(f32[8,48]{1,0:T(8,128)} %gain_ref.1) | copy-start | bytes 4612
  71.6 26.9 %all-to-all-start.1 = ((f32[8,136,128]{2,1,0:T(8,128)}), f32[8,136,128]{2,1,0:T(8,128)S(1)}, u32[]{:S(2)}, u32[]{:S(2)}) async-start(f32[8,136,128]{2,1,0:T(8,128)} %get-tuple-element.4), calls=%async_computation.1 | async-start | bytes 1114112 | tf_op jit(solution)/shard_map/all_to_all | solution.py:195

commit v3 on v2

--- a/solution.py
+++ b/solution.py
@@ -185,11 +185,9 @@
     windows, class_evidence = class_pass(
         rows_ext, templates, scale_row, energy_col, insert_weights, pix, groups
     )
-    stacked = class_evidence.reshape(slot_depth, sources)
-    returned = lax.all_to_all(stacked, "dev", split_axis=1, concat_axis=1, tiled=True).reshape(
-        total_slots
-    )
-    particle_evidence = jnp.take(returned, slot_index)
+    gathered = lax.all_gather(class_evidence.reshape(total_slots), "dev", tiled=True)
+    me = lax.axis_index("dev")
+    particle_evidence = jnp.take(gathered, position * total_slots + arrival * sources + me)
     depth = insert_weights.shape[0]
     band = IMG // groups
     mine = jnp.sum(lax.all_to_all(windows, "grp", split_axis=0, concat_axis=0, tiled=True), 0)

time: 101 us -> 136 us (1.35)
  blocking collectives: 10.6 us -> 64.1 us
  waiting for transfers between devices: 45.2 us -> 26.7 us
    all_gather x0 -> x1, blocking collectives: none -> 64.1 us  [on_device(): lax.all_gather(class_evidence.reshape(total_slots), 'dev', tiled=True)]
    all_to_all x1, waiting for transfers between devices: 17.2 us -> 0.01 us  [on_device(): lax.all_to_all(windows, 'grp', split_axis=0, concat_axis=0, tiled=True)]
    all_to_all x1 -> x0, blocking collectives: 10.6 us -> none  [on_device(): lax.all_to_all(stacked, 'dev', split_axis=1, concat_axis=1, tiled=True)]
  transfers between devices with their start and end apart: 2 -> 2, of which waited for: 2 -> 1; matrix products, arithmetic and copies ran while one was open for 2% -> 2% of each run, Pallas kernels for 0% -> 0%
where the time goes in v3:
time: 136 us; the launch traced here: 135 us
  blocking collectives  64.1 us (47%)
  waiting for transfers between devices  26.7 us (20%)
  starting transfers between devices  17 us (12%)
  Pallas kernels  13.3 us (10%)
  local copies, waits for them, and re-layouts  7.86 us (6%)
  matrix products  2.79 us (2%)
  other arithmetic  2.02 us (1%)
  between operations  1.42 us (1%)
    all_gather x1, blocking collectives, on_device(): lax.all_gather(class_evidence.reshape(total_slots), 'dev', tiled=True)  64.1 us
    all_to_all x1, waiting for transfers between devices, on_device(): lax.all_to_all(outgoing, 'dev', split_axis=1, concat_axis=1, tiled=True)  26.7 us
    pallas_call x1, Pallas kernels, class_pass(): pl.pallas_call(functools.partial(class_kernel, pix, groups), out_shape=(j...  13.3 us
    all_to_all x1, starting transfers between devices, on_device(): lax.all_to_all(outgoing, 'dev', split_axis=1, concat_axis=1, tiled=True)  8.77 us
    all_to_all x1, starting transfers between devices, on_device(): lax.all_to_all(windows, 'grp', split_axis=0, concat_axis=0, tiled=True)  8.18 us
    reshape x1, local copies, waits for them, and re-layouts, on_device(): outgoing = outgoing.reshape(slot_depth, sources, owned_classes * width)  2.94 us
  transfers between devices with their start and end apart: 2, of which 1 were waited for; matrix products, arithmetic and copies ran while one was open for 2% of the time, Pallas kernels for 0%

profile of v3, /device:TPU:1, one launch (start us, length us, event | category | flops | bytes accessed | tf_op | source)
XLA Modules:
  0.0 135.2 jit_solution(7545658216265480633)
XLA Ops:
  0.6 0.9 convert_reduce_fusion.1
  1.6 0.7 broadcast_in_dim.84
  2.3 1.9 %convolution_convert_fusion = bf16[64,16512]{1,0:T(8,128)(2,1)S(1)} fusion(bf16[32,128]{1,0:T(8,128)(2,1)S(1)} %broadcast_in_dim.84, bf16[32,16384]{1,0:T(8,128)(2,1)} %param.6, s32[32]{0:T(128)S(1)} %multiply_add_fusion), kind=kOutput, calls=%fused_computation.1 | convolution fusion | flops 70805504 | bytes 3170432 | tf_op jit(solution)/shard_map/dot_general | solution.py:178
  4.2 2.9 %copy.16 = bf16[2,32,16512]{2,0,1:T(2,128)(2,1)} copy(bf16[2,32,16512]{2,1,0:T(8,128)(2,1)S(1)} %bitcast.26) | data formatting | bytes 4227072 | tf_op jit(solution)/shard_map/reshape | solution.py:179
  7.1 0.0 copy-start
  7.1 0.0 copy-start.2
  7.1 8.8 %all-to-all-start = ((bf16[2,32,16512]{2,0,1:T(2,128)(2,1)}), bf16[2,32,16512]{2,0,1:T(2,128)(2,1)}, u32[]{:S(2)}, u32[]{:S(2)}) async-start(bf16[2,32,16512]{2,0,1:T(2,128)(2,1)} %copy.16), calls=%async_computation | async-start | bytes 4227072 | tf_op jit(solution)/shard_map/all_to_all | solution.py:180
  15.9 0.0 copy-done
  15.9 0.4 multiply_reduce_fusion
  16.3 0.1 copy.18.energy_ref
  16.4 0.0 copy-done.2
  16.4 0.6 dynamic-slice
  17.7 0.0 copy-start.1
  17.7 26.7 %all-to-all-done = bf16[2,32,16512]{2,0,1:T(2,128)(2,1)} async-done(((bf16[2,32,16512]{2,0,1:T(2,128)(2,1)}), bf16[2,32,16512]{2,0,1:T(2,128)(2,1)}, u32[]{:S(2)}, u32[]{:S(2)}) %all-to-all-start) | async-done | bytes 2113568 | tf_op jit(solution)/shard_map/all_to_all | solution.py:180
  44.4 1.8 %copy.17 = bf16[2,32,16512]{2,1,0:T(8,128)(2,1)S(1)} copy(bf16[2,32,16512]{2,0,1:T(2,128)(2,1)} %all-to-all-done) | data formatting | bytes 4227072 | tf_op jit(solution)/shard_map/all_to_all | solution.py:180
  46.3 0.1 convert_reduce_fusion
  46.4 0.0 copy-done.1
  46.4 13.3 %shard_map.77 = (f32[8,136,128]{2,1,0:T(8,128)}, f32[1,64]{1,0:T(1,128)S(1)}) custom-call(bf16[64,16512]{1,0:T(8,128)(2,1)S(1)} %bitcast.23, bf16[48,16384]{1,0:T(8,128)(2,1)S(1)} %bitcast.24, f32[1,64]{1,0:T(1,128)S(1)} %bitcast.25, f32[48,1]{1,0:T(8,128)S(1)} %copy.18.energy_ref, f32[8,48]{1,0:T(8,128)S(1)} %copy-done.1), custom_call_target="tpu_custom_call" | custom-call | flops 1207959552 | bytes 4210688 | tf_op jit(solution)/shard_map/pallas_call | solution.py:135
  59.6 8.2 %all-to-all-start.1 = ((f32[8,136,128]{2,1,0:T(8,128)}), f32[8,136,128]{2,1,0:T(8,128)S(1)}, u32[]{:S(2)}, u32[]{:S(2)}) async-start(f32[8,136,128]{2,1,0:T(8,128)} %get-tuple-element.4), calls=%async_computation.1 | async-start | bytes 1114112 | tf_op jit(solution)/shard_map/all_to_all | solution.py:193
  67.9 0.1 bitcast_dynamic-update-slice_fusion
  68.0 64.1 %all-reduce = f32[2048]{0:T(1024)S(1)} all-reduce(f32[2048]{0:T(1024)S(1)} %bitcast_dynamic-update-slice_fusion), channel_id=2, replica_groups=mesh['grp'=8,'dev'=32] {'dev'}, use_global_device_ids=true, to_apply=%add | all-reduce | flops 2048 | bytes 16384 | tf_op jit(solution)/shard_map/all_gather | solution.py:188
  132.1 0.7 gather_fusion
  132.8 0.5 and_select_fusion
  133.4 0.0 all-to-all-done.1
  133.4 0.5 fusion.7
  133.9 0.4 fusion.24
  134.3 0.9 copy.19
  (10 shorter events, 0.1 us)
Async XLA Ops:
  7.1 8.8 %copy-start = (bf16[1,48,16384]{2,1,0:T(8,128)(2,1)S(1)}, bf16[1,48,16384]{2,1,0:T(8,128)(2,1)}, u32[]{:S(2)}) copy-start(bf16[1,48,16384]{2,1,0:T(8,128)(2,1)} %param.10) | copy-start | bytes 4718596
  7.1 9.3 %copy-start.2 = (u32[256]{0:T(256)S(1)}, u32[256]{0:T(256)}, u32[]{:S(2)}) copy-start(u32[256]{0:T(256)} %constant.105) | copy-start | bytes 3076
  7.1 37.3 %all-to-all-start = ((bf16[2,32,16512]{2,0,1:T(2,128)(2,1)}), bf16[2,32,16512]{2,0,1:T(2,128)(2,1)}, u32[]{:S(2)}, u32[]{:S(2)}) async-start(bf16[2,32,16512]{2,0,1:T(2,128)(2,1)} %copy.16), calls=%async_computation | async-start | bytes 4227072 | tf_op jit(solution)/shard_map/all_to_all | solution.py:180
  17.7 28.7 %copy-start.1 = (f32[8,48]{1,0:T(8,128)S(1)}, f32[8,48]{1,0:T(8,128)}, u32[]{:S(2)}) copy-start(f32[8,48]{1,0:T(8,128)} %gain_ref.1) | copy-start | bytes 4612
  59.6 73.7 %all-to-all-start.1 = ((f32[8,136,128]{2,1,0:T(8,128)}), f32[8,136,128]{2,1,0:T(8,128)S(1)}, u32[]{:S(2)}, u32[]{:S(2)}) async-start(f32[8,136,128]{2,1,0:T(8,128)} %get-tuple-element.4), calls=%async_computation.1 | async-start | bytes 1114112 | tf_op jit(solution)/shard_map/all_to_all | solution.py:193

commit v4 on v2

--- a/solution.py
+++ b/solution.py
@@ -192,7 +192,12 @@
     particle_evidence = jnp.take(returned, slot_index)
     depth = insert_weights.shape[0]
     band = IMG // groups
-    mine = jnp.sum(lax.all_to_all(windows, "grp", split_axis=0, concat_axis=0, tiled=True), 0)
+    here = lax.axis_index("grp")
+    mine = lax.dynamic_index_in_dim(windows, here, 0, keepdims=False)
+    for step in range(1, groups):
+        part = lax.dynamic_index_in_dim(windows, lax.rem(here + step, groups), 0, keepdims=False)
+        pairs = [(g, (g + step) % groups) for g in range(groups)]
+        mine = mine + lax.ppermute(part, "grp", pairs)
     mine = mine.reshape(depth, band + 1, IMG)
     interp = upsample_table(VOL, IMG)
     across = jnp.einsum("zjv,xv->zjx", mine, interp, precision=lax.Precision.HIGHEST)

time: 101 us -> 93.5 us (0.926)
  blocking collectives: 10.6 us -> 0 us
  starting transfers between devices: 17 us -> 27.2 us
  waiting for transfers between devices: 45.2 us -> 38.6 us
    all_to_all x1, waiting for transfers between devices: 17.2 us -> 1.96 us  [on_device(): lax.all_to_all(stacked, 'dev', split_axis=1, concat_axis=1, tiled=True)]
    ppermute x0 -> x7, starting transfers between devices: none -> 13.5 us  [on_device(): mine = mine + lax.ppermute(part, 'grp', pairs)]
    all_to_all x1 -> x0, blocking collectives: 10.6 us -> none  [on_device(): lax.all_to_all(stacked, 'dev', split_axis=1, concat_axis=1, tiled=True)]
    ppermute x0 -> x7, waiting for transfers between devices: none -> 8.76 us  [on_device(): mine = mine + lax.ppermute(part, 'grp', pairs)]
    all_to_all x1, starting transfers between devices: 8.2 us -> 4.91 us  [on_device(): lax.all_to_all(stacked, 'dev', split_axis=1, concat_axis=1, tiled=True)]
  transfers between devices with their start and end apart: 2 -> 9, of which waited for: 2 -> 5; matrix products, arithmetic and copies ran while one was open for 2% -> 4% of each run, Pallas kernels for 0% -> 0%
where the time goes in v4:
time: 93.5 us; the launch traced here: 93.2 us
  waiting for transfers between devices  38.6 us (41%)
  starting transfers between devices  27.2 us (29%)
  Pallas kernels  12.5 us (13%)
  local copies, waits for them, and re-layouts  8.66 us (9%)
  matrix products  2.79 us (3%)
  other arithmetic  2.68 us (3%)
    all_to_all x1, waiting for transfers between devices, on_device(): lax.all_to_all(outgoing, 'dev', split_axis=1, concat_axis=1, tiled=True)  27.9 us
    ppermute x7, starting transfers between devices, on_device(): mine = mine + lax.ppermute(part, 'grp', pairs)  13.5 us
    pallas_call x1, Pallas kernels, class_pass(): pl.pallas_call(functools.partial(class_kernel, pix, groups), out_shape=(j...  12.5 us
    all_to_all x1, starting transfers between devices, on_device(): lax.all_to_all(outgoing, 'dev', split_axis=1, concat_axis=1, tiled=True)  8.77 us
    ppermute x7, waiting for transfers between devices, on_device(): mine = mine + lax.ppermute(part, 'grp', pairs)  8.76 us
    all_to_all x1, starting transfers between devices, on_device(): lax.all_to_all(stacked, 'dev', split_axis=1, concat_axis=1, tiled=True)  4.91 us
    reshape x1, local copies, waits for them, and re-layouts, on_device(): outgoing = outgoing.reshape(slot_depth, sources, owned_classes * width)  2.95 us
    all_to_all x1, waiting for transfers between devices, on_device(): lax.all_to_all(stacked, 'dev', split_axis=1, concat_axis=1, tiled=True)  1.96 us
  transfers between devices with their start and end apart: 9, of which 5 were waited for; matrix products, arithmetic and copies ran while one was open for 4% of the time, Pallas kernels for 0%

profile of v4, /device:TPU:1, one launch (start us, length us, event | category | flops | bytes accessed | tf_op | source)
XLA Modules:
  0.0 93.2 jit_solution(15611589667428549755)
XLA Ops:
  0.6 0.9 convert_reduce_fusion.1
  1.6 0.7 broadcast_in_dim.84
  2.3 1.9 %convolution_convert_fusion = bf16[64,16512]{1,0:T(8,128)(2,1)S(1)} fusion(bf16[32,128]{1,0:T(8,128)(2,1)S(1)} %broadcast_in_dim.84, bf16[32,16384]{1,0:T(8,128)(2,1)} %param.6, s32[32]{0:T(128)S(1)} %get-tuple-element.17), kind=kOutput, calls=%fused_computation.1 | convolution fusion | flops 70805504 | bytes 3170432 | tf_op jit(solution)/shard_map/dot_general | solution.py:178
  4.2 2.9 %copy.18 = bf16[2,32,16512]{2,0,1:T(2,128)(2,1)} copy(bf16[2,32,16512]{2,1,0:T(8,128)(2,1)S(1)} %bitcast.53) | data formatting | bytes 4227072 | tf_op jit(solution)/shard_map/reshape | solution.py:179
  7.1 0.0 copy-start
  7.1 8.8 %all-to-all-start = ((bf16[2,32,16512]{2,0,1:T(2,128)(2,1)}), bf16[2,32,16512]{2,0,1:T(2,128)(2,1)}, u32[]{:S(2)}, u32[]{:S(2)}) async-start(bf16[2,32,16512]{2,0,1:T(2,128)(2,1)} %copy.18), calls=%async_computation | async-start | bytes 4227072 | tf_op jit(solution)/shard_map/all_to_all | solution.py:180
  16.0 0.0 copy-done
  16.0 0.4 multiply_reduce_fusion
  16.4 0.1 copy.20.energy_ref
  16.5 0.0 copy-start.1
  16.5 27.9 %all-to-all-done = bf16[2,32,16512]{2,0,1:T(2,128)(2,1)} async-done(((bf16[2,32,16512]{2,0,1:T(2,128)(2,1)}), bf16[2,32,16512]{2,0,1:T(2,128)(2,1)}, u32[]{:S(2)}, u32[]{:S(2)}) %all-to-all-start) | async-done | bytes 2113568 | tf_op jit(solution)/shard_map/all_to_all | solution.py:180
  44.5 1.8 %copy.19 = bf16[2,32,16512]{2,1,0:T(8,128)(2,1)S(1)} copy(bf16[2,32,16512]{2,0,1:T(2,128)(2,1)} %all-to-all-done) | data formatting | bytes 4227072 | tf_op jit(solution)/shard_map/all_to_all | solution.py:180
  46.3 0.1 convert_reduce_fusion
  46.4 0.0 copy-done.1
  46.4 12.5 %shard_map.77 = (f32[8,136,128]{2,1,0:T(8,128)S(1)}, f32[1,64]{1,0:T(1,128)S(1)}) custom-call(bf16[64,16512]{1,0:T(8,128)(2,1)S(1)} %bitcast.50, bf16[48,16384]{1,0:T(8,128)(2,1)S(1)} %bitcast.51, f32[1,64]{1,0:T(1,128)S(1)} %bitcast.52, f32[48,1]{1,0:T(8,128)S(1)} %copy.20.energy_ref, f32[8,48]{1,0:T(8,128)S(1)} %copy-done.1), custom_call_target="tpu_custom_call" | custom-call | flops 1207959552 | bytes 4210688 | tf_op jit(solution)/shard_map/pallas_call | solution.py:135
  58.9 0.1 dynamic-slice_bitcast_fusion.6
  58.9 5.7 %collective-permute-start.6 = (f32[136,128]{1,0:T(8,128)S(1)}, f32[136,128]{1,0:T(8,128)S(1)}, u32[]{:S(2)}, u32[]{:S(2)}) collective-permute-start(f32[136,128]{1,0:T(8,128)S(1)} %get-tuple-element.19), channel_id=1, source_target_pairs={{0,224},{32,0},{64,32},{96,64},{128,96},{160,128},{192,160},{224,1... | collective-permute-start | bytes 208904 | tf_op jit(solution)/shard_map/ppermute | solution.py:200
  64.6 1.2 %collective-permute-start.5 = (f32[136,128]{1,0:T(8,128)S(1)}, f32[136,128]{1,0:T(8,128)S(1)}, u32[]{:S(2)}, u32[]{:S(2)}) collective-permute-start(f32[136,128]{1,0:T(8,128)S(1)} %get-tuple-element.20), channel_id=1, source_target_pairs={{0,192},{32,224},{64,0},{96,32},{128,64},{160,96},{192,128},{224,1... | collective-permute-start | bytes 208904 | tf_op jit(solution)/shard_map/ppermute | solution.py:200
  65.7 0.5 broadcast.274
  66.3 0.7 reduce.5
  66.9 0.1 all_to_all.10
  67.0 0.7 copy.21
  67.7 4.9 %all-to-all-start.1 = ((f32[2,32,1]{0,2,1:T(1,128)}), f32[2,32,1]{0,2,1:T(1,128)S(1)}, u32[]{:S(2)}, u32[]{:S(2)}) async-start(f32[2,32,1]{0,2,1:T(1,128)} %copy.21), calls=%async_computation.1 | async-start | bytes 32768 | tf_op jit(solution)/shard_map/all_to_all | solution.py:189
  72.6 0.2 collective-permute-start.4
  72.9 4.8 %collective-permute-start.3 = (f32[136,128]{1,0:T(8,128)S(1)}, f32[136,128]{1,0:T(8,128)S(1)}, u32[]{:S(2)}, u32[]{:S(2)}) collective-permute-start(f32[136,128]{1,0:T(8,128)S(1)} %get-tuple-element.22), channel_id=1, source_target_pairs={{0,128},{32,160},{64,192},{96,224},{128,0},{160,32},{192,64},{224,... | collective-permute-start | bytes 208904 | tf_op jit(solution)/shard_map/ppermute | solution.py:200
  77.6 0.0 collective-permute-start.2
  77.6 2.0 %all-to-all-done.1 = f32[2,32,1]{0,2,1:T(1,128)S(1)} async-done(((f32[2,32,1]{0,2,1:T(1,128)}), f32[2,32,1]{0,2,1:T(1,128)S(1)}, u32[]{:S(2)}, u32[]{:S(2)}) %all-to-all-start.1) | async-done | bytes 288 | tf_op jit(solution)/shard_map/all_to_all | solution.py:189
  79.6 0.1 copy.22
  79.7 0.1 reshape.213
  79.8 0.7 gather_fusion
  80.5 0.0 collective-permute-done.6
  80.5 1.3 %collective-permute-start.1 = (f32[136,128]{1,0:T(8,128)S(1)}, f32[136,128]{1,0:T(8,128)S(1)}, u32[]{:S(2)}, u32[]{:S(2)}) collective-permute-start(f32[136,128]{1,0:T(8,128)S(1)} %get-tuple-element.24), channel_id=1, source_target_pairs={{0,64},{32,96},{64,128},{96,160},{128,192},{160,224},{192,0},{224,... | collective-permute-start | bytes 208904 | tf_op jit(solution)/shard_map/ppermute | solution.py:200
  81.7 0.0 collective-permute-done.5
  81.7 0.4 collective-permute-start
  82.1 0.5 and_select_fusion
  82.6 0.0 collective-permute-done.4
  82.6 0.0 collective-permute-done.3
  82.6 2.0 %collective-permute-done.2 = f32[136,128]{1,0:T(8,128)S(1)} collective-permute-done((f32[136,128]{1,0:T(8,128)S(1)}, f32[136,128]{1,0:T(8,128)S(1)}, u32[]{:S(2)}, u32[]{:S(2)}) %collective-permute-start.2) | collective-permute-done | bytes 69664 | tf_op jit(solution)/shard_map/ppermute | solution.py:200
  84.6 5.0 %collective-permute-done.1 = f32[136,128]{1,0:T(8,128)S(1)} collective-permute-done((f32[136,128]{1,0:T(8,128)S(1)}, f32[136,128]{1,0:T(8,128)S(1)}, u32[]{:S(2)}, u32[]{:S(2)}) %collective-permute-start.1) | collective-permute-done | bytes 69664 | tf_op jit(solution)/shard_map/ppermute | solution.py:200
  89.6 1.8 %collective-permute-done = f32[136,128]{1,0:T(8,128)S(1)} collective-permute-done((f32[136,128]{1,0:T(8,128)S(1)}, f32[136,128]{1,0:T(8,128)S(1)}, u32[]{:S(2)}, u32[]{:S(2)}) %collective-permute-start) | collective-permute-done | bytes 69664 | tf_op jit(solution)/shard_map/ppermute | solution.py:200
  91.4 0.5 fusion.7
  91.9 0.4 fusion.30
  92.3 0.9 copy.23
  (8 shorter events, 0.1 us)
Async XLA Ops:
  7.1 8.8 %copy-start = (bf16[1,48,16384]{2,1,0:T(8,128)(2,1)S(1)}, bf16[1,48,16384]{2,1,0:T(8,128)(2,1)}, u32[]{:S(2)}) copy-start(bf16[1,48,16384]{2,1,0:T(8,128)(2,1)} %param.10) | copy-start | bytes 4718596
  7.1 37.3 %all-to-all-start = ((bf16[2,32,16512]{2,0,1:T(2,128)(2,1)}), bf16[2,32,16512]{2,0,1:T(2,128)(2,1)}, u32[]{:S(2)}, u32[]{:S(2)}) async-start(bf16[2,32,16512]{2,0,1:T(2,128)(2,1)} %copy.18), calls=%async_computation | async-start | bytes 4227072 | tf_op jit(solution)/shard_map/all_to_all | solution.py:180
  16.5 29.9 %copy-start.1 = (f32[8,48]{1,0:T(8,128)S(1)}, f32[8,48]{1,0:T(8,128)}, u32[]{:S(2)}) copy-start(f32[8,48]{1,0:T(8,128)} %gain_ref.1) | copy-start | bytes 4612
  58.9 21.5 %collective-permute-start.6 = (f32[136,128]{1,0:T(8,128)S(1)}, f32[136,128]{1,0:T(8,128)S(1)}, u32[]{:S(2)}, u32[]{:S(2)}) collective-permute-start(f32[136,128]{1,0:T(8,128)S(1)} %get-tuple-element.19), channel_id=1, source_target_pairs={{0,224},{32,0},{64,32},{96,64},{128,96},{160,128},{192,160},{224,1... | collective-permute-start | bytes 208904 | tf_op jit(solution)/shard_map/ppermute | solution.py:200
  64.6 17.2 %collective-permute-start.5 = (f32[136,128]{1,0:T(8,128)S(1)}, f32[136,128]{1,0:T(8,128)S(1)}, u32[]{:S(2)}, u32[]{:S(2)}) collective-permute-start(f32[136,128]{1,0:T(8,128)S(1)} %get-tuple-element.20), channel_id=1, source_target_pairs={{0,192},{32,224},{64,0},{96,32},{128,64},{160,96},{192,128},{224,1... | collective-permute-start | bytes 208904 | tf_op jit(solution)/shard_map/ppermute | solution.py:200
  67.7 11.9 %all-to-all-start.1 = ((f32[2,32,1]{0,2,1:T(1,128)}), f32[2,32,1]{0,2,1:T(1,128)S(1)}, u32[]{:S(2)}, u32[]{:S(2)}) async-start(f32[2,32,1]{0,2,1:T(1,128)} %copy.21), calls=%async_computation.1 | async-start | bytes 32768 | tf_op jit(solution)/shard_map/all_to_all | solution.py:189
  72.6 10.0 %collective-permute-start.4 = (f32[136,128]{1,0:T(8,128)S(1)}, f32[136,128]{1,0:T(8,128)S(1)}, u32[]{:S(2)}, u32[]{:S(2)}) collective-permute-start(f32[136,128]{1,0:T(8,128)S(1)} %get-tuple-element.21), channel_id=1, source_target_pairs={{0,160},{32,192},{64,224},{96,0},{128,32},{160,64},{192,96},{224,1... | collective-permute-start | bytes 208904 | tf_op jit(solution)/shard_map/ppermute | solution.py:200
  72.9 9.8 %collective-permute-start.3 = (f32[136,128]{1,0:T(8,128)S(1)}, f32[136,128]{1,0:T(8,128)S(1)}, u32[]{:S(2)}, u32[]{:S(2)}) collective-permute-start(f32[136,128]{1,0:T(8,128)S(1)} %get-tuple-element.22), channel_id=1, source_target_pairs={{0,128},{32,160},{64,192},{96,224},{128,0},{160,32},{192,64},{224,... | collective-permute-start | bytes 208904 | tf_op jit(solution)/shard_map/ppermute | solution.py:200
  77.6 7.0 %collective-permute-start.2 = (f32[136,128]{1,0:T(8,128)S(1)}, f32[136,128]{1,0:T(8,128)S(1)}, u32[]{:S(2)}, u32[]{:S(2)}) collective-permute-start(f32[136,128]{1,0:T(8,128)S(1)} %get-tuple-element.23), channel_id=1, source_target_pairs={{0,96},{32,128},{64,160},{96,192},{128,224},{160,0},{192,32},{224,... | collective-permute-start | bytes 208904 | tf_op jit(solution)/shard_map/ppermute | solution.py:200
  80.5 9.1 %collective-permute-start.1 = (f32[136,128]{1,0:T(8,128)S(1)}, f32[136,128]{1,0:T(8,128)S(1)}, u32[]{:S(2)}, u32[]{:S(2)}) collective-permute-start(f32[136,128]{1,0:T(8,128)S(1)} %get-tuple-element.24), channel_id=1, source_target_pairs={{0,64},{32,96},{64,128},{96,160},{128,192},{160,224},{192,0},{224,... | collective-permute-start | bytes 208904 | tf_op jit(solution)/shard_map/ppermute | solution.py:200
  81.7 9.6 %collective-permute-start = (f32[136,128]{1,0:T(8,128)S(1)}, f32[136,128]{1,0:T(8,128)S(1)}, u32[]{:S(2)}, u32[]{:S(2)}) collective-permute-start(f32[136,128]{1,0:T(8,128)S(1)} %get-tuple-element.18), channel_id=1, source_target_pairs={{0,32},{32,64},{64,96},{96,128},{128,160},{160,192},{192,224},{224... | collective-permute-start | bytes 208904 | tf_op jit(solution)/shard_map/ppermute | solution.py:200

commit v5 on v4

--- a/solution.py
+++ b/solution.py
@@ -167,7 +167,9 @@
     ordinal = jnp.arange(local_count, dtype=jnp.int32)
     earlier = (labels[:, None] == labels[None, :]) & (ordinal[None, :] < ordinal[:, None])
     arrival = jnp.sum(earlier, axis=1)
-    slot_index = arrival * classes + position
+    me = lax.axis_index("dev")
+    relative = lax.rem(position - me + sources, sources)
+    slot_index = relative * slot_depth + arrival
     total_slots = classes * slot_depth
     placing = (jnp.arange(total_slots, dtype=jnp.int32)[:, None] == slot_index[None, :]).astype(
         jnp.bfloat16
@@ -176,20 +178,24 @@
     carried = jnp.concatenate([particles, extra], axis=1)
     width = pix + IMG
     outgoing = jnp.dot(placing, carried, preferred_element_type=jnp.float32).astype(jnp.bfloat16)
-    outgoing = outgoing.reshape(slot_depth, sources, owned_classes * width)
-    arrived = lax.all_to_all(outgoing, "dev", split_axis=1, concat_axis=1, tiled=True)
-    rows_ext = arrived.reshape(slot_depth * sources, width)
-    scale_row = rows_ext[:, pix].astype(jnp.float32).reshape(1, slot_depth * sources)
+    outgoing = outgoing.reshape(sources, owned_classes * slot_depth, width)
+    pieces = [outgoing[0]]
+    for step in range(1, sources):
+        pairs = [(d, (d + step) % sources) for d in range(sources)]
+        pieces.append(lax.ppermute(outgoing[step], "dev", pairs))
+    rows_ext = jnp.stack(pieces, 0).reshape(sources * slot_depth, width)
+    scale_row = rows_ext[:, pix].astype(jnp.float32).reshape(1, sources * slot_depth)
     templates = references[0]
     energy_col = jnp.sum(jnp.square(templates.astype(jnp.float32)), axis=1).reshape(-1, 1)
     windows, class_evidence = class_pass(
         rows_ext, templates, scale_row, energy_col, insert_weights, pix, groups
     )
-    stacked = class_evidence.reshape(slot_depth, sources)
-    returned = lax.all_to_all(stacked, "dev", split_axis=1, concat_axis=1, tiled=True).reshape(
+    by_step = class_evidence.reshape(sources, slot_depth)
+    by_source = jnp.roll(jnp.flip(by_step, 0), me + 1, axis=0)
+    returned = lax.all_to_all(by_source, "dev", split_axis=0, concat_axis=0, tiled=True).reshape(
         total_slots
     )
-    particle_evidence = jnp.take(returned, slot_index)
+    particle_evidence = jnp.take(returned, position * slot_depth + arrival)
     depth = insert_weights.shape[0]
     band = IMG // groups
     here = lax.axis_index("grp")

time: 93.5 us -> 263 us (2.81)
  starting transfers between devices: 27.2 us -> 126 us
  waiting for transfers between devices: 38.6 us -> 75.7 us
  local copies, waits for them, and re-layouts: 8.66 us -> 37.6 us
  other arithmetic: 2.68 us -> 6.2 us
    ppermute x0 -> x31, starting transfers between devices: none -> 73.8 us  [on_device(): pieces.append(lax.ppermute(outgoing[step], 'dev', pairs))]
    ppermute x0 -> x31, waiting for transfers between devices: none -> 67.1 us  [on_device(): pieces.append(lax.ppermute(outgoing[step], 'dev', pairs))]
    ppermute x7, starting transfers between devices: 13.5 us -> 45.2 us  [on_device(): mine = mine + lax.ppermute(part, 'grp', pairs)]
    all_to_all x2 -> x1, waiting for transfers between devices: 29.9 us -> 0.01 us  [on_device(): lax.all_to_all(by_source, 'dev', split_axis=0, concat_axis=0, tiled=True)]
    unnamed x5 -> x56, local copies, waits for them, and re-layouts: 0.87 us -> 25.3 us
    all_to_all x2 -> x1, starting transfers between devices: 13.7 us -> 7.38 us  [on_device(): lax.all_to_all(by_source, 'dev', split_axis=0, concat_axis=0, tiled=True)]
    slice x0 -> x2, local copies, waits for them, and re-layouts: none -> 5.03 us  [on_device(): pieces.append(lax.ppermute(outgoing[step], 'dev', pairs))]
  transfers between devices with their start and end apart: 9 -> 39, of which waited for: 5 -> 24; matrix products, arithmetic and copies ran while one was open for 4% -> 12% of each run, Pallas kernels for 0% -> 0%
where the time goes in v5:
time: 263 us; the launch traced here: 262 us
  starting transfers between devices  126 us (48%)
  waiting for transfers between devices  75.7 us (29%)
  local copies, waits for them, and re-layouts  37.6 us (14%)
  Pallas kernels  12.5 us (5%)
  other arithmetic  6.2 us (2%)
  matrix products  2.8 us (1%)
    ppermute x31, starting transfers between devices, on_device(): pieces.append(lax.ppermute(outgoing[step], 'dev', pairs))  73.8 us
    ppermute x31, waiting for transfers between devices, on_device(): pieces.append(lax.ppermute(outgoing[step], 'dev', pairs))  67.1 us
    ppermute x7, starting transfers between devices, on_device(): mine = mine + lax.ppermute(part, 'grp', pairs)  45.2 us
    unnamed x56, local copies, waits for them, and re-layouts  25.3 us
    pallas_call x1, Pallas kernels, class_pass(): pl.pallas_call(functools.partial(class_kernel, pix, groups), out_shape=(j...  12.5 us
    ppermute x7, waiting for transfers between devices, on_device(): mine = mine + lax.ppermute(part, 'grp', pairs)  8.63 us
    all_to_all x1, starting transfers between devices, on_device(): lax.all_to_all(by_source, 'dev', split_axis=0, concat_axis=0, tiled=True)  7.38 us
  transfers between devices with their start and end apart: 39, of which 24 were waited for; matrix products, arithmetic and copies ran while one was open for 12% of the time, Pallas kernels for 0%

profile of v5, /device:TPU:1, one launch (start us, length us, event | category | flops | bytes accessed | tf_op | source)
XLA Modules:
  0.0 262.1 jit_solution(12860653971806756573)
XLA Ops:
  2.9 1.9 convolution_convert_fusion
  4.8 1.4 copy-done.3
  6.7 4.7 %collective-permute-start.11 = (bf16[2,16512]{1,0:T(2,128)(2,1)S(1)}, bf16[2,16512]{1,0:T(2,128)(2,1)S(1)}, u32[]{:S(2)}, u32[]{:S(2)}) collective-permute-start(bf16[2,16512]{1,0:T(2,128)(2,1)S(1)} %get-tuple-element.35), channel_id=1, source_target_pairs={{0,12},{1,13},{2,14},{3,15},{4,16},{5,17},{6,18},{7,19},{8,20},{9,... | collective-permute-start | bytes 198152 | tf_op jit(solution)/shard_map/ppermute | solution.py:185
  11.5 2.5 collective-permute-start.10
  14.5 1.5 collective-permute-start.8
  19.0 4.4 %fusion.58 = (bf16[2,16512]{1,0:T(2,128)(2,1)S(1)}, bf16[2,16512]{1,0:T(2,128)(2,1)S(1)}, bf16[2,16512]{1,0:T(2,128)(2,1)S(1)}, bf16[2,16512]{1,0:T(2,128)(2,1)S...) fusion(bf16[64,16512]{1,0:T(8,128)(2,1)} %copy-done.3), kind=kLoop, calls=%fused_computation.130 | loop fusion | bytes 2509824 | tf_op jit(solution)/shard_map/slice | solution.py:185
  23.5 1.6 fusion.18
  28.6 5.5 %collective-permute-done.1 = bf16[2,16512]{1,0:T(2,128)(2,1)S(1)} collective-permute-done((bf16[2,16512]{1,0:T(2,128)(2,1)S(1)}, bf16[2,16512]{1,0:T(2,128)(2,1)S(1)}, u32[]{:S(2)}, u32[]{:S(2)}) %collective-permute-start.1) | collective-permute-done | bytes 66080 | tf_op jit(solution)/shard_map/ppermute | solution.py:185
  34.8 7.1 %collective-permute-done.2 = bf16[2,16512]{1,0:T(2,128)(2,1)S(1)} collective-permute-done((bf16[2,16512]{1,0:T(2,128)(2,1)S(1)}, bf16[2,16512]{1,0:T(2,128)(2,1)S(1)}, u32[]{:S(2)}, u32[]{:S(2)}) %collective-permute-start.2) | collective-permute-done | bytes 66080 | tf_op jit(solution)/shard_map/ppermute | solution.py:185
  42.5 6.1 %collective-permute-done.3 = bf16[2,16512]{1,0:T(2,128)(2,1)S(1)} collective-permute-done((bf16[2,16512]{1,0:T(2,128)(2,1)S(1)}, bf16[2,16512]{1,0:T(2,128)(2,1)S(1)}, u32[]{:S(2)}, u32[]{:S(2)}) %collective-permute-start.3) | collective-permute-done | bytes 66080 | tf_op jit(solution)/shard_map/ppermute | solution.py:185
  49.2 6.6 %collective-permute-done.4 = bf16[2,16512]{1,0:T(2,128)(2,1)S(1)} collective-permute-done((bf16[2,16512]{1,0:T(2,128)(2,1)S(1)}, bf16[2,16512]{1,0:T(2,128)(2,1)S(1)}, u32[]{:S(2)}, u32[]{:S(2)}) %collective-permute-start.4) | collective-permute-done | bytes 66080 | tf_op jit(solution)/shard_map/ppermute | solution.py:185
  56.6 4.6 %collective-permute-done.5 = bf16[2,16512]{1,0:T(2,128)(2,1)S(1)} collective-permute-done((bf16[2,16512]{1,0:T(2,128)(2,1)S(1)}, bf16[2,16512]{1,0:T(2,128)(2,1)S(1)}, u32[]{:S(2)}, u32[]{:S(2)}) %collective-permute-start.5) | collective-permute-done | bytes 66080 | tf_op jit(solution)/shard_map/ppermute | solution.py:185
  61.8 5.1 %collective-permute-done.6 = bf16[2,16512]{1,0:T(2,128)(2,1)S(1)} collective-permute-done((bf16[2,16512]{1,0:T(2,128)(2,1)S(1)}, bf16[2,16512]{1,0:T(2,128)(2,1)S(1)}, u32[]{:S(2)}, u32[]{:S(2)}) %collective-permute-start.6) | collective-permute-done | bytes 66080 | tf_op jit(solution)/shard_map/ppermute | solution.py:185
  67.6 3.7 %collective-permute-done.7 = bf16[2,16512]{1,0:T(2,128)(2,1)S(1)} collective-permute-done((bf16[2,16512]{1,0:T(2,128)(2,1)S(1)}, bf16[2,16512]{1,0:T(2,128)(2,1)S(1)}, u32[]{:S(2)}, u32[]{:S(2)}) %collective-permute-start.7) | collective-permute-done | bytes 66080 | tf_op jit(solution)/shard_map/ppermute | solution.py:185
  71.3 1.7 collective-permute-start.30
  75.0 2.5 collective-permute-start.27
  78.2 2.2 collective-permute-start.12
  81.1 5.5 %collective-permute-done.12 = bf16[2,16512]{1,0:T(2,128)(2,1)S(1)} collective-permute-done((bf16[2,16512]{1,0:T(2,128)(2,1)}, bf16[2,16512]{1,0:T(2,128)(2,1)S(1)}, u32[]{:S(2)}, u32[]{:S(2)}) %collective-permute-start.12) | collective-permute-done | bytes 66080 | tf_op jit(solution)/shard_map/ppermute | solution.py:185
  87.6 4.7 %collective-permute-done.13 = bf16[2,16512]{1,0:T(2,128)(2,1)S(1)} collective-permute-done((bf16[2,16512]{1,0:T(2,128)(2,1)}, bf16[2,16512]{1,0:T(2,128)(2,1)S(1)}, u32[]{:S(2)}, u32[]{:S(2)}) %collective-permute-start.13) | collective-permute-done | bytes 66080 | tf_op jit(solution)/shard_map/ppermute | solution.py:185
  92.3 3.0 %collective-permute-start.14 = (bf16[2,16512]{1,0:T(2,128)(2,1)}, bf16[2,16512]{1,0:T(2,128)(2,1)S(1)}, u32[]{:S(2)}, u32[]{:S(2)}) collective-permute-start(bf16[2,16512]{1,0:T(2,128)(2,1)} %get-tuple-element.32), channel_id=1, source_target_pairs={{0,15},{1,16},{2,17},{3,18},{4,19},{5,20},{6,21},{7,22},{8,23},{9,... | collective-permute-start | bytes 198152 | tf_op jit(solution)/shard_map/ppermute | solution.py:185
  95.9 3.1 %collective-permute-done.14 = bf16[2,16512]{1,0:T(2,128)(2,1)S(1)} collective-permute-done((bf16[2,16512]{1,0:T(2,128)(2,1)}, bf16[2,16512]{1,0:T(2,128)(2,1)S(1)}, u32[]{:S(2)}, u32[]{:S(2)}) %collective-permute-start.14) | collective-permute-done | bytes 66080 | tf_op jit(solution)/shard_map/ppermute | solution.py:185
  99.0 2.4 collective-permute-start.15
  102.1 1.9 collective-permute-done.15
  104.0 1.5 collective-permute-start.16
  106.1 3.5 %collective-permute-done.16 = bf16[2,16512]{1,0:T(2,128)(2,1)S(1)} collective-permute-done((bf16[2,16512]{1,0:T(2,128)(2,1)}, bf16[2,16512]{1,0:T(2,128)(2,1)S(1)}, u32[]{:S(2)}, u32[]{:S(2)}) %collective-permute-start.16) | collective-permute-done | bytes 66080 | tf_op jit(solution)/shard_map/ppermute | solution.py:185
  109.7 1.7 collective-permute-start.17
  112.1 2.8 %collective-permute-done.17 = bf16[2,16512]{1,0:T(2,128)(2,1)S(1)} collective-permute-done((bf16[2,16512]{1,0:T(2,128)(2,1)S(1)}, bf16[2,16512]{1,0:T(2,128)(2,1)S(1)}, u32[]{:S(2)}, u32[]{:S(2)}) %collective-permute-start.17) | collective-permute-done | bytes 66080 | tf_op jit(solution)/shard_map/ppermute | solution.py:185
  114.9 5.0 %collective-permute-start.18 = (bf16[2,16512]{1,0:T(2,128)(2,1)S(1)}, bf16[2,16512]{1,0:T(2,128)(2,1)S(1)}, u32[]{:S(2)}, u32[]{:S(2)}) collective-permute-start(bf16[2,16512]{1,0:T(2,128)(2,1)S(1)} %copy-done.5), channel_id=1, source_target_pairs={{0,19},{1,20},{2,21},{3,22},{4,23},{5,24},{6,25},{7,26},{8,27},{9,... | collective-permute-start | bytes 198152 | tf_op jit(solution)/shard_map/ppermute | solution.py:185
  121.2 3.5 %collective-permute-start.19 = (bf16[2,16512]{1,0:T(2,128)(2,1)S(1)}, bf16[2,16512]{1,0:T(2,128)(2,1)S(1)}, u32[]{:S(2)}, u32[]{:S(2)}) collective-permute-start(bf16[2,16512]{1,0:T(2,128)(2,1)S(1)} %copy-done.4), channel_id=1, source_target_pairs={{0,20},{1,21},{2,22},{3,23},{4,24},{5,25},{6,26},{7,27},{8,28},{9,... | collective-permute-start | bytes 198152 | tf_op jit(solution)/shard_map/ppermute | solution.py:185
  125.4 1.4 collective-permute-done.19
  126.8 9.4 %collective-permute-start.20 = (bf16[2,16512]{1,0:T(2,128)(2,1)S(1)}, bf16[2,16512]{1,0:T(2,128)(2,1)S(1)}, u32[]{:S(2)}, u32[]{:S(2)}) collective-permute-start(bf16[2,16512]{1,0:T(2,128)(2,1)S(1)} %get-tuple-element.26), channel_id=1, source_target_pairs={{0,21},{1,22},{2,23},{3,24},{4,25},{5,26},{6,27},{7,28},{8,29},{9,... | collective-permute-start | bytes 198152 | tf_op jit(solution)/shard_map/ppermute | solution.py:185
  137.5 2.7 %collective-permute-start.21 = (bf16[2,16512]{1,0:T(2,128)(2,1)S(1)}, bf16[2,16512]{1,0:T(2,128)(2,1)S(1)}, u32[]{:S(2)}, u32[]{:S(2)}) collective-permute-start(bf16[2,16512]{1,0:T(2,128)(2,1)S(1)} %get-tuple-element.25), channel_id=1, source_target_pairs={{0,22},{1,23},{2,24},{3,25},{4,26},{5,27},{6,28},{7,29},{8,30},{9,... | collective-permute-start | bytes 198152 | tf_op jit(solution)/shard_map/ppermute | solution.py:185
  141.5 6.5 %collective-permute-start.22 = (bf16[2,16512]{1,0:T(2,128)(2,1)S(1)}, bf16[2,16512]{1,0:T(2,128)(2,1)S(1)}, u32[]{:S(2)}, u32[]{:S(2)}) collective-permute-start(bf16[2,16512]{1,0:T(2,128)(2,1)S(1)} %get-tuple-element.24), channel_id=1, source_target_pairs={{0,23},{1,24},{2,25},{3,26},{4,27},{5,28},{6,29},{7,30},{8,31},{9,... | collective-permute-start | bytes 198152 | tf_op jit(solution)/shard_map/ppermute | solution.py:185
  149.5 1.8 collective-permute-start.23
  152.6 5.9 %collective-permute-start.24 = (bf16[2,16512]{1,0:T(2,128)(2,1)S(1)}, bf16[2,16512]{1,0:T(2,128)(2,1)S(1)}, u32[]{:S(2)}, u32[]{:S(2)}) collective-permute-start(bf16[2,16512]{1,0:T(2,128)(2,1)S(1)} %get-tuple-element.22), channel_id=1, source_target_pairs={{0,25},{1,26},{2,27},{3,28},{4,29},{5,30},{6,31},{7,0},{8,1},{9,2}... | collective-permute-start | bytes 198152 | tf_op jit(solution)/shard_map/ppermute | solution.py:185
  159.9 3.7 %collective-permute-start.25 = (bf16[2,16512]{1,0:T(2,128)(2,1)S(1)}, bf16[2,16512]{1,0:T(2,128)(2,1)S(1)}, u32[]{:S(2)}, u32[]{:S(2)}) collective-permute-start(bf16[2,16512]{1,0:T(2,128)(2,1)S(1)} %get-tuple-element.21), channel_id=1, source_target_pairs={{0,26},{1,27},{2,28},{3,29},{4,30},{5,31},{6,0},{7,1},{8,2},{9,3},... | collective-permute-start | bytes 198152 | tf_op jit(solution)/shard_map/ppermute | solution.py:185
  164.9 8.3 %collective-permute-start.26 = (bf16[2,16512]{1,0:T(2,128)(2,1)S(1)}, bf16[2,16512]{1,0:T(2,128)(2,1)S(1)}, u32[]{:S(2)}, u32[]{:S(2)}) collective-permute-start(bf16[2,16512]{1,0:T(2,128)(2,1)S(1)} %get-tuple-element.20), channel_id=1, source_target_pairs={{0,27},{1,28},{2,29},{3,30},{4,31},{5,0},{6,1},{7,2},{8,3},{9,4},{... | collective-permute-start | bytes 198152 | tf_op jit(solution)/shard_map/ppermute | solution.py:185
  177.9 2.8 %reshape.279.rows_ref = bf16[64,16512]{1,0:T(8,128)(2,1)S(1)} reshape(bf16[32,2,16512]{2,1,0:T(2,128)(2,1)} %bitcast_dynamic-update-slice_fusion) | data formatting | bytes 4227072 | tf_op jit(solution)/shard_map/reshape | solution.py:186
  180.8 1.4 copy-done.1
  182.2 12.5 %shard_map.77 = (f32[8,136,128]{2,1,0:T(8,128)S(1)}, f32[1,64]{1,0:T(1,128)S(1)}) custom-call(bf16[64,16512]{1,0:T(8,128)(2,1)S(1)} %reshape.279.rows_ref, bf16[48,16384]{1,0:T(8,128)(2,1)S(1)} %bitcast.113, f32[1,64]{1,0:T(1,128)S(1)} %bitcast.114, f32[48,1]{1,0:T(8,128)S(1)} %copy.21.energy_ref, f32[8,48]{1,0:T(8,128)S(1)} %copy-done.2), custom_call_target="tpu_custom_call" | custom-call | flops 1207959552 | bytes 4210688 | tf_op jit(solution)/shard_map/pallas_call | solution.py:135
  196.2 1.7 collective-permute-start.31
  197.9 12.4 %collective-permute-start.37 = (f32[136,128]{1,0:T(8,128)S(1)}, f32[136,128]{1,0:T(8,128)S(1)}, u32[]{:S(2)}, u32[]{:S(2)}) collective-permute-start(f32[136,128]{1,0:T(8,128)S(1)} %get-tuple-element.48), channel_id=1, source_target_pairs={{0,224},{32,0},{64,32},{96,64},{128,96},{160,128},{192,160},{224,1... | collective-permute-start | bytes 208904 | tf_op jit(solution)/shard_map/ppermute | solution.py:206
  211.1 7.4 %all-to-all-start = ((f32[32,1,2]{2,1,0:T(1,128)}), f32[32,1,2]{2,1,0:T(1,128)S(1)}, u32[]{:S(2)}, u32[]{:S(2)}) async-start(f32[32,1,2]{2,1,0:T(1,128)} %copy.24), calls=%async_computation | async-start | bytes 32768 | tf_op jit(solution)/shard_map/all_to_all | solution.py:195
  218.5 11.9 %collective-permute-start.36 = (f32[136,128]{1,0:T(8,128)S(1)}, f32[136,128]{1,0:T(8,128)S(1)}, u32[]{:S(2)}, u32[]{:S(2)}) collective-permute-start(f32[136,128]{1,0:T(8,128)S(1)} %get-tuple-element.49), channel_id=1, source_target_pairs={{0,192},{32,224},{64,0},{96,32},{128,64},{160,96},{192,128},{224,1... | collective-permute-start | bytes 208904 | tf_op jit(solution)/shard_map/ppermute | solution.py:206
  230.4 11.8 %collective-permute-start.35 = (f32[136,128]{1,0:T(8,128)S(1)}, f32[136,128]{1,0:T(8,128)S(1)}, u32[]{:S(2)}, u32[]{:S(2)}) collective-permute-start(f32[136,128]{1,0:T(8,128)S(1)} %get-tuple-element.50), channel_id=1, source_target_pairs={{0,160},{32,192},{64,224},{96,0},{128,32},{160,64},{192,96},{224,1... | collective-permute-start | bytes 208904 | tf_op jit(solution)/shard_map/ppermute | solution.py:206
  242.2 6.2 %collective-permute-start.34 = (f32[136,128]{1,0:T(8,128)S(1)}, f32[136,128]{1,0:T(8,128)S(1)}, u32[]{:S(2)}, u32[]{:S(2)}) collective-permute-start(f32[136,128]{1,0:T(8,128)S(1)} %get-tuple-element.51), channel_id=1, source_target_pairs={{0,128},{32,160},{64,192},{96,224},{128,0},{160,32},{192,64},{224,... | collective-permute-start | bytes 208904 | tf_op jit(solution)/shard_map/ppermute | solution.py:206
  251.7 6.8 %collective-permute-done.33 = f32[136,128]{1,0:T(8,128)S(1)} collective-permute-done((f32[136,128]{1,0:T(8,128)S(1)}, f32[136,128]{1,0:T(8,128)S(1)}, u32[]{:S(2)}, u32[]{:S(2)}) %collective-permute-start.33) | collective-permute-done | bytes 69664 | tf_op jit(solution)/shard_map/ppermute | solution.py:206
  258.5 1.8 collective-permute-done.32
  (121 shorter events, 43.2 us)
Async XLA Ops:
  6.1 18.9 %copy-start = (bf16[1,48,16384]{2,1,0:T(8,128)(2,1)S(1)}, bf16[1,48,16384]{2,1,0:T(8,128)(2,1)}, u32[]{:S(2)}) copy-start(bf16[1,48,16384]{2,1,0:T(8,128)(2,1)} %param.10) | copy-start | bytes 4718596
  6.7 71.5 %collective-permute-start.11 = (bf16[2,16512]{1,0:T(2,128)(2,1)S(1)}, bf16[2,16512]{1,0:T(2,128)(2,1)S(1)}, u32[]{:S(2)}, u32[]{:S(2)}) collective-permute-start(bf16[2,16512]{1,0:T(2,128)(2,1)S(1)} %get-tuple-element.35), channel_id=1, source_target_pairs={{0,12},{1,13},{2,14},{3,15},{4,16},{5,17},{6,18},{7,19},{8,20},{9,... | collective-permute-start | bytes 198152 | tf_op jit(solution)/shard_map/ppermute | solution.py:185
  11.5 63.5 %collective-permute-start.10 = (bf16[2,16512]{1,0:T(2,128)(2,1)S(1)}, bf16[2,16512]{1,0:T(2,128)(2,1)S(1)}, u32[]{:S(2)}, u32[]{:S(2)}) collective-permute-start(bf16[2,16512]{1,0:T(2,128)(2,1)S(1)} %get-tuple-element.36), channel_id=1, source_target_pairs={{0,11},{1,12},{2,13},{3,14},{4,15},{5,16},{6,17},{7,18},{8,19},{9,... | collective-permute-start | bytes 198152 | tf_op jit(solution)/shard_map/ppermute | solution.py:185
  13.9 60.4 %collective-permute-start.9 = (bf16[2,16512]{1,0:T(2,128)(2,1)S(1)}, bf16[2,16512]{1,0:T(2,128)(2,1)S(1)}, u32[]{:S(2)}, u32[]{:S(2)}) collective-permute-start(bf16[2,16512]{1,0:T(2,128)(2,1)S(1)} %get-tuple-element.37), channel_id=1, source_target_pairs={{0,10},{1,11},{2,12},{3,13},{4,14},{5,15},{6,16},{7,17},{8,18},{9,... | collective-permute-start | bytes 198152 | tf_op jit(solution)/shard_map/ppermute | solution.py:185
  14.5 59.1 %collective-permute-start.8 = (bf16[2,16512]{1,0:T(2,128)(2,1)S(1)}, bf16[2,16512]{1,0:T(2,128)(2,1)S(1)}, u32[]{:S(2)}, u32[]{:S(2)}) collective-permute-start(bf16[2,16512]{1,0:T(2,128)(2,1)S(1)} %get-tuple-element.38), channel_id=1, source_target_pairs={{0,9},{1,10},{2,11},{3,12},{4,13},{5,14},{6,15},{7,16},{8,17},{9,1... | collective-permute-start | bytes 198152 | tf_op jit(solution)/shard_map/ppermute | solution.py:185
  16.1 10.7 %collective-permute-start = (bf16[2,16512]{1,0:T(2,128)(2,1)S(1)}, bf16[2,16512]{1,0:T(2,128)(2,1)S(1)}, u32[]{:S(2)}, u32[]{:S(2)}) collective-permute-start(bf16[2,16512]{1,0:T(2,128)(2,1)S(1)} %get-tuple-element.46), channel_id=1, source_target_pairs={{0,1},{1,2},{2,3},{3,4},{4,5},{5,6},{6,7},{7,8},{8,9},{9,10},{10,1... | collective-permute-start | bytes 198152 | tf_op jit(solution)/shard_map/ppermute | solution.py:185
  26.0 83.7 %copy-start.6 = (bf16[2,16512]{1,0:T(2,128)(2,1)S(1)}, bf16[2,16512]{1,0:T(2,128)(2,1)}, u32[]{:S(2)}) copy-start(bf16[2,16512]{1,0:T(2,128)(2,1)} %get-tuple-element.29) | copy-start | bytes 198148
  26.0 88.9 %copy-start.5 = (bf16[2,16512]{1,0:T(2,128)(2,1)S(1)}, bf16[2,16512]{1,0:T(2,128)(2,1)}, u32[]{:S(2)}) copy-start(bf16[2,16512]{1,0:T(2,128)(2,1)} %get-tuple-element.28) | copy-start | bytes 198148
  26.0 95.2 %copy-start.4 = (bf16[2,16512]{1,0:T(2,128)(2,1)S(1)}, bf16[2,16512]{1,0:T(2,128)(2,1)}, u32[]{:S(2)}) copy-start(bf16[2,16512]{1,0:T(2,128)(2,1)} %get-tuple-element.27) | copy-start | bytes 198148
  26.8 7.3 %collective-permute-start.1 = (bf16[2,16512]{1,0:T(2,128)(2,1)S(1)}, bf16[2,16512]{1,0:T(2,128)(2,1)S(1)}, u32[]{:S(2)}, u32[]{:S(2)}) collective-permute-start(bf16[2,16512]{1,0:T(2,128)(2,1)S(1)} %get-tuple-element.45), channel_id=1, source_target_pairs={{0,2},{1,3},{2,4},{3,5},{4,6},{5,7},{6,8},{7,9},{8,10},{9,11},{10,... | collective-permute-start | bytes 198152 | tf_op jit(solution)/shard_map/ppermute | solution.py:185
  34.1 7.7 %collective-permute-start.2 = (bf16[2,16512]{1,0:T(2,128)(2,1)S(1)}, bf16[2,16512]{1,0:T(2,128)(2,1)S(1)}, u32[]{:S(2)}, u32[]{:S(2)}) collective-permute-start(bf16[2,16512]{1,0:T(2,128)(2,1)S(1)} %get-tuple-element.44), channel_id=1, source_target_pairs={{0,3},{1,4},{2,5},{3,6},{4,7},{5,8},{6,9},{7,10},{8,11},{9,12},{10... | collective-permute-start | bytes 198152 | tf_op jit(solution)/shard_map/ppermute | solution.py:185
  41.8 6.7 %collective-permute-start.3 = (bf16[2,16512]{1,0:T(2,128)(2,1)S(1)}, bf16[2,16512]{1,0:T(2,128)(2,1)S(1)}, u32[]{:S(2)}, u32[]{:S(2)}) collective-permute-start(bf16[2,16512]{1,0:T(2,128)(2,1)S(1)} %get-tuple-element.43), channel_id=1, source_target_pairs={{0,4},{1,5},{2,6},{3,7},{4,8},{5,9},{6,10},{7,11},{8,12},{9,13},{1... | collective-permute-start | bytes 198152 | tf_op jit(solution)/shard_map/ppermute | solution.py:185
  48.6 7.3 %collective-permute-start.4 = (bf16[2,16512]{1,0:T(2,128)(2,1)S(1)}, bf16[2,16512]{1,0:T(2,128)(2,1)S(1)}, u32[]{:S(2)}, u32[]{:S(2)}) collective-permute-start(bf16[2,16512]{1,0:T(2,128)(2,1)S(1)} %get-tuple-element.42), channel_id=1, source_target_pairs={{0,5},{1,6},{2,7},{3,8},{4,9},{5,10},{6,11},{7,12},{8,13},{9,14},{... | collective-permute-start | bytes 198152 | tf_op jit(solution)/shard_map/ppermute | solution.py:185
  55.9 5.2 %collective-permute-start.5 = (bf16[2,16512]{1,0:T(2,128)(2,1)S(1)}, bf16[2,16512]{1,0:T(2,128)(2,1)S(1)}, u32[]{:S(2)}, u32[]{:S(2)}) collective-permute-start(bf16[2,16512]{1,0:T(2,128)(2,1)S(1)} %get-tuple-element.41), channel_id=1, source_target_pairs={{0,6},{1,7},{2,8},{3,9},{4,10},{5,11},{6,12},{7,13},{8,14},{9,15},... | collective-permute-start | bytes 198152 | tf_op jit(solution)/shard_map/ppermute | solution.py:185
  61.1 5.8 %collective-permute-start.6 = (bf16[2,16512]{1,0:T(2,128)(2,1)S(1)}, bf16[2,16512]{1,0:T(2,128)(2,1)S(1)}, u32[]{:S(2)}, u32[]{:S(2)}) collective-permute-start(bf16[2,16512]{1,0:T(2,128)(2,1)S(1)} %get-tuple-element.40), channel_id=1, source_target_pairs={{0,7},{1,8},{2,9},{3,10},{4,11},{5,12},{6,13},{7,14},{8,15},{9,16}... | collective-permute-start | bytes 198152 | tf_op jit(solution)/shard_map/ppermute | solution.py:185
  66.9 4.3 %collective-permute-start.7 = (bf16[2,16512]{1,0:T(2,128)(2,1)S(1)}, bf16[2,16512]{1,0:T(2,128)(2,1)S(1)}, u32[]{:S(2)}, u32[]{:S(2)}) collective-permute-start(bf16[2,16512]{1,0:T(2,128)(2,1)S(1)} %get-tuple-element.39), channel_id=1, source_target_pairs={{0,8},{1,9},{2,10},{3,11},{4,12},{5,13},{6,14},{7,15},{8,16},{9,17... | collective-permute-start | bytes 198152 | tf_op jit(solution)/shard_map/ppermute | solution.py:185
  71.3 105.9 %collective-permute-start.30 = (bf16[2,16512]{1,0:T(2,128)(2,1)S(1)}, bf16[2,16512]{1,0:T(2,128)(2,1)S(1)}, u32[]{:S(2)}, u32[]{:S(2)}) collective-permute-start(bf16[2,16512]{1,0:T(2,128)(2,1)S(1)} %get-tuple-element.16), channel_id=1, source_target_pairs={{0,31},{1,0},{2,1},{3,2},{4,3},{5,4},{6,5},{7,6},{8,7},{9,8},{10,9... | collective-permute-start | bytes 198152 | tf_op jit(solution)/shard_map/ppermute | solution.py:185
  73.6 102.9 %collective-permute-start.29 = (bf16[2,16512]{1,0:T(2,128)(2,1)S(1)}, bf16[2,16512]{1,0:T(2,128)(2,1)S(1)}, u32[]{:S(2)}, u32[]{:S(2)}) collective-permute-start(bf16[2,16512]{1,0:T(2,128)(2,1)S(1)} %get-tuple-element.17), channel_id=1, source_target_pairs={{0,30},{1,31},{2,0},{3,1},{4,2},{5,3},{6,4},{7,5},{8,6},{9,7},{10,... | collective-permute-start | bytes 198152 | tf_op jit(solution)/shard_map/ppermute | solution.py:185
  74.3 101.5 %collective-permute-start.28 = (bf16[2,16512]{1,0:T(2,128)(2,1)S(1)}, bf16[2,16512]{1,0:T(2,128)(2,1)S(1)}, u32[]{:S(2)}, u32[]{:S(2)}) collective-permute-start(bf16[2,16512]{1,0:T(2,128)(2,1)S(1)} %get-tuple-element.18), channel_id=1, source_target_pairs={{0,29},{1,30},{2,31},{3,0},{4,1},{5,2},{6,3},{7,4},{8,5},{9,6},{10... | collective-permute-start | bytes 198152 | tf_op jit(solution)/shard_map/ppermute | solution.py:185
  75.0 100.2 %collective-permute-start.27 = (bf16[2,16512]{1,0:T(2,128)(2,1)S(1)}, bf16[2,16512]{1,0:T(2,128)(2,1)S(1)}, u32[]{:S(2)}, u32[]{:S(2)}) collective-permute-start(bf16[2,16512]{1,0:T(2,128)(2,1)S(1)} %get-tuple-element.19), channel_id=1, source_target_pairs={{0,28},{1,29},{2,30},{3,31},{4,0},{5,1},{6,2},{7,3},{8,4},{9,5},{1... | collective-permute-start | bytes 198152 | tf_op jit(solution)/shard_map/ppermute | solution.py:185
  78.2 8.3 %collective-permute-start.12 = (bf16[2,16512]{1,0:T(2,128)(2,1)}, bf16[2,16512]{1,0:T(2,128)(2,1)S(1)}, u32[]{:S(2)}, u32[]{:S(2)}) collective-permute-start(bf16[2,16512]{1,0:T(2,128)(2,1)} %get-tuple-element.34), channel_id=1, source_target_pairs={{0,13},{1,14},{2,15},{3,16},{4,17},{5,18},{6,19},{7,20},{8,21},{9,... | collective-permute-start | bytes 198152 | tf_op jit(solution)/shard_map/ppermute | solution.py:185
  86.5 5.7 %collective-permute-start.13 = (bf16[2,16512]{1,0:T(2,128)(2,1)}, bf16[2,16512]{1,0:T(2,128)(2,1)S(1)}, u32[]{:S(2)}, u32[]{:S(2)}) collective-permute-start(bf16[2,16512]{1,0:T(2,128)(2,1)} %get-tuple-element.33), channel_id=1, source_target_pairs={{0,14},{1,15},{2,16},{3,17},{4,18},{5,19},{6,20},{7,21},{8,22},{9,... | collective-permute-start | bytes 198152 | tf_op jit(solution)/shard_map/ppermute | solution.py:185
  92.3 6.7 %collective-permute-start.14 = (bf16[2,16512]{1,0:T(2,128)(2,1)}, bf16[2,16512]{1,0:T(2,128)(2,1)S(1)}, u32[]{:S(2)}, u32[]{:S(2)}) collective-permute-start(bf16[2,16512]{1,0:T(2,128)(2,1)} %get-tuple-element.32), channel_id=1, source_target_pairs={{0,15},{1,16},{2,17},{3,18},{4,19},{5,20},{6,21},{7,22},{8,23},{9,... | collective-permute-start | bytes 198152 | tf_op jit(solution)/shard_map/ppermute | solution.py:185
  99.0 4.9 %collective-permute-start.15 = (bf16[2,16512]{1,0:T(2,128)(2,1)}, bf16[2,16512]{1,0:T(2,128)(2,1)S(1)}, u32[]{:S(2)}, u32[]{:S(2)}) collective-permute-start(bf16[2,16512]{1,0:T(2,128)(2,1)} %get-tuple-element.31), channel_id=1, source_target_pairs={{0,16},{1,17},{2,18},{3,19},{4,20},{5,21},{6,22},{7,23},{8,24},{9,... | collective-permute-start | bytes 198152 | tf_op jit(solution)/shard_map/ppermute | solution.py:185
  104.0 5.7 %collective-permute-start.16 = (bf16[2,16512]{1,0:T(2,128)(2,1)}, bf16[2,16512]{1,0:T(2,128)(2,1)S(1)}, u32[]{:S(2)}, u32[]{:S(2)}) collective-permute-start(bf16[2,16512]{1,0:T(2,128)(2,1)} %get-tuple-element.30), channel_id=1, source_target_pairs={{0,17},{1,18},{2,19},{3,20},{4,21},{5,22},{6,23},{7,24},{8,25},{9,... | collective-permute-start | bytes 198152 | tf_op jit(solution)/shard_map/ppermute | solution.py:185
  109.7 5.2 %collective-permute-start.17 = (bf16[2,16512]{1,0:T(2,128)(2,1)S(1)}, bf16[2,16512]{1,0:T(2,128)(2,1)S(1)}, u32[]{:S(2)}, u32[]{:S(2)}) collective-permute-start(bf16[2,16512]{1,0:T(2,128)(2,1)S(1)} %copy-done.6), channel_id=1, source_target_pairs={{0,18},{1,19},{2,20},{3,21},{4,22},{5,23},{6,24},{7,25},{8,26},{9,... | collective-permute-start | bytes 198152 | tf_op jit(solution)/shard_map/ppermute | solution.py:185
  114.9 6.3 %collective-permute-start.18 = (bf16[2,16512]{1,0:T(2,128)(2,1)S(1)}, bf16[2,16512]{1,0:T(2,128)(2,1)S(1)}, u32[]{:S(2)}, u32[]{:S(2)}) collective-permute-start(bf16[2,16512]{1,0:T(2,128)(2,1)S(1)} %copy-done.5), channel_id=1, source_target_pairs={{0,19},{1,20},{2,21},{3,22},{4,23},{5,24},{6,25},{7,26},{8,27},{9,... | collective-permute-start | bytes 198152 | tf_op jit(solution)/shard_map/ppermute | solution.py:185
  121.2 5.5 %collective-permute-start.19 = (bf16[2,16512]{1,0:T(2,128)(2,1)S(1)}, bf16[2,16512]{1,0:T(2,128)(2,1)S(1)}, u32[]{:S(2)}, u32[]{:S(2)}) collective-permute-start(bf16[2,16512]{1,0:T(2,128)(2,1)S(1)} %copy-done.4), channel_id=1, source_target_pairs={{0,20},{1,21},{2,22},{3,23},{4,24},{5,25},{6,26},{7,27},{8,28},{9,... | collective-permute-start | bytes 198152 | tf_op jit(solution)/shard_map/ppermute | solution.py:185
  126.8 10.7 %collective-permute-start.20 = (bf16[2,16512]{1,0:T(2,128)(2,1)S(1)}, bf16[2,16512]{1,0:T(2,128)(2,1)S(1)}, u32[]{:S(2)}, u32[]{:S(2)}) collective-permute-start(bf16[2,16512]{1,0:T(2,128)(2,1)S(1)} %get-tuple-element.26), channel_id=1, source_target_pairs={{0,21},{1,22},{2,23},{3,24},{4,25},{5,26},{6,27},{7,28},{8,29},{9,... | collective-permute-start | bytes 198152 | tf_op jit(solution)/shard_map/ppermute | solution.py:185
  137.5 4.0 %collective-permute-start.21 = (bf16[2,16512]{1,0:T(2,128)(2,1)S(1)}, bf16[2,16512]{1,0:T(2,128)(2,1)S(1)}, u32[]{:S(2)}, u32[]{:S(2)}) collective-permute-start(bf16[2,16512]{1,0:T(2,128)(2,1)S(1)} %get-tuple-element.25), channel_id=1, source_target_pairs={{0,22},{1,23},{2,24},{3,25},{4,26},{5,27},{6,28},{7,29},{8,30},{9,... | collective-permute-start | bytes 198152 | tf_op jit(solution)/shard_map/ppermute | solution.py:185
  141.5 7.9 %collective-permute-start.22 = (bf16[2,16512]{1,0:T(2,128)(2,1)S(1)}, bf16[2,16512]{1,0:T(2,128)(2,1)S(1)}, u32[]{:S(2)}, u32[]{:S(2)}) collective-permute-start(bf16[2,16512]{1,0:T(2,128)(2,1)S(1)} %get-tuple-element.24), channel_id=1, source_target_pairs={{0,23},{1,24},{2,25},{3,26},{4,27},{5,28},{6,29},{7,30},{8,31},{9,... | collective-permute-start | bytes 198152 | tf_op jit(solution)/shard_map/ppermute | solution.py:185
  149.5 3.1 %collective-permute-start.23 = (bf16[2,16512]{1,0:T(2,128)(2,1)S(1)}, bf16[2,16512]{1,0:T(2,128)(2,1)S(1)}, u32[]{:S(2)}, u32[]{:S(2)}) collective-permute-start(bf16[2,16512]{1,0:T(2,128)(2,1)S(1)} %get-tuple-element.23), channel_id=1, source_target_pairs={{0,24},{1,25},{2,26},{3,27},{4,28},{5,29},{6,30},{7,31},{8,0},{9,1... | collective-permute-start | bytes 198152 | tf_op jit(solution)/shard_map/ppermute | solution.py:185
  152.6 7.3 %collective-permute-start.24 = (bf16[2,16512]{1,0:T(2,128)(2,1)S(1)}, bf16[2,16512]{1,0:T(2,128)(2,1)S(1)}, u32[]{:S(2)}, u32[]{:S(2)}) collective-permute-start(bf16[2,16512]{1,0:T(2,128)(2,1)S(1)} %get-tuple-element.22), channel_id=1, source_target_pairs={{0,25},{1,26},{2,27},{3,28},{4,29},{5,30},{6,31},{7,0},{8,1},{9,2}... | collective-permute-start | bytes 198152 | tf_op jit(solution)/shard_map/ppermute | solution.py:185
  159.9 5.0 %collective-permute-start.25 = (bf16[2,16512]{1,0:T(2,128)(2,1)S(1)}, bf16[2,16512]{1,0:T(2,128)(2,1)S(1)}, u32[]{:S(2)}, u32[]{:S(2)}) collective-permute-start(bf16[2,16512]{1,0:T(2,128)(2,1)S(1)} %get-tuple-element.21), channel_id=1, source_target_pairs={{0,26},{1,27},{2,28},{3,29},{4,30},{5,31},{6,0},{7,1},{8,2},{9,3},... | collective-permute-start | bytes 198152 | tf_op jit(solution)/shard_map/ppermute | solution.py:185
  164.9 9.6 %collective-permute-start.26 = (bf16[2,16512]{1,0:T(2,128)(2,1)S(1)}, bf16[2,16512]{1,0:T(2,128)(2,1)S(1)}, u32[]{:S(2)}, u32[]{:S(2)}) collective-permute-start(bf16[2,16512]{1,0:T(2,128)(2,1)S(1)} %get-tuple-element.20), channel_id=1, source_target_pairs={{0,27},{1,28},{2,29},{3,30},{4,31},{5,0},{6,1},{7,2},{8,3},{9,4},{... | collective-permute-start | bytes 198152 | tf_op jit(solution)/shard_map/ppermute | solution.py:185
  194.7 65.7 %copy-start.8 = (s32[256]{0:T(256)S(1)}, s32[256]{0:T(256)}, u32[]{:S(2)}) copy-start(s32[256]{0:T(256)} %get-tuple-element.54) | copy-start | bytes 3076
  194.7 65.7 %copy-start.9 = (s32[256]{0:T(256)S(1)}, s32[256]{0:T(256)}, u32[]{:S(2)}) copy-start(s32[256]{0:T(256)} %get-tuple-element.55) | copy-start | bytes 3076
  194.7 66.1 %copy-start.7 = (s32[32]{0:T(128)S(1)}, s32[32]{0:T(128)}, u32[]{:S(2)}) copy-start(s32[32]{0:T(128)} %get-tuple-element.56) | copy-start | bytes 388
  194.7 66.1 %copy-start.10 = (s32[32]{0:T(128)S(1)}, s32[32]{0:T(128)}, u32[]{:S(2)}) copy-start(s32[32]{0:T(128)} %broadcast_add_fusion) | copy-start | bytes 388
  194.7 66.1 %copy-start.11 = (pred[32]{0:T(512)(128)(4,1)S(1)}, pred[32]{0:T(512)(128)(4,1)}, u32[]{:S(2)}) copy-start(pred[32]{0:T(512)(128)(4,1)} %fusion.46) | copy-start | bytes 100
  196.2 53.7 %collective-permute-start.31 = (f32[136,128]{1,0:T(8,128)S(1)}, f32[136,128]{1,0:T(8,128)S(1)}, u32[]{:S(2)}, u32[]{:S(2)}) collective-permute-start(f32[136,128]{1,0:T(8,128)S(1)} %get-tuple-element.47), channel_id=1, source_target_pairs={{0,32},{32,64},{64,96},{96,128},{128,160},{160,192},{192,224},{224... | collective-permute-start | bytes 208904 | tf_op jit(solution)/shard_map/ppermute | solution.py:206
  197.9 53.2 %collective-permute-start.37 = (f32[136,128]{1,0:T(8,128)S(1)}, f32[136,128]{1,0:T(8,128)S(1)}, u32[]{:S(2)}, u32[]{:S(2)}) collective-permute-start(f32[136,128]{1,0:T(8,128)S(1)} %get-tuple-element.48), channel_id=1, source_target_pairs={{0,224},{32,0},{64,32},{96,64},{128,96},{160,128},{192,160},{224,1... | collective-permute-start | bytes 208904 | tf_op jit(solution)/shard_map/ppermute | solution.py:206
  211.1 37.4 %all-to-all-start = ((f32[32,1,2]{2,1,0:T(1,128)}), f32[32,1,2]{2,1,0:T(1,128)S(1)}, u32[]{:S(2)}, u32[]{:S(2)}) async-start(f32[32,1,2]{2,1,0:T(1,128)} %copy.24), calls=%async_computation | async-start | bytes 32768 | tf_op jit(solution)/shard_map/all_to_all | solution.py:195
  218.5 33.2 %collective-permute-start.36 = (f32[136,128]{1,0:T(8,128)S(1)}, f32[136,128]{1,0:T(8,128)S(1)}, u32[]{:S(2)}, u32[]{:S(2)}) collective-permute-start(f32[136,128]{1,0:T(8,128)S(1)} %get-tuple-element.49), channel_id=1, source_target_pairs={{0,192},{32,224},{64,0},{96,32},{128,64},{160,96},{192,128},{224,1... | collective-permute-start | bytes 208904 | tf_op jit(solution)/shard_map/ppermute | solution.py:206
  230.4 21.3 %collective-permute-start.35 = (f32[136,128]{1,0:T(8,128)S(1)}, f32[136,128]{1,0:T(8,128)S(1)}, u32[]{:S(2)}, u32[]{:S(2)}) collective-permute-start(f32[136,128]{1,0:T(8,128)S(1)} %get-tuple-element.50), channel_id=1, source_target_pairs={{0,160},{32,192},{64,224},{96,0},{128,32},{160,64},{192,96},{224,1... | collective-permute-start | bytes 208904 | tf_op jit(solution)/shard_map/ppermute | solution.py:206
  242.2 9.4 %collective-permute-start.34 = (f32[136,128]{1,0:T(8,128)S(1)}, f32[136,128]{1,0:T(8,128)S(1)}, u32[]{:S(2)}, u32[]{:S(2)}) collective-permute-start(f32[136,128]{1,0:T(8,128)S(1)} %get-tuple-element.51), channel_id=1, source_target_pairs={{0,128},{32,160},{64,192},{96,224},{128,0},{160,32},{192,64},{224,... | collective-permute-start | bytes 208904 | tf_op jit(solution)/shard_map/ppermute | solution.py:206
  249.9 8.5 %collective-permute-start.33 = (f32[136,128]{1,0:T(8,128)S(1)}, f32[136,128]{1,0:T(8,128)S(1)}, u32[]{:S(2)}, u32[]{:S(2)}) collective-permute-start(f32[136,128]{1,0:T(8,128)S(1)} %get-tuple-element.52), channel_id=1, source_target_pairs={{0,96},{32,128},{64,160},{96,192},{128,224},{160,0},{192,32},{224,... | collective-permute-start | bytes 208904 | tf_op jit(solution)/shard_map/ppermute | solution.py:206
  251.1 9.1 %collective-permute-start.32 = (f32[136,128]{1,0:T(8,128)S(1)}, f32[136,128]{1,0:T(8,128)S(1)}, u32[]{:S(2)}, u32[]{:S(2)}) collective-permute-start(f32[136,128]{1,0:T(8,128)S(1)} %get-tuple-element.53), channel_id=1, source_target_pairs={{0,64},{32,96},{64,128},{96,160},{128,192},{160,224},{192,0},{224,... | collective-permute-start | bytes 208904 | tf_op jit(solution)/shard_map/ppermute | solution.py:206
  (3 other events, 5.7 us)

commit v6 on v4

--- a/solution.py
+++ b/solution.py
@@ -60,14 +60,12 @@
 
     def products(j, carry):
         k0 = pl.multiple_of(j * TK, TK)
-        tile = ref_ref[:, pl.ds(k0, TK)]
+        tile = ref_ref[pl.ds(k0, TK), :]
         for ai, a in enumerate(SHIFTS):
             start = pl.multiple_of(k0 + IMG * (1 - a), IMG)
             for bi in range(3):
                 moved = ext_ref[bi, :, pl.ds(start, TK)]
-                acc_ref[ai * 3 + bi] += lax.dot_general(
-                    tile, moved, (((1,), (1,)), ((), ())), preferred_element_type=jnp.float32
-                )
+                acc_ref[ai * 3 + bi] += jnp.dot(moved, tile, preferred_element_type=jnp.float32)
         return carry
 
     lax.fori_loop(0, pix // TK, products, 0)
@@ -75,23 +73,24 @@
     scale = scale_ref[...]
     half_energy = 0.5 * energy_ref[...]
     scores = [scale * (acc_ref[t] - half_energy) for t in range(9)]
-    highest = jnp.max(scores[0], axis=0, keepdims=True)
+    highest = jnp.max(scores[0], axis=1, keepdims=True)
     for t in range(1, 9):
-        highest = jnp.maximum(highest, jnp.max(scores[t], axis=0, keepdims=True))
-    total = jnp.sum(jnp.exp(scores[0] - highest), axis=0, keepdims=True)
+        highest = jnp.maximum(highest, jnp.max(scores[t], axis=1, keepdims=True))
+    total = jnp.sum(jnp.exp(scores[0] - highest), axis=1, keepdims=True)
     for t in range(1, 9):
-        total = total + jnp.sum(jnp.exp(scores[t] - highest), axis=0, keepdims=True)
+        total = total + jnp.sum(jnp.exp(scores[t] - highest), axis=1, keepdims=True)
     evidence = highest + jnp.log(total)
     evid_ref[...] = evidence
     gain = gain_ref[...]
     gain_hi = gain.astype(jnp.bfloat16)
     gain_lo = (gain - gain_hi.astype(jnp.float32)).astype(jnp.bfloat16)
     depth = gain.shape[0]
+    contract = (((1,), (1,)), ((), ()))
     for t in range(9):
         weights = jnp.exp(scores[t] - evidence).astype(jnp.bfloat16)
-        mixed = jnp.dot(gain_hi, weights, preferred_element_type=jnp.float32) + jnp.dot(
-            gain_lo, weights, preferred_element_type=jnp.float32
-        )
+        mixed = lax.dot_general(
+            gain_hi, weights, contract, preferred_element_type=jnp.float32
+        ) + lax.dot_general(gain_lo, weights, contract, preferred_element_type=jnp.float32)
         mixed_hi = mixed.astype(jnp.bfloat16).astype(jnp.float32)
         v_ref[t, 0:depth] = mixed_hi
         v_ref[t, depth:2 * depth] = mixed - mixed_hi
@@ -124,7 +123,7 @@
 
 def class_pass(rows_ext, templates, scale_row, energy_col, gain, pix, groups):
     rowcount = rows_ext.shape[0]
-    refcount = templates.shape[0]
+    refcount = templates.shape[1]
     depth = gain.shape[0]
     vmem = pl.BlockSpec(memory_space=pltpu.VMEM)
     flops = 2 * 9 * (refcount + 2 * depth) * rowcount * pix
@@ -136,13 +135,13 @@
         functools.partial(class_kernel, pix, groups),
         out_shape=(
             jax.ShapeDtypeStruct((groups, depth * (pix // groups // IMG + 1), IMG), jnp.float32),
-            jax.ShapeDtypeStruct((1, rowcount), jnp.float32),
+            jax.ShapeDtypeStruct((rowcount, 1), jnp.float32),
         ),
         in_specs=[vmem] * 5,
         out_specs=(vmem, vmem),
         scratch_shapes=[
             pltpu.VMEM((3, rowcount, pix + 2 * IMG), jnp.bfloat16),
-            pltpu.VMEM((9, refcount, rowcount), jnp.float32),
+            pltpu.VMEM((9, rowcount, refcount), jnp.float32),
             pltpu.VMEM((9, 2 * depth, rowcount), jnp.float32),
         ],
         compiler_params=pltpu.CompilerParams(vmem_limit_bytes=48 * 1024 * 1024),
@@ -179,11 +178,11 @@
     outgoing = outgoing.reshape(slot_depth, sources, owned_classes * width)
     arrived = lax.all_to_all(outgoing, "dev", split_axis=1, concat_axis=1, tiled=True)
     rows_ext = arrived.reshape(slot_depth * sources, width)
-    scale_row = rows_ext[:, pix].astype(jnp.float32).reshape(1, slot_depth * sources)
+    scale_col = rows_ext[:, pix].astype(jnp.float32).reshape(slot_depth * sources, 1)
     templates = references[0]
-    energy_col = jnp.sum(jnp.square(templates.astype(jnp.float32)), axis=1).reshape(-1, 1)
+    energy_row = jnp.sum(jnp.square(templates.astype(jnp.float32)), axis=1).reshape(1, -1)
     windows, class_evidence = class_pass(
-        rows_ext, templates, scale_row, energy_col, insert_weights, pix, groups
+        rows_ext, templates.T, scale_col, energy_row, insert_weights, pix, groups
     )
     stacked = class_evidence.reshape(slot_depth, sources)
     returned = lax.all_to_all(stacked, "dev", split_axis=1, concat_axis=1, tiled=True).reshape(

time: 93.5 us -> 94.3 us (level)
  waiting for transfers between devices: 38.6 us -> 30.7 us
  Pallas kernels: 12.5 us -> 16.1 us
  other arithmetic: 2.68 us -> 5.39 us
  local copies, waits for them, and re-layouts: 8.66 us -> 11.2 us
    all_to_all x1, waiting for transfers between devices: 27.9 us -> 19.9 us  [on_device(): lax.all_to_all(outgoing, 'dev', split_axis=1, concat_axis=1, tiled=True)]
    unnamed x5 -> x4, local copies, waits for them, and re-layouts: 0.87 us -> 5.54 us
    pallas_call x1, Pallas kernels: 12.5 us -> 16.1 us  [class_pass(): pl.pallas_call(functools.partial(class_kernel, pix, groups), out_shape=(j...]
    reduce_sum x1, other arithmetic: 0.41 us -> 3.78 us  [on_device(): jnp.sum(jnp.square(templates.astype(jnp.float32)), axis=1).reshape(1, -1)]
    all_to_all x1, local copies, waits for them, and re-layouts: 1.8 us -> 0.21 us  [on_device(): lax.all_to_all(outgoing, 'dev', split_axis=1, concat_axis=1, tiled=True)]
  transfers between devices with their start and end apart: 9 -> 9, of which waited for: 5 -> 5; matrix products, arithmetic and copies ran while one was open for 4% -> 11% of each run, Pallas kernels for 0% -> 0%
where the time goes in v6:
time: 94.3 us; the launch traced here: 93.9 us
  waiting for transfers between devices  30.7 us (33%)
  starting transfers between devices  27 us (29%)
  Pallas kernels  16.1 us (17%)
  local copies, waits for them, and re-layouts  11.2 us (12%)
  other arithmetic  5.39 us (6%)
  matrix products  2.79 us (3%)
    all_to_all x1, waiting for transfers between devices, on_device(): lax.all_to_all(outgoing, 'dev', split_axis=1, concat_axis=1, tiled=True)  19.9 us
    pallas_call x1, Pallas kernels, class_pass(): pl.pallas_call(functools.partial(class_kernel, pix, groups), out_shape=(j...  16.1 us
    ppermute x7, starting transfers between devices, on_device(): mine = mine + lax.ppermute(part, 'grp', pairs)  13.5 us
    ppermute x7, waiting for transfers between devices, on_device(): mine = mine + lax.ppermute(part, 'grp', pairs)  8.76 us
    all_to_all x1, starting transfers between devices, on_device(): lax.all_to_all(outgoing, 'dev', split_axis=1, concat_axis=1, tiled=True)  8.59 us
    unnamed x4, local copies, waits for them, and re-layouts  5.54 us
    all_to_all x1, starting transfers between devices, on_device(): lax.all_to_all(stacked, 'dev', split_axis=1, concat_axis=1, tiled=True)  4.91 us
    reduce_sum x1, other arithmetic, on_device(): jnp.sum(jnp.square(templates.astype(jnp.float32)), axis=1).reshape(1, -1)  3.78 us
  transfers between devices with their start and end apart: 9, of which 5 were waited for; matrix products, arithmetic and copies ran while one was open for 11% of the time, Pallas kernels for 0%

profile of v6, /device:TPU:1, one launch (start us, length us, event | category | flops | bytes accessed | tf_op | source)
XLA Modules:
  0.0 93.9 jit_solution(15276317660272033)
XLA Ops:
  0.6 0.9 convert_reduce_fusion
  1.6 0.7 broadcast_in_dim.84
  2.3 1.9 %convolution_convert_fusion = bf16[64,16512]{1,0:T(8,128)(2,1)S(1)} fusion(bf16[32,128]{1,0:T(8,128)(2,1)S(1)} %broadcast_in_dim.84, bf16[32,16384]{1,0:T(8,128)(2,1)} %param.6, s32[32]{0:T(128)S(1)} %get-tuple-element.17), kind=kOutput, calls=%fused_computation.1 | convolution fusion | flops 70805504 | bytes 3170432 | tf_op jit(solution)/shard_map/dot_general | solution.py:177
  4.2 3.0 %copy.18 = bf16[2,32,16512]{2,0,1:T(2,128)(2,1)} copy(bf16[2,32,16512]{2,1,0:T(8,128)(2,1)S(1)} %bitcast.54) | data formatting | bytes 4227072 | tf_op jit(solution)/shard_map/reshape | solution.py:178
  7.2 8.6 %all-to-all-start = ((bf16[2,32,16512]{2,0,1:T(2,128)(2,1)}), bf16[2,32,16512]{2,0,1:T(2,128)(2,1)S(1)}, u32[]{:S(2)}, u32[]{:S(2)}) async-start(bf16[2,32,16512]{2,0,1:T(2,128)(2,1)} %copy.18), calls=%async_computation | async-start | bytes 4227072 | tf_op jit(solution)/shard_map/all_to_all | solution.py:179
  15.8 4.7 %copy.20 = bf16[1,48,16384]{1,2,0:T(8,128)(2,1)} copy(bf16[1,48,16384]{2,1,0:T(8,128)(2,1)} %param.10) | data formatting | bytes 3145728 | tf_op args[4]
  20.5 3.8 %multiply_reduce_fusion = f32[48]{0:T(128)S(1)} fusion(bf16[1,48,16384]{1,2,0:T(8,128)(2,1)} %copy.20), kind=kLoop, calls=%fused_computation.2 | loop fusion | flops 2359248 | bytes 1573056 | tf_op jit(solution)/shard_map/reduce_sum | solution.py:183
  24.3 0.0 copy-start
  24.3 19.9 %all-to-all-done = bf16[2,32,16512]{2,0,1:T(2,128)(2,1)S(1)} async-done(((bf16[2,32,16512]{2,0,1:T(2,128)(2,1)}), bf16[2,32,16512]{2,0,1:T(2,128)(2,1)S(1)}, u32[]{:S(2)}, u32[]{:S(2)}) %all-to-all-start) | async-done | bytes 2113568 | tf_op jit(solution)/shard_map/all_to_all | solution.py:179
  44.2 0.2 copy.19
  44.5 0.0 copy-done
  44.5 16.1 %shard_map.77 = (f32[8,136,128]{2,1,0:T(8,128)S(1)}, f32[64,1]{1,0:T(8,128)S(1)}) custom-call(bf16[64,16512]{1,0:T(8,128)(2,1)S(1)} %bitcast.51, bf16[16384,48]{1,0:T(8,128)(2,1)} %bitcast.53, f32[64,1]{1,0:T(8,128)S(1)} %slice_convert_fusion.scale_ref, f32[1,48]{1,0:T(1,128)S(1)} %bitcast.52, f32[8,48]{1,0:T(8,128)S(1)} %copy-done), custom_call_target="tpu_custom_call" | custom-call | flops 1207959552 | bytes 4210688 | tf_op jit(solution)/shard_map/pallas_call | solution.py:134
  60.6 0.1 dynamic-slice_bitcast_fusion.6
  60.7 5.6 %collective-permute-start.6 = (f32[136,128]{1,0:T(8,128)S(1)}, f32[136,128]{1,0:T(8,128)S(1)}, u32[]{:S(2)}, u32[]{:S(2)}) collective-permute-start(f32[136,128]{1,0:T(8,128)S(1)} %get-tuple-element.19), channel_id=1, source_target_pairs={{0,224},{32,0},{64,32},{96,64},{128,96},{160,128},{192,160},{224,1... | collective-permute-start | bytes 208904 | tf_op jit(solution)/shard_map/ppermute | solution.py:199
  66.3 1.2 %collective-permute-start.5 = (f32[136,128]{1,0:T(8,128)S(1)}, f32[136,128]{1,0:T(8,128)S(1)}, u32[]{:S(2)}, u32[]{:S(2)}) collective-permute-start(f32[136,128]{1,0:T(8,128)S(1)} %get-tuple-element.20), channel_id=1, source_target_pairs={{0,192},{32,224},{64,0},{96,32},{128,64},{160,96},{192,128},{224,1... | collective-permute-start | bytes 208904 | tf_op jit(solution)/shard_map/ppermute | solution.py:199
  67.5 0.1 reduce
  67.6 0.1 all_to_all.10
  67.7 0.7 copy.21
  68.4 4.9 %all-to-all-start.1 = ((f32[2,32,1]{0,2,1:T(1,128)}), f32[2,32,1]{0,2,1:T(1,128)S(1)}, u32[]{:S(2)}, u32[]{:S(2)}) async-start(f32[2,32,1]{0,2,1:T(1,128)} %copy.21), calls=%async_computation.1 | async-start | bytes 32768 | tf_op jit(solution)/shard_map/all_to_all | solution.py:188
  73.3 0.2 collective-permute-start.4
  73.5 4.8 %collective-permute-start.3 = (f32[136,128]{1,0:T(8,128)S(1)}, f32[136,128]{1,0:T(8,128)S(1)}, u32[]{:S(2)}, u32[]{:S(2)}) collective-permute-start(f32[136,128]{1,0:T(8,128)S(1)} %get-tuple-element.22), channel_id=1, source_target_pairs={{0,128},{32,160},{64,192},{96,224},{128,0},{160,32},{192,64},{224,... | collective-permute-start | bytes 208904 | tf_op jit(solution)/shard_map/ppermute | solution.py:199
  78.3 0.0 collective-permute-start.2
  78.3 2.0 %all-to-all-done.1 = f32[2,32,1]{0,2,1:T(1,128)S(1)} async-done(((f32[2,32,1]{0,2,1:T(1,128)}), f32[2,32,1]{0,2,1:T(1,128)S(1)}, u32[]{:S(2)}, u32[]{:S(2)}) %all-to-all-start.1) | async-done | bytes 288 | tf_op jit(solution)/shard_map/all_to_all | solution.py:188
  80.3 0.1 copy.22
  80.4 0.1 reshape.201
  80.4 0.7 gather_fusion
  81.1 0.0 collective-permute-done.6
  81.1 1.3 %collective-permute-start.1 = (f32[136,128]{1,0:T(8,128)S(1)}, f32[136,128]{1,0:T(8,128)S(1)}, u32[]{:S(2)}, u32[]{:S(2)}) collective-permute-start(f32[136,128]{1,0:T(8,128)S(1)} %get-tuple-element.24), channel_id=1, source_target_pairs={{0,64},{32,96},{64,128},{96,160},{128,192},{160,224},{192,0},{224,... | collective-permute-start | bytes 208904 | tf_op jit(solution)/shard_map/ppermute | solution.py:199
  82.4 0.0 collective-permute-done.5
  82.4 0.4 collective-permute-start
  82.8 0.5 and_select_fusion
  83.3 0.0 collective-permute-done.4
  83.3 0.0 collective-permute-done.3
  83.3 2.0 %collective-permute-done.2 = f32[136,128]{1,0:T(8,128)S(1)} collective-permute-done((f32[136,128]{1,0:T(8,128)S(1)}, f32[136,128]{1,0:T(8,128)S(1)}, u32[]{:S(2)}, u32[]{:S(2)}) %collective-permute-start.2) | collective-permute-done | bytes 69664 | tf_op jit(solution)/shard_map/ppermute | solution.py:199
  85.3 5.0 %collective-permute-done.1 = f32[136,128]{1,0:T(8,128)S(1)} collective-permute-done((f32[136,128]{1,0:T(8,128)S(1)}, f32[136,128]{1,0:T(8,128)S(1)}, u32[]{:S(2)}, u32[]{:S(2)}) %collective-permute-start.1) | collective-permute-done | bytes 69664 | tf_op jit(solution)/shard_map/ppermute | solution.py:199
  90.3 1.8 %collective-permute-done = f32[136,128]{1,0:T(8,128)S(1)} collective-permute-done((f32[136,128]{1,0:T(8,128)S(1)}, f32[136,128]{1,0:T(8,128)S(1)}, u32[]{:S(2)}, u32[]{:S(2)}) %collective-permute-start) | collective-permute-done | bytes 69664 | tf_op jit(solution)/shard_map/ppermute | solution.py:199
  92.1 0.5 fusion.7
  92.6 0.4 fusion.30
  93.0 0.9 copy.23
  (9 shorter events, 0.1 us)
Async XLA Ops:
  7.2 37.1 %all-to-all-start = ((bf16[2,32,16512]{2,0,1:T(2,128)(2,1)}), bf16[2,32,16512]{2,0,1:T(2,128)(2,1)S(1)}, u32[]{:S(2)}, u32[]{:S(2)}) async-start(bf16[2,32,16512]{2,0,1:T(2,128)(2,1)} %copy.18), calls=%async_computation | async-start | bytes 4227072 | tf_op jit(solution)/shard_map/all_to_all | solution.py:179
  24.3 20.2 %copy-start = (f32[8,48]{1,0:T(8,128)S(1)}, f32[8,48]{1,0:T(8,128)}, u32[]{:S(2)}) copy-start(f32[8,48]{1,0:T(8,128)} %gain_ref.1) | copy-start | bytes 4612
  60.7 20.5 %collective-permute-start.6 = (f32[136,128]{1,0:T(8,128)S(1)}, f32[136,128]{1,0:T(8,128)S(1)}, u32[]{:S(2)}, u32[]{:S(2)}) collective-permute-start(f32[136,128]{1,0:T(8,128)S(1)} %get-tuple-element.19), channel_id=1, source_target_pairs={{0,224},{32,0},{64,32},{96,64},{128,96},{160,128},{192,160},{224,1... | collective-permute-start | bytes 208904 | tf_op jit(solution)/shard_map/ppermute | solution.py:199
  66.3 16.1 %collective-permute-start.5 = (f32[136,128]{1,0:T(8,128)S(1)}, f32[136,128]{1,0:T(8,128)S(1)}, u32[]{:S(2)}, u32[]{:S(2)}) collective-permute-start(f32[136,128]{1,0:T(8,128)S(1)} %get-tuple-element.20), channel_id=1, source_target_pairs={{0,192},{32,224},{64,0},{96,32},{128,64},{160,96},{192,128},{224,1... | collective-permute-start | bytes 208904 | tf_op jit(solution)/shard_map/ppermute | solution.py:199
  68.4 11.9 %all-to-all-start.1 = ((f32[2,32,1]{0,2,1:T(1,128)}), f32[2,32,1]{0,2,1:T(1,128)S(1)}, u32[]{:S(2)}, u32[]{:S(2)}) async-start(f32[2,32,1]{0,2,1:T(1,128)} %copy.21), calls=%async_computation.1 | async-start | bytes 32768 | tf_op jit(solution)/shard_map/all_to_all | solution.py:188
  73.3 10.0 %collective-permute-start.4 = (f32[136,128]{1,0:T(8,128)S(1)}, f32[136,128]{1,0:T(8,128)S(1)}, u32[]{:S(2)}, u32[]{:S(2)}) collective-permute-start(f32[136,128]{1,0:T(8,128)S(1)} %get-tuple-element.21), channel_id=1, source_target_pairs={{0,160},{32,192},{64,224},{96,0},{128,32},{160,64},{192,96},{224,1... | collective-permute-start | bytes 208904 | tf_op jit(solution)/shard_map/ppermute | solution.py:199
  73.5 9.8 %collective-permute-start.3 = (f32[136,128]{1,0:T(8,128)S(1)}, f32[136,128]{1,0:T(8,128)S(1)}, u32[]{:S(2)}, u32[]{:S(2)}) collective-permute-start(f32[136,128]{1,0:T(8,128)S(1)} %get-tuple-element.22), channel_id=1, source_target_pairs={{0,128},{32,160},{64,192},{96,224},{128,0},{160,32},{192,64},{224,... | collective-permute-start | bytes 208904 | tf_op jit(solution)/shard_map/ppermute | solution.py:199
  78.3 7.0 %collective-permute-start.2 = (f32[136,128]{1,0:T(8,128)S(1)}, f32[136,128]{1,0:T(8,128)S(1)}, u32[]{:S(2)}, u32[]{:S(2)}) collective-permute-start(f32[136,128]{1,0:T(8,128)S(1)} %get-tuple-element.23), channel_id=1, source_target_pairs={{0,96},{32,128},{64,160},{96,192},{128,224},{160,0},{192,32},{224,... | collective-permute-start | bytes 208904 | tf_op jit(solution)/shard_map/ppermute | solution.py:199
  81.1 9.1 %collective-permute-start.1 = (f32[136,128]{1,0:T(8,128)S(1)}, f32[136,128]{1,0:T(8,128)S(1)}, u32[]{:S(2)}, u32[]{:S(2)}) collective-permute-start(f32[136,128]{1,0:T(8,128)S(1)} %get-tuple-element.24), channel_id=1, source_target_pairs={{0,64},{32,96},{64,128},{96,160},{128,192},{160,224},{192,0},{224,... | collective-permute-start | bytes 208904 | tf_op jit(solution)/shard_map/ppermute | solution.py:199
  82.4 9.6 %collective-permute-start = (f32[136,128]{1,0:T(8,128)S(1)}, f32[136,128]{1,0:T(8,128)S(1)}, u32[]{:S(2)}, u32[]{:S(2)}) collective-permute-start(f32[136,128]{1,0:T(8,128)S(1)} %get-tuple-element.18), channel_id=1, source_target_pairs={{0,32},{32,64},{64,96},{96,128},{128,160},{160,192},{192,224},{224... | collective-permute-start | bytes 208904 | tf_op jit(solution)/shard_map/ppermute | solution.py:199

commit v7 on v4

--- a/solution.py
+++ b/solution.py
@@ -38,6 +38,38 @@
     return jnp.where(is_even, even_part, odd_part).astype(jnp.float32)
 
 
+def ref_kernel(pix, ref_ref, out_ref):
+    chunks = pix // IMG
+
+    def build(u, carry):
+        off = pl.multiple_of(u * IMG, IMG)
+        dst = pl.multiple_of(off + IMG, IMG)
+        chunk = ref_ref[:, pl.ds(off, IMG)]
+        wide = chunk.astype(jnp.float32)
+        out_ref[0, :, pl.ds(dst, IMG)] = pltpu.roll(wide, 1, 1).astype(jnp.bfloat16)
+        out_ref[1, :, pl.ds(dst, IMG)] = chunk
+        out_ref[2, :, pl.ds(dst, IMG)] = pltpu.roll(wide, IMG - 1, 1).astype(jnp.bfloat16)
+        return carry
+
+    lax.fori_loop(0, chunks, build, 0, unroll=8)
+    out_ref[:, :, 0:IMG] = out_ref[:, :, pix:pix + IMG]
+    out_ref[:, :, pix + IMG:pix + 2 * IMG] = out_ref[:, :, IMG:2 * IMG]
+
+
+def shifted_refs(templates):
+    refcount, pix = templates.shape
+    vmem = pl.BlockSpec(memory_space=pltpu.VMEM)
+    return pl.pallas_call(
+        functools.partial(ref_kernel, pix),
+        out_shape=jax.ShapeDtypeStruct((3, refcount, pix + 2 * IMG), jnp.bfloat16),
+        in_specs=[vmem],
+        out_specs=vmem,
+        cost_estimate=pl.CostEstimate(
+            flops=0, transcendentals=0, bytes_accessed=templates.size * 8
+        ),
+    )(templates)
+
+
 def class_kernel(pix, groups, rows_ref, ref_ref, scale_ref, energy_ref, gain_ref, planes_ref, evid_ref,
                  ext_ref, acc_ref, v_ref):
     chunks = pix // IMG
@@ -60,13 +92,13 @@
 
     def products(j, carry):
         k0 = pl.multiple_of(j * TK, TK)
-        tile = ref_ref[:, pl.ds(k0, TK)]
+        tile = rows_ref[:, pl.ds(k0, TK)]
         for ai, a in enumerate(SHIFTS):
-            start = pl.multiple_of(k0 + IMG * (1 - a), IMG)
+            start = pl.multiple_of(k0 + IMG * (1 + a), IMG)
             for bi in range(3):
-                moved = ext_ref[bi, :, pl.ds(start, TK)]
+                moved = ref_ref[bi, :, pl.ds(start, TK)]
                 acc_ref[ai * 3 + bi] += lax.dot_general(
-                    tile, moved, (((1,), (1,)), ((), ())), preferred_element_type=jnp.float32
+                    moved, tile, (((1,), (1,)), ((), ())), preferred_element_type=jnp.float32
                 )
         return carry
 
@@ -124,7 +156,7 @@
 
 def class_pass(rows_ext, templates, scale_row, energy_col, gain, pix, groups):
     rowcount = rows_ext.shape[0]
-    refcount = templates.shape[0]
+    refcount = templates.shape[1]
     depth = gain.shape[0]
     vmem = pl.BlockSpec(memory_space=pltpu.VMEM)
     flops = 2 * 9 * (refcount + 2 * depth) * rowcount * pix
@@ -183,7 +215,7 @@
     templates = references[0]
     energy_col = jnp.sum(jnp.square(templates.astype(jnp.float32)), axis=1).reshape(-1, 1)
     windows, class_evidence = class_pass(
-        rows_ext, templates, scale_row, energy_col, insert_weights, pix, groups
+        rows_ext, shifted_refs(templates), scale_row, energy_col, insert_weights, pix, groups
     )
     stacked = class_evidence.reshape(slot_depth, sources)
     returned = lax.all_to_all(stacked, "dev", split_axis=1, concat_axis=1, tiled=True).reshape(

time: 93.5 us -> 94.1 us (level)
  Pallas kernels: 12.5 us -> 20.3 us
  waiting for transfers between devices: 38.6 us -> 31.7 us
  local copies, waits for them, and re-layouts: 8.66 us -> 7.12 us
  other arithmetic: 2.68 us -> 4.08 us
    all_to_all x1, waiting for transfers between devices: 27.9 us -> 20.9 us  [on_device(): lax.all_to_all(outgoing, 'dev', split_axis=1, concat_axis=1, tiled=True)]
    pallas_call x0 -> x1, Pallas kernels: none -> 5.55 us  [shifted_refs(): pl.pallas_call(functools.partial(ref_kernel, pix), out_shape=jax.ShapeDty...]
    pallas_call x1, Pallas kernels: 12.5 us -> 14.8 us  [class_pass(): pl.pallas_call(functools.partial(class_kernel, pix, groups), out_shape=(j...]
    all_to_all x1, local copies, waits for them, and re-layouts: 1.8 us -> 0.21 us  [on_device(): lax.all_to_all(outgoing, 'dev', split_axis=1, concat_axis=1, tiled=True)]
    reduce_sum x1, other arithmetic: 0.41 us -> 1.81 us  [on_device(): jnp.sum(jnp.square(templates.astype(jnp.float32)), axis=1).reshape(-1, 1)]
  transfers between devices with their start and end apart: 9 -> 9, of which waited for: 5 -> 5; matrix products, arithmetic and copies ran while one was open for 4% -> 6% of each run, Pallas kernels for 0% -> 6%
where the time goes in v7:
time: 94.1 us; the launch traced here: 93.7 us
  waiting for transfers between devices  31.7 us (34%)
  starting transfers between devices  27 us (29%)
  Pallas kernels  20.3 us (22%)
  local copies, waits for them, and re-layouts  7.12 us (8%)
  other arithmetic  4.08 us (4%)
  matrix products  2.79 us (3%)
    all_to_all x1, waiting for transfers between devices, on_device(): lax.all_to_all(outgoing, 'dev', split_axis=1, concat_axis=1, tiled=True)  20.9 us
    pallas_call x1, Pallas kernels, class_pass(): pl.pallas_call(functools.partial(class_kernel, pix, groups), out_shape=(j...  14.8 us
    ppermute x7, starting transfers between devices, on_device(): mine = mine + lax.ppermute(part, 'grp', pairs)  13.5 us
    ppermute x7, waiting for transfers between devices, on_device(): mine = mine + lax.ppermute(part, 'grp', pairs)  8.76 us
    all_to_all x1, starting transfers between devices, on_device(): lax.all_to_all(outgoing, 'dev', split_axis=1, concat_axis=1, tiled=True)  8.59 us
    pallas_call x1, Pallas kernels, shifted_refs(): pl.pallas_call(functools.partial(ref_kernel, pix), out_shape=jax.ShapeDty...  5.55 us
    all_to_all x1, starting transfers between devices, on_device(): lax.all_to_all(stacked, 'dev', split_axis=1, concat_axis=1, tiled=True)  4.91 us
    reshape x1, local copies, waits for them, and re-layouts, on_device(): outgoing = outgoing.reshape(slot_depth, sources, owned_classes * width)  3.01 us
  transfers between devices with their start and end apart: 9, of which 5 were waited for; matrix products, arithmetic and copies ran while one was open for 6% of the time, Pallas kernels for 6%

profile of v7, /device:TPU:1, one launch (start us, length us, event | category | flops | bytes accessed | tf_op | source)
XLA Modules:
  0.0 93.7 jit_solution(10082471831300109806)
XLA Ops:
  0.6 0.9 convert_reduce_fusion.1
  1.6 0.7 broadcast_in_dim.84
  2.3 1.9 %convolution_convert_fusion = bf16[64,16512]{1,0:T(8,128)(2,1)S(1)} fusion(bf16[32,128]{1,0:T(8,128)(2,1)S(1)} %broadcast_in_dim.84, bf16[32,16384]{1,0:T(8,128)(2,1)} %param.6, s32[32]{0:T(128)S(1)} %get-tuple-element.17), kind=kOutput, calls=%fused_computation.1 | convolution fusion | flops 70805504 | bytes 3170432 | tf_op jit(solution)/shard_map/dot_general | solution.py:210
  4.2 3.0 %copy.18 = bf16[2,32,16512]{2,0,1:T(2,128)(2,1)} copy(bf16[2,32,16512]{2,1,0:T(8,128)(2,1)S(1)} %bitcast.52) | data formatting | bytes 4227072 | tf_op jit(solution)/shard_map/reshape | solution.py:211
  7.2 8.6 %all-to-all-start = ((bf16[2,32,16512]{2,0,1:T(2,128)(2,1)}), bf16[2,32,16512]{2,0,1:T(2,128)(2,1)S(1)}, u32[]{:S(2)}, u32[]{:S(2)}) async-start(bf16[2,32,16512]{2,0,1:T(2,128)(2,1)} %copy.18), calls=%async_computation | async-start | bytes 4227072 | tf_op jit(solution)/shard_map/all_to_all | solution.py:212
  15.8 5.5 %shard_map.77.ref_ref = bf16[3,48,16640]{2,1,0:T(8,128)(2,1)} custom-call(bf16[48,16384]{1,0:T(8,128)(2,1)} %bitcast.53), custom_call_target="tpu_custom_call" | custom-call | bytes 6291456 | tf_op jit(solution)/shard_map/pallas_call | solution.py:62
  21.4 1.8 %multiply_reduce_fusion = f32[48]{0:T(128)S(1)} fusion(bf16[1,48,16384]{2,1,0:T(8,128)(2,1)} %param.10), kind=kLoop, calls=%fused_computation.2 | loop fusion | flops 2359248 | bytes 1573056 | tf_op jit(solution)/shard_map/reduce_sum | solution.py:216
  23.2 0.1 copy.20.energy_ref
  23.3 0.0 copy-start
  23.4 20.9 %all-to-all-done = bf16[2,32,16512]{2,0,1:T(2,128)(2,1)S(1)} async-done(((bf16[2,32,16512]{2,0,1:T(2,128)(2,1)}), bf16[2,32,16512]{2,0,1:T(2,128)(2,1)S(1)}, u32[]{:S(2)}, u32[]{:S(2)}) %all-to-all-start) | async-done | bytes 2113568 | tf_op jit(solution)/shard_map/all_to_all | solution.py:212
  44.3 0.2 copy.19
  44.5 0.1 convert_reduce_fusion
  44.6 0.0 copy-done
  44.6 14.8 %shard_map.78 = (f32[8,136,128]{2,1,0:T(8,128)S(1)}, f32[1,64]{1,0:T(1,128)S(1)}) custom-call(bf16[64,16512]{1,0:T(8,128)(2,1)S(1)} %bitcast.50, bf16[3,48,16640]{2,1,0:T(8,128)(2,1)} %shard_map.77.ref_ref, f32[1,64]{1,0:T(1,128)S(1)} %bitcast.51, f32[48,1]{1,0:T(8,128)S(1)} %copy.20.energy_ref, f32[8,48]{1,0:T(8,128)S(1)} %copy-done), custom_call_target="tpu_custom_call" | custom-call | flops 1207959552 | bytes 7430144 | tf_op jit(solution)/shard_map/pallas_call | solution.py:167
  59.4 0.1 dynamic-slice_bitcast_fusion.6
  59.4 5.7 %collective-permute-start.6 = (f32[136,128]{1,0:T(8,128)S(1)}, f32[136,128]{1,0:T(8,128)S(1)}, u32[]{:S(2)}, u32[]{:S(2)}) collective-permute-start(f32[136,128]{1,0:T(8,128)S(1)} %get-tuple-element.19), channel_id=1, source_target_pairs={{0,224},{32,0},{64,32},{96,64},{128,96},{160,128},{192,160},{224,1... | collective-permute-start | bytes 208904 | tf_op jit(solution)/shard_map/ppermute | solution.py:232
  65.1 1.2 %collective-permute-start.5 = (f32[136,128]{1,0:T(8,128)S(1)}, f32[136,128]{1,0:T(8,128)S(1)}, u32[]{:S(2)}, u32[]{:S(2)}) collective-permute-start(f32[136,128]{1,0:T(8,128)S(1)} %get-tuple-element.20), channel_id=1, source_target_pairs={{0,192},{32,224},{64,0},{96,32},{128,64},{160,96},{192,128},{224,1... | collective-permute-start | bytes 208904 | tf_op jit(solution)/shard_map/ppermute | solution.py:232
  66.3 0.5 broadcast.274
  66.8 0.7 reduce.5
  67.4 0.1 all_to_all.10
  67.5 0.7 copy.21
  68.2 4.9 %all-to-all-start.1 = ((f32[2,32,1]{0,2,1:T(1,128)}), f32[2,32,1]{0,2,1:T(1,128)S(1)}, u32[]{:S(2)}, u32[]{:S(2)}) async-start(f32[2,32,1]{0,2,1:T(1,128)} %copy.21), calls=%async_computation.1 | async-start | bytes 32768 | tf_op jit(solution)/shard_map/all_to_all | solution.py:221
  73.1 0.2 collective-permute-start.4
  73.4 4.8 %collective-permute-start.3 = (f32[136,128]{1,0:T(8,128)S(1)}, f32[136,128]{1,0:T(8,128)S(1)}, u32[]{:S(2)}, u32[]{:S(2)}) collective-permute-start(f32[136,128]{1,0:T(8,128)S(1)} %get-tuple-element.22), channel_id=1, source_target_pairs={{0,128},{32,160},{64,192},{96,224},{128,0},{160,32},{192,64},{224,... | collective-permute-start | bytes 208904 | tf_op jit(solution)/shard_map/ppermute | solution.py:232
  78.1 0.0 collective-permute-start.2
  78.1 2.0 %all-to-all-done.1 = f32[2,32,1]{0,2,1:T(1,128)S(1)} async-done(((f32[2,32,1]{0,2,1:T(1,128)}), f32[2,32,1]{0,2,1:T(1,128)S(1)}, u32[]{:S(2)}, u32[]{:S(2)}) %all-to-all-start.1) | async-done | bytes 288 | tf_op jit(solution)/shard_map/all_to_all | solution.py:221
  80.1 0.1 copy.22
  80.2 0.1 reshape.213
  80.3 0.7 gather_fusion
  81.0 0.0 collective-permute-done.6
  81.0 1.3 %collective-permute-start.1 = (f32[136,128]{1,0:T(8,128)S(1)}, f32[136,128]{1,0:T(8,128)S(1)}, u32[]{:S(2)}, u32[]{:S(2)}) collective-permute-start(f32[136,128]{1,0:T(8,128)S(1)} %get-tuple-element.24), channel_id=1, source_target_pairs={{0,64},{32,96},{64,128},{96,160},{128,192},{160,224},{192,0},{224,... | collective-permute-start | bytes 208904 | tf_op jit(solution)/shard_map/ppermute | solution.py:232
  82.2 0.0 collective-permute-done.5
  82.2 0.4 collective-permute-start
  82.6 0.5 and_select_fusion
  83.1 0.0 collective-permute-done.4
  83.1 0.0 collective-permute-done.3
  83.1 2.0 %collective-permute-done.2 = f32[136,128]{1,0:T(8,128)S(1)} collective-permute-done((f32[136,128]{1,0:T(8,128)S(1)}, f32[136,128]{1,0:T(8,128)S(1)}, u32[]{:S(2)}, u32[]{:S(2)}) %collective-permute-start.2) | collective-permute-done | bytes 69664 | tf_op jit(solution)/shard_map/ppermute | solution.py:232
  85.1 5.0 %collective-permute-done.1 = f32[136,128]{1,0:T(8,128)S(1)} collective-permute-done((f32[136,128]{1,0:T(8,128)S(1)}, f32[136,128]{1,0:T(8,128)S(1)}, u32[]{:S(2)}, u32[]{:S(2)}) %collective-permute-start.1) | collective-permute-done | bytes 69664 | tf_op jit(solution)/shard_map/ppermute | solution.py:232
  90.1 1.8 %collective-permute-done = f32[136,128]{1,0:T(8,128)S(1)} collective-permute-done((f32[136,128]{1,0:T(8,128)S(1)}, f32[136,128]{1,0:T(8,128)S(1)}, u32[]{:S(2)}, u32[]{:S(2)}) %collective-permute-start) | collective-permute-done | bytes 69664 | tf_op jit(solution)/shard_map/ppermute | solution.py:232
  92.0 0.5 fusion.7
  92.4 0.4 fusion.30
  92.9 0.9 copy.23
  (8 shorter events, 0.1 us)
Async XLA Ops:
  7.2 37.1 %all-to-all-start = ((bf16[2,32,16512]{2,0,1:T(2,128)(2,1)}), bf16[2,32,16512]{2,0,1:T(2,128)(2,1)S(1)}, u32[]{:S(2)}, u32[]{:S(2)}) async-start(bf16[2,32,16512]{2,0,1:T(2,128)(2,1)} %copy.18), calls=%async_computation | async-start | bytes 4227072 | tf_op jit(solution)/shard_map/all_to_all | solution.py:212
  23.3 21.3 %copy-start = (f32[8,48]{1,0:T(8,128)S(1)}, f32[8,48]{1,0:T(8,128)}, u32[]{:S(2)}) copy-start(f32[8,48]{1,0:T(8,128)} %gain_ref.1) | copy-start | bytes 4612
  59.4 21.5 %collective-permute-start.6 = (f32[136,128]{1,0:T(8,128)S(1)}, f32[136,128]{1,0:T(8,128)S(1)}, u32[]{:S(2)}, u32[]{:S(2)}) collective-permute-start(f32[136,128]{1,0:T(8,128)S(1)} %get-tuple-element.19), channel_id=1, source_target_pairs={{0,224},{32,0},{64,32},{96,64},{128,96},{160,128},{192,160},{224,1... | collective-permute-start | bytes 208904 | tf_op jit(solution)/shard_map/ppermute | solution.py:232
  65.1 17.2 %collective-permute-start.5 = (f32[136,128]{1,0:T(8,128)S(1)}, f32[136,128]{1,0:T(8,128)S(1)}, u32[]{:S(2)}, u32[]{:S(2)}) collective-permute-start(f32[136,128]{1,0:T(8,128)S(1)} %get-tuple-element.20), channel_id=1, source_target_pairs={{0,192},{32,224},{64,0},{96,32},{128,64},{160,96},{192,128},{224,1... | collective-permute-start | bytes 208904 | tf_op jit(solution)/shard_map/ppermute | solution.py:232
  68.2 11.9 %all-to-all-start.1 = ((f32[2,32,1]{0,2,1:T(1,128)}), f32[2,32,1]{0,2,1:T(1,128)S(1)}, u32[]{:S(2)}, u32[]{:S(2)}) async-start(f32[2,32,1]{0,2,1:T(1,128)} %copy.21), calls=%async_computation.1 | async-start | bytes 32768 | tf_op jit(solution)/shard_map/all_to_all | solution.py:221
  73.1 10.0 %collective-permute-start.4 = (f32[136,128]{1,0:T(8,128)S(1)}, f32[136,128]{1,0:T(8,128)S(1)}, u32[]{:S(2)}, u32[]{:S(2)}) collective-permute-start(f32[136,128]{1,0:T(8,128)S(1)} %get-tuple-element.21), channel_id=1, source_target_pairs={{0,160},{32,192},{64,224},{96,0},{128,32},{160,64},{192,96},{224,1... | collective-permute-start | bytes 208904 | tf_op jit(solution)/shard_map/ppermute | solution.py:232
  73.4 9.8 %collective-permute-start.3 = (f32[136,128]{1,0:T(8,128)S(1)}, f32[136,128]{1,0:T(8,128)S(1)}, u32[]{:S(2)}, u32[]{:S(2)}) collective-permute-start(f32[136,128]{1,0:T(8,128)S(1)} %get-tuple-element.22), channel_id=1, source_target_pairs={{0,128},{32,160},{64,192},{96,224},{128,0},{160,32},{192,64},{224,... | collective-permute-start | bytes 208904 | tf_op jit(solution)/shard_map/ppermute | solution.py:232
  78.1 7.0 %collective-permute-start.2 = (f32[136,128]{1,0:T(8,128)S(1)}, f32[136,128]{1,0:T(8,128)S(1)}, u32[]{:S(2)}, u32[]{:S(2)}) collective-permute-start(f32[136,128]{1,0:T(8,128)S(1)} %get-tuple-element.23), channel_id=1, source_target_pairs={{0,96},{32,128},{64,160},{96,192},{128,224},{160,0},{192,32},{224,... | collective-permute-start | bytes 208904 | tf_op jit(solution)/shard_map/ppermute | solution.py:232
  81.0 9.1 %collective-permute-start.1 = (f32[136,128]{1,0:T(8,128)S(1)}, f32[136,128]{1,0:T(8,128)S(1)}, u32[]{:S(2)}, u32[]{:S(2)}) collective-permute-start(f32[136,128]{1,0:T(8,128)S(1)} %get-tuple-element.24), channel_id=1, source_target_pairs={{0,64},{32,96},{64,128},{96,160},{128,192},{160,224},{192,0},{224,... | collective-permute-start | bytes 208904 | tf_op jit(solution)/shard_map/ppermute | solution.py:232
  82.2 9.7 %collective-permute-start = (f32[136,128]{1,0:T(8,128)S(1)}, f32[136,128]{1,0:T(8,128)S(1)}, u32[]{:S(2)}, u32[]{:S(2)}) collective-permute-start(f32[136,128]{1,0:T(8,128)S(1)} %get-tuple-element.18), channel_id=1, source_target_pairs={{0,32},{32,64},{64,96},{96,128},{128,160},{160,192},{192,224},{224... | collective-permute-start | bytes 208904 | tf_op jit(solution)/shard_map/ppermute | solution.py:232

commit v8 on v4

--- a/solution.py
+++ b/solution.py
@@ -198,11 +198,14 @@
         part = lax.dynamic_index_in_dim(windows, lax.rem(here + step, groups), 0, keepdims=False)
         pairs = [(g, (g + step) % groups) for g in range(groups)]
         mine = mine + lax.ppermute(part, "grp", pairs)
-    mine = mine.reshape(depth, band + 1, IMG)
     interp = upsample_table(VOL, IMG)
-    across = jnp.einsum("zjv,xv->zjx", mine, interp, precision=lax.Precision.HIGHEST)
+    across = jnp.dot(mine, interp.T, precision=lax.Precision.HIGHEST)
     rows_table = local_table(2 * band, band + 1)
-    volume = jnp.einsum("yj,zjx->yzx", rows_table, across, precision=lax.Precision.HIGHEST)
+    eye = jnp.eye(depth, dtype=jnp.float32)
+    block = (rows_table[:, None, None, :] * eye[None, :, :, None]).reshape(
+        2 * band * depth, depth * (band + 1)
+    )
+    volume = jnp.dot(block, across, precision=lax.Precision.HIGHEST).reshape(2 * band, depth, VOL)
     return (volume, particle_evidence)
 
 

time: 93.5 us -> 93.2 us (level)
  no operation moved by 1% of the time
where the time goes in v8:
time: 93.2 us; the launch traced here: 92.9 us
  waiting for transfers between devices  38.2 us (41%)
  starting transfers between devices  27.2 us (29%)
  Pallas kernels  12.5 us (13%)
  local copies, waits for them, and re-layouts  8.04 us (9%)
  matrix products  3.4 us (4%)
  other arithmetic  2.73 us (3%)
    all_to_all x1, waiting for transfers between devices, on_device(): lax.all_to_all(outgoing, 'dev', split_axis=1, concat_axis=1, tiled=True)  27.5 us
    ppermute x7, starting transfers between devices, on_device(): mine = mine + lax.ppermute(part, 'grp', pairs)  13.5 us
    pallas_call x1, Pallas kernels, class_pass(): pl.pallas_call(functools.partial(class_kernel, pix, groups), out_shape=(j...  12.5 us
    all_to_all x1, starting transfers between devices, on_device(): lax.all_to_all(outgoing, 'dev', split_axis=1, concat_axis=1, tiled=True)  8.77 us
    ppermute x7, waiting for transfers between devices, on_device(): mine = mine + lax.ppermute(part, 'grp', pairs)  8.76 us
    all_to_all x1, starting transfers between devices, on_device(): lax.all_to_all(stacked, 'dev', split_axis=1, concat_axis=1, tiled=True)  4.91 us
    reshape x1, local copies, waits for them, and re-layouts, on_device(): outgoing = outgoing.reshape(slot_depth, sources, owned_classes * width)  2.95 us
    all_to_all x1, waiting for transfers between devices, on_device(): lax.all_to_all(stacked, 'dev', split_axis=1, concat_axis=1, tiled=True)  1.96 us
  transfers between devices with their start and end apart: 9, of which 5 were waited for; matrix products, arithmetic and copies ran while one was open for 4% of the time, Pallas kernels for 0%

profile of v8, /device:TPU:1, one launch (start us, length us, event | category | flops | bytes accessed | tf_op | source)
XLA Modules:
  0.0 92.9 jit_solution(1901606293781824006)
XLA Ops:
  0.6 0.9 convert_reduce_fusion.1
  1.6 0.7 broadcast_in_dim.86
  2.3 1.9 %convolution_convert_fusion = bf16[64,16512]{1,0:T(8,128)(2,1)S(1)} fusion(bf16[32,128]{1,0:T(8,128)(2,1)S(1)} %broadcast_in_dim.86, bf16[32,16384]{1,0:T(8,128)(2,1)} %param.6, s32[32]{0:T(128)S(1)} %get-tuple-element.9), kind=kOutput, calls=%fused_computation.1 | convolution fusion | flops 70805504 | bytes 3170432 | tf_op jit(solution)/shard_map/dot_general | solution.py:178
  4.2 2.9 %copy.15 = bf16[2,32,16512]{2,0,1:T(2,128)(2,1)} copy(bf16[2,32,16512]{2,1,0:T(8,128)(2,1)S(1)} %bitcast.49) | data formatting | bytes 4227072 | tf_op jit(solution)/shard_map/reshape | solution.py:179
  7.1 0.0 copy-start
  7.1 8.8 %all-to-all-start = ((bf16[2,32,16512]{2,0,1:T(2,128)(2,1)}), bf16[2,32,16512]{2,0,1:T(2,128)(2,1)}, u32[]{:S(2)}, u32[]{:S(2)}) async-start(bf16[2,32,16512]{2,0,1:T(2,128)(2,1)} %copy.15), calls=%async_computation | async-start | bytes 4227072 | tf_op jit(solution)/shard_map/all_to_all | solution.py:180
  16.0 0.0 copy-done
  16.0 0.4 multiply_reduce_fusion
  16.4 0.1 copy.17.energy_ref
  16.5 0.1 mul.46
  16.6 0.1 mul.47
  16.7 0.1 add_select_fusion
  16.8 0.1 mul.44
  16.9 0.0 copy-start.1
  16.9 27.5 %all-to-all-done = bf16[2,32,16512]{2,0,1:T(2,128)(2,1)} async-done(((bf16[2,32,16512]{2,0,1:T(2,128)(2,1)}), bf16[2,32,16512]{2,0,1:T(2,128)(2,1)}, u32[]{:S(2)}, u32[]{:S(2)}) %all-to-all-start) | async-done | bytes 2113568 | tf_op jit(solution)/shard_map/all_to_all | solution.py:180
  44.5 1.8 %copy.16 = bf16[2,32,16512]{2,1,0:T(8,128)(2,1)S(1)} copy(bf16[2,32,16512]{2,0,1:T(2,128)(2,1)} %all-to-all-done) | data formatting | bytes 4227072 | tf_op jit(solution)/shard_map/all_to_all | solution.py:180
  46.3 0.1 convert_reduce_fusion
  46.4 0.0 copy-done.1
  46.4 12.5 %shard_map.77 = (f32[8,136,128]{2,1,0:T(8,128)S(1)}, f32[1,64]{1,0:T(1,128)S(1)}) custom-call(bf16[64,16512]{1,0:T(8,128)(2,1)S(1)} %bitcast.46, bf16[48,16384]{1,0:T(8,128)(2,1)S(1)} %bitcast.47, f32[1,64]{1,0:T(1,128)S(1)} %bitcast.48, f32[48,1]{1,0:T(8,128)S(1)} %copy.17.energy_ref, f32[8,48]{1,0:T(8,128)S(1)} %copy-done.1), custom_call_target="tpu_custom_call" | custom-call | flops 1207959552 | bytes 4210688 | tf_op jit(solution)/shard_map/pallas_call | solution.py:135
  58.9 0.1 dynamic-slice_bitcast_fusion.6
  58.9 5.7 %collective-permute-start.6 = (f32[136,128]{1,0:T(8,128)S(1)}, f32[136,128]{1,0:T(8,128)S(1)}, u32[]{:S(2)}, u32[]{:S(2)}) collective-permute-start(f32[136,128]{1,0:T(8,128)S(1)} %get-tuple-element.11), channel_id=1, source_target_pairs={{0,224},{32,0},{64,32},{96,64},{128,96},{160,128},{192,160},{224,1... | collective-permute-start | bytes 208904 | tf_op jit(solution)/shard_map/ppermute | solution.py:200
  64.6 1.2 %collective-permute-start.5 = (f32[136,128]{1,0:T(8,128)S(1)}, f32[136,128]{1,0:T(8,128)S(1)}, u32[]{:S(2)}, u32[]{:S(2)}) collective-permute-start(f32[136,128]{1,0:T(8,128)S(1)} %get-tuple-element.12), channel_id=1, source_target_pairs={{0,192},{32,224},{64,0},{96,32},{128,64},{160,96},{192,128},{224,1... | collective-permute-start | bytes 208904 | tf_op jit(solution)/shard_map/ppermute | solution.py:200
  65.7 0.5 broadcast.332
  66.3 0.7 reduce.5
  66.9 0.1 all_to_all.10
  67.0 0.7 copy.18
  67.7 4.9 %all-to-all-start.1 = ((f32[2,32,1]{0,2,1:T(1,128)}), f32[2,32,1]{0,2,1:T(1,128)S(1)}, u32[]{:S(2)}, u32[]{:S(2)}) async-start(f32[2,32,1]{0,2,1:T(1,128)} %copy.18), calls=%async_computation.1 | async-start | bytes 32768 | tf_op jit(solution)/shard_map/all_to_all | solution.py:189
  72.6 0.2 collective-permute-start.4
  72.9 4.8 %collective-permute-start.3 = (f32[136,128]{1,0:T(8,128)S(1)}, f32[136,128]{1,0:T(8,128)S(1)}, u32[]{:S(2)}, u32[]{:S(2)}) collective-permute-start(f32[136,128]{1,0:T(8,128)S(1)} %get-tuple-element.14), channel_id=1, source_target_pairs={{0,128},{32,160},{64,192},{96,224},{128,0},{160,32},{192,64},{224,... | collective-permute-start | bytes 208904 | tf_op jit(solution)/shard_map/ppermute | solution.py:200
  77.6 0.0 collective-permute-start.2
  77.6 2.0 %all-to-all-done.1 = f32[2,32,1]{0,2,1:T(1,128)S(1)} async-done(((f32[2,32,1]{0,2,1:T(1,128)}), f32[2,32,1]{0,2,1:T(1,128)S(1)}, u32[]{:S(2)}, u32[]{:S(2)}) %all-to-all-start.1) | async-done | bytes 288 | tf_op jit(solution)/shard_map/all_to_all | solution.py:189
  79.6 0.1 copy.19
  79.7 0.1 reshape.276
  79.8 0.7 gather_fusion
  80.5 0.0 collective-permute-done.6
  80.5 1.3 %collective-permute-start.1 = (f32[136,128]{1,0:T(8,128)S(1)}, f32[136,128]{1,0:T(8,128)S(1)}, u32[]{:S(2)}, u32[]{:S(2)}) collective-permute-start(f32[136,128]{1,0:T(8,128)S(1)} %get-tuple-element.16), channel_id=1, source_target_pairs={{0,64},{32,96},{64,128},{96,160},{128,192},{160,224},{192,0},{224,... | collective-permute-start | bytes 208904 | tf_op jit(solution)/shard_map/ppermute | solution.py:200
  81.7 0.0 collective-permute-done.5
  81.7 0.4 collective-permute-start
  82.1 0.5 and_select_fusion
  82.6 0.0 collective-permute-done.4
  82.6 0.0 collective-permute-done.3
  82.6 2.0 %collective-permute-done.2 = f32[136,128]{1,0:T(8,128)S(1)} collective-permute-done((f32[136,128]{1,0:T(8,128)S(1)}, f32[136,128]{1,0:T(8,128)S(1)}, u32[]{:S(2)}, u32[]{:S(2)}) %collective-permute-start.2) | collective-permute-done | bytes 69664 | tf_op jit(solution)/shard_map/ppermute | solution.py:200
  84.6 5.0 %collective-permute-done.1 = f32[136,128]{1,0:T(8,128)S(1)} collective-permute-done((f32[136,128]{1,0:T(8,128)S(1)}, f32[136,128]{1,0:T(8,128)S(1)}, u32[]{:S(2)}, u32[]{:S(2)}) %collective-permute-start.1) | collective-permute-done | bytes 69664 | tf_op jit(solution)/shard_map/ppermute | solution.py:200
  89.6 1.8 %collective-permute-done = f32[136,128]{1,0:T(8,128)S(1)} collective-permute-done((f32[136,128]{1,0:T(8,128)S(1)}, f32[136,128]{1,0:T(8,128)S(1)}, u32[]{:S(2)}, u32[]{:S(2)}) %collective-permute-start) | collective-permute-done | bytes 69664 | tf_op jit(solution)/shard_map/ppermute | solution.py:200
  91.4 0.4 convolution_bitcast_fusion
  91.8 1.1 %fusion.3 = f32[32,8,256]{2,1,0:T(8,128)} fusion(f32[136,256,1]{1,0,2:T(8,128)S(1)} %convolution_bitcast_fusion, f32[8,136]{1,0:T(8,128)S(1)} %mul.47, f32[32,136]{1,0:T(8,128)S(1)} %mul.44), kind=kOutput, calls=%fused_computation.7 | convolution fusion | flops 106989568 | bytes 423168 | tf_op jit(solution)/shard_map/dot_general | solution.py:208
  (8 shorter events, 0.1 us)
Async XLA Ops:
  7.1 8.8 %copy-start = (bf16[1,48,16384]{2,1,0:T(8,128)(2,1)S(1)}, bf16[1,48,16384]{2,1,0:T(8,128)(2,1)}, u32[]{:S(2)}) copy-start(bf16[1,48,16384]{2,1,0:T(8,128)(2,1)} %param.10) | copy-start | bytes 4718596
  7.1 37.3 %all-to-all-start = ((bf16[2,32,16512]{2,0,1:T(2,128)(2,1)}), bf16[2,32,16512]{2,0,1:T(2,128)(2,1)}, u32[]{:S(2)}, u32[]{:S(2)}) async-start(bf16[2,32,16512]{2,0,1:T(2,128)(2,1)} %copy.15), calls=%async_computation | async-start | bytes 4227072 | tf_op jit(solution)/shard_map/all_to_all | solution.py:180
  16.9 29.4 %copy-start.1 = (f32[8,48]{1,0:T(8,128)S(1)}, f32[8,48]{1,0:T(8,128)}, u32[]{:S(2)}) copy-start(f32[8,48]{1,0:T(8,128)} %gain_ref.1) | copy-start | bytes 4612
  58.9 21.5 %collective-permute-start.6 = (f32[136,128]{1,0:T(8,128)S(1)}, f32[136,128]{1,0:T(8,128)S(1)}, u32[]{:S(2)}, u32[]{:S(2)}) collective-permute-start(f32[136,128]{1,0:T(8,128)S(1)} %get-tuple-element.11), channel_id=1, source_target_pairs={{0,224},{32,0},{64,32},{96,64},{128,96},{160,128},{192,160},{224,1... | collective-permute-start | bytes 208904 | tf_op jit(solution)/shard_map/ppermute | solution.py:200
  64.6 17.2 %collective-permute-start.5 = (f32[136,128]{1,0:T(8,128)S(1)}, f32[136,128]{1,0:T(8,128)S(1)}, u32[]{:S(2)}, u32[]{:S(2)}) collective-permute-start(f32[136,128]{1,0:T(8,128)S(1)} %get-tuple-element.12), channel_id=1, source_target_pairs={{0,192},{32,224},{64,0},{96,32},{128,64},{160,96},{192,128},{224,1... | collective-permute-start | bytes 208904 | tf_op jit(solution)/shard_map/ppermute | solution.py:200
  67.7 11.9 %all-to-all-start.1 = ((f32[2,32,1]{0,2,1:T(1,128)}), f32[2,32,1]{0,2,1:T(1,128)S(1)}, u32[]{:S(2)}, u32[]{:S(2)}) async-start(f32[2,32,1]{0,2,1:T(1,128)} %copy.18), calls=%async_computation.1 | async-start | bytes 32768 | tf_op jit(solution)/shard_map/all_to_all | solution.py:189
  72.6 10.0 %collective-permute-start.4 = (f32[136,128]{1,0:T(8,128)S(1)}, f32[136,128]{1,0:T(8,128)S(1)}, u32[]{:S(2)}, u32[]{:S(2)}) collective-permute-start(f32[136,128]{1,0:T(8,128)S(1)} %get-tuple-element.13), channel_id=1, source_target_pairs={{0,160},{32,192},{64,224},{96,0},{128,32},{160,64},{192,96},{224,1... | collective-permute-start | bytes 208904 | tf_op jit(solution)/shard_map/ppermute | solution.py:200
  72.9 9.8 %collective-permute-start.3 = (f32[136,128]{1,0:T(8,128)S(1)}, f32[136,128]{1,0:T(8,128)S(1)}, u32[]{:S(2)}, u32[]{:S(2)}) collective-permute-start(f32[136,128]{1,0:T(8,128)S(1)} %get-tuple-element.14), channel_id=1, source_target_pairs={{0,128},{32,160},{64,192},{96,224},{128,0},{160,32},{192,64},{224,... | collective-permute-start | bytes 208904 | tf_op jit(solution)/shard_map/ppermute | solution.py:200
  77.6 7.0 %collective-permute-start.2 = (f32[136,128]{1,0:T(8,128)S(1)}, f32[136,128]{1,0:T(8,128)S(1)}, u32[]{:S(2)}, u32[]{:S(2)}) collective-permute-start(f32[136,128]{1,0:T(8,128)S(1)} %get-tuple-element.15), channel_id=1, source_target_pairs={{0,96},{32,128},{64,160},{96,192},{128,224},{160,0},{192,32},{224,... | collective-permute-start | bytes 208904 | tf_op jit(solution)/shard_map/ppermute | solution.py:200
  80.5 9.1 %collective-permute-start.1 = (f32[136,128]{1,0:T(8,128)S(1)}, f32[136,128]{1,0:T(8,128)S(1)}, u32[]{:S(2)}, u32[]{:S(2)}) collective-permute-start(f32[136,128]{1,0:T(8,128)S(1)} %get-tuple-element.16), channel_id=1, source_target_pairs={{0,64},{32,96},{64,128},{96,160},{128,192},{160,224},{192,0},{224,... | collective-permute-start | bytes 208904 | tf_op jit(solution)/shard_map/ppermute | solution.py:200
  81.7 9.6 %collective-permute-start = (f32[136,128]{1,0:T(8,128)S(1)}, f32[136,128]{1,0:T(8,128)S(1)}, u32[]{:S(2)}, u32[]{:S(2)}) collective-permute-start(f32[136,128]{1,0:T(8,128)S(1)} %get-tuple-element.10), channel_id=1, source_target_pairs={{0,32},{32,64},{64,96},{96,128},{128,160},{160,192},{192,224},{224... | collective-permute-start | bytes 208904 | tf_op jit(solution)/shard_map/ppermute | solution.py:200

commit v9 on v8

--- a/solution.py
+++ b/solution.py
@@ -10,7 +10,7 @@
 IMG = 128
 VOL = 256
 SHIFTS = (-1, 0, 1)
-TK = 2048
+TK = 8192
 TN = 1024
 
 
@@ -52,7 +52,7 @@
         ext_ref[2, :, pl.ds(dst, IMG)] = pltpu.roll(wide, 1, 1).astype(jnp.bfloat16)
         return carry
 
-    lax.fori_loop(0, chunks, build, 0, unroll=8)
+    lax.fori_loop(0, chunks, build, 0, unroll=32)
     ext_ref[:, :, 0:IMG] = ext_ref[:, :, pix:pix + IMG]
     ext_ref[:, :, pix + IMG:pix + 2 * IMG] = ext_ref[:, :, IMG:2 * IMG]
 

time: 93.2 us -> 91.5 us (0.982)
  Pallas kernels: 12.5 us -> 10.8 us
    pallas_call x1, Pallas kernels: 12.5 us -> 10.8 us  [class_pass(): pl.pallas_call(functools.partial(class_kernel, pix, groups), out_shape=(j...]
  transfers between devices with their start and end apart: 9 -> 9, of which waited for: 5 -> 5; matrix products, arithmetic and copies ran while one was open for 4% -> 5% of each run, Pallas kernels for 0% -> 0%
where the time goes in v9:
time: 91.5 us; the launch traced here: 91.2 us
  waiting for transfers between devices  38.2 us (42%)
  starting transfers between devices  27.2 us (30%)
  Pallas kernels  10.8 us (12%)
  local copies, waits for them, and re-layouts  8.04 us (9%)
  matrix products  3.4 us (4%)
  other arithmetic  2.73 us (3%)
    all_to_all x1, waiting for transfers between devices, on_device(): lax.all_to_all(outgoing, 'dev', split_axis=1, concat_axis=1, tiled=True)  27.5 us
    ppermute x7, starting transfers between devices, on_device(): mine = mine + lax.ppermute(part, 'grp', pairs)  13.5 us
    pallas_call x1, Pallas kernels, class_pass(): pl.pallas_call(functools.partial(class_kernel, pix, groups), out_shape=(j...  10.8 us
    all_to_all x1, starting transfers between devices, on_device(): lax.all_to_all(outgoing, 'dev', split_axis=1, concat_axis=1, tiled=True)  8.77 us
    ppermute x7, waiting for transfers between devices, on_device(): mine = mine + lax.ppermute(part, 'grp', pairs)  8.77 us
    all_to_all x1, starting transfers between devices, on_device(): lax.all_to_all(stacked, 'dev', split_axis=1, concat_axis=1, tiled=True)  4.91 us
    reshape x1, local copies, waits for them, and re-layouts, on_device(): outgoing = outgoing.reshape(slot_depth, sources, owned_classes * width)  2.95 us
    all_to_all x1, waiting for transfers between devices, on_device(): lax.all_to_all(stacked, 'dev', split_axis=1, concat_axis=1, tiled=True)  1.97 us
  transfers between devices with their start and end apart: 9, of which 5 were waited for; matrix products, arithmetic and copies ran while one was open for 5% of the time, Pallas kernels for 0%

profile of v9, /device:TPU:1, one launch (start us, length us, event | category | flops | bytes accessed | tf_op | source)
XLA Modules:
  0.0 91.2 jit_solution(16123796901294315062)
XLA Ops:
  0.6 0.9 convert_reduce_fusion.1
  1.6 0.7 broadcast_in_dim.86
  2.3 1.9 %convolution_convert_fusion = bf16[64,16512]{1,0:T(8,128)(2,1)S(1)} fusion(bf16[32,128]{1,0:T(8,128)(2,1)S(1)} %broadcast_in_dim.86, bf16[32,16384]{1,0:T(8,128)(2,1)} %param.6, s32[32]{0:T(128)S(1)} %get-tuple-element.9), kind=kOutput, calls=%fused_computation.1 | convolution fusion | flops 70805504 | bytes 3170432 | tf_op jit(solution)/shard_map/dot_general | solution.py:178
  4.2 2.9 %copy.15 = bf16[2,32,16512]{2,0,1:T(2,128)(2,1)} copy(bf16[2,32,16512]{2,1,0:T(8,128)(2,1)S(1)} %bitcast.49) | data formatting | bytes 4227072 | tf_op jit(solution)/shard_map/reshape | solution.py:179
  7.1 0.0 copy-start
  7.1 8.8 %all-to-all-start = ((bf16[2,32,16512]{2,0,1:T(2,128)(2,1)}), bf16[2,32,16512]{2,0,1:T(2,128)(2,1)}, u32[]{:S(2)}, u32[]{:S(2)}) async-start(bf16[2,32,16512]{2,0,1:T(2,128)(2,1)} %copy.15), calls=%async_computation | async-start | bytes 4227072 | tf_op jit(solution)/shard_map/all_to_all | solution.py:180
  16.0 0.0 copy-done
  16.0 0.4 multiply_reduce_fusion
  16.4 0.1 copy.17.energy_ref
  16.5 0.1 mul.46
  16.6 0.1 mul.47
  16.7 0.1 add_select_fusion
  16.8 0.1 mul.44
  16.9 0.0 copy-start.1
  16.9 27.5 %all-to-all-done = bf16[2,32,16512]{2,0,1:T(2,128)(2,1)} async-done(((bf16[2,32,16512]{2,0,1:T(2,128)(2,1)}), bf16[2,32,16512]{2,0,1:T(2,128)(2,1)}, u32[]{:S(2)}, u32[]{:S(2)}) %all-to-all-start) | async-done | bytes 2113568 | tf_op jit(solution)/shard_map/all_to_all | solution.py:180
  44.5 1.8 %copy.16 = bf16[2,32,16512]{2,1,0:T(8,128)(2,1)S(1)} copy(bf16[2,32,16512]{2,0,1:T(2,128)(2,1)} %all-to-all-done) | data formatting | bytes 4227072 | tf_op jit(solution)/shard_map/all_to_all | solution.py:180
  46.3 0.1 convert_reduce_fusion
  46.4 0.0 copy-done.1
  46.4 10.8 %shard_map.77 = (f32[8,136,128]{2,1,0:T(8,128)S(1)}, f32[1,64]{1,0:T(1,128)S(1)}) custom-call(bf16[64,16512]{1,0:T(8,128)(2,1)S(1)} %bitcast.46, bf16[48,16384]{1,0:T(8,128)(2,1)S(1)} %bitcast.47, f32[1,64]{1,0:T(1,128)S(1)} %bitcast.48, f32[48,1]{1,0:T(8,128)S(1)} %copy.17.energy_ref, f32[8,48]{1,0:T(8,128)S(1)} %copy-done.1), custom_call_target="tpu_custom_call" | custom-call | flops 1207959552 | bytes 4210688 | tf_op jit(solution)/shard_map/pallas_call | solution.py:135
  57.2 0.1 dynamic-slice_bitcast_fusion.6
  57.2 5.7 %collective-permute-start.6 = (f32[136,128]{1,0:T(8,128)S(1)}, f32[136,128]{1,0:T(8,128)S(1)}, u32[]{:S(2)}, u32[]{:S(2)}) collective-permute-start(f32[136,128]{1,0:T(8,128)S(1)} %get-tuple-element.11), channel_id=1, source_target_pairs={{0,224},{32,0},{64,32},{96,64},{128,96},{160,128},{192,160},{224,1... | collective-permute-start | bytes 208904 | tf_op jit(solution)/shard_map/ppermute | solution.py:200
  62.9 1.2 %collective-permute-start.5 = (f32[136,128]{1,0:T(8,128)S(1)}, f32[136,128]{1,0:T(8,128)S(1)}, u32[]{:S(2)}, u32[]{:S(2)}) collective-permute-start(f32[136,128]{1,0:T(8,128)S(1)} %get-tuple-element.12), channel_id=1, source_target_pairs={{0,192},{32,224},{64,0},{96,32},{128,64},{160,96},{192,128},{224,1... | collective-permute-start | bytes 208904 | tf_op jit(solution)/shard_map/ppermute | solution.py:200
  64.1 0.5 broadcast.332
  64.6 0.7 reduce.5
  65.2 0.1 all_to_all.10
  65.3 0.7 copy.18
  66.0 4.9 %all-to-all-start.1 = ((f32[2,32,1]{0,2,1:T(1,128)}), f32[2,32,1]{0,2,1:T(1,128)S(1)}, u32[]{:S(2)}, u32[]{:S(2)}) async-start(f32[2,32,1]{0,2,1:T(1,128)} %copy.18), calls=%async_computation.1 | async-start | bytes 32768 | tf_op jit(solution)/shard_map/all_to_all | solution.py:189
  70.9 0.2 collective-permute-start.4
  71.2 4.8 %collective-permute-start.3 = (f32[136,128]{1,0:T(8,128)S(1)}, f32[136,128]{1,0:T(8,128)S(1)}, u32[]{:S(2)}, u32[]{:S(2)}) collective-permute-start(f32[136,128]{1,0:T(8,128)S(1)} %get-tuple-element.14), channel_id=1, source_target_pairs={{0,128},{32,160},{64,192},{96,224},{128,0},{160,32},{192,64},{224,... | collective-permute-start | bytes 208904 | tf_op jit(solution)/shard_map/ppermute | solution.py:200
  75.9 0.0 collective-permute-start.2
  76.0 2.0 %all-to-all-done.1 = f32[2,32,1]{0,2,1:T(1,128)S(1)} async-done(((f32[2,32,1]{0,2,1:T(1,128)}), f32[2,32,1]{0,2,1:T(1,128)S(1)}, u32[]{:S(2)}, u32[]{:S(2)}) %all-to-all-start.1) | async-done | bytes 288 | tf_op jit(solution)/shard_map/all_to_all | solution.py:189
  77.9 0.1 copy.19
  78.0 0.1 reshape.276
  78.1 0.7 gather_fusion
  78.8 0.0 collective-permute-done.6
  78.8 1.3 %collective-permute-start.1 = (f32[136,128]{1,0:T(8,128)S(1)}, f32[136,128]{1,0:T(8,128)S(1)}, u32[]{:S(2)}, u32[]{:S(2)}) collective-permute-start(f32[136,128]{1,0:T(8,128)S(1)} %get-tuple-element.16), channel_id=1, source_target_pairs={{0,64},{32,96},{64,128},{96,160},{128,192},{160,224},{192,0},{224,... | collective-permute-start | bytes 208904 | tf_op jit(solution)/shard_map/ppermute | solution.py:200
  80.1 0.0 collective-permute-done.5
  80.1 0.4 collective-permute-start
  80.4 0.5 and_select_fusion
  81.0 0.0 collective-permute-done.4
  81.0 0.0 collective-permute-done.3
  81.0 2.0 %collective-permute-done.2 = f32[136,128]{1,0:T(8,128)S(1)} collective-permute-done((f32[136,128]{1,0:T(8,128)S(1)}, f32[136,128]{1,0:T(8,128)S(1)}, u32[]{:S(2)}, u32[]{:S(2)}) %collective-permute-start.2) | collective-permute-done | bytes 69664 | tf_op jit(solution)/shard_map/ppermute | solution.py:200
  82.9 5.0 %collective-permute-done.1 = f32[136,128]{1,0:T(8,128)S(1)} collective-permute-done((f32[136,128]{1,0:T(8,128)S(1)}, f32[136,128]{1,0:T(8,128)S(1)}, u32[]{:S(2)}, u32[]{:S(2)}) %collective-permute-start.1) | collective-permute-done | bytes 69664 | tf_op jit(solution)/shard_map/ppermute | solution.py:200
  87.9 1.8 %collective-permute-done = f32[136,128]{1,0:T(8,128)S(1)} collective-permute-done((f32[136,128]{1,0:T(8,128)S(1)}, f32[136,128]{1,0:T(8,128)S(1)}, u32[]{:S(2)}, u32[]{:S(2)}) %collective-permute-start) | collective-permute-done | bytes 69664 | tf_op jit(solution)/shard_map/ppermute | solution.py:200
  89.7 0.4 convolution_bitcast_fusion
  90.1 1.1 %fusion.3 = f32[32,8,256]{2,1,0:T(8,128)} fusion(f32[136,256,1]{1,0,2:T(8,128)S(1)} %convolution_bitcast_fusion, f32[8,136]{1,0:T(8,128)S(1)} %mul.47, f32[32,136]{1,0:T(8,128)S(1)} %mul.44), kind=kOutput, calls=%fused_computation.7 | convolution fusion | flops 106989568 | bytes 423168 | tf_op jit(solution)/shard_map/dot_general | solution.py:208
  (8 shorter events, 0.1 us)
Async XLA Ops:
  7.1 8.8 %copy-start = (bf16[1,48,16384]{2,1,0:T(8,128)(2,1)S(1)}, bf16[1,48,16384]{2,1,0:T(8,128)(2,1)}, u32[]{:S(2)}) copy-start(bf16[1,48,16384]{2,1,0:T(8,128)(2,1)} %param.10) | copy-start | bytes 4718596
  7.1 37.3 %all-to-all-start = ((bf16[2,32,16512]{2,0,1:T(2,128)(2,1)}), bf16[2,32,16512]{2,0,1:T(2,128)(2,1)}, u32[]{:S(2)}, u32[]{:S(2)}) async-start(bf16[2,32,16512]{2,0,1:T(2,128)(2,1)} %copy.15), calls=%async_computation | async-start | bytes 4227072 | tf_op jit(solution)/shard_map/all_to_all | solution.py:180
  16.9 29.4 %copy-start.1 = (f32[8,48]{1,0:T(8,128)S(1)}, f32[8,48]{1,0:T(8,128)}, u32[]{:S(2)}) copy-start(f32[8,48]{1,0:T(8,128)} %gain_ref.1) | copy-start | bytes 4612
  57.2 21.6 %collective-permute-start.6 = (f32[136,128]{1,0:T(8,128)S(1)}, f32[136,128]{1,0:T(8,128)S(1)}, u32[]{:S(2)}, u32[]{:S(2)}) collective-permute-start(f32[136,128]{1,0:T(8,128)S(1)} %get-tuple-element.11), channel_id=1, source_target_pairs={{0,224},{32,0},{64,32},{96,64},{128,96},{160,128},{192,160},{224,1... | collective-permute-start | bytes 208904 | tf_op jit(solution)/shard_map/ppermute | solution.py:200
  62.9 17.2 %collective-permute-start.5 = (f32[136,128]{1,0:T(8,128)S(1)}, f32[136,128]{1,0:T(8,128)S(1)}, u32[]{:S(2)}, u32[]{:S(2)}) collective-permute-start(f32[136,128]{1,0:T(8,128)S(1)} %get-tuple-element.12), channel_id=1, source_target_pairs={{0,192},{32,224},{64,0},{96,32},{128,64},{160,96},{192,128},{224,1... | collective-permute-start | bytes 208904 | tf_op jit(solution)/shard_map/ppermute | solution.py:200
  66.0 11.9 %all-to-all-start.1 = ((f32[2,32,1]{0,2,1:T(1,128)}), f32[2,32,1]{0,2,1:T(1,128)S(1)}, u32[]{:S(2)}, u32[]{:S(2)}) async-start(f32[2,32,1]{0,2,1:T(1,128)} %copy.18), calls=%async_computation.1 | async-start | bytes 32768 | tf_op jit(solution)/shard_map/all_to_all | solution.py:189
  70.9 10.0 %collective-permute-start.4 = (f32[136,128]{1,0:T(8,128)S(1)}, f32[136,128]{1,0:T(8,128)S(1)}, u32[]{:S(2)}, u32[]{:S(2)}) collective-permute-start(f32[136,128]{1,0:T(8,128)S(1)} %get-tuple-element.13), channel_id=1, source_target_pairs={{0,160},{32,192},{64,224},{96,0},{128,32},{160,64},{192,96},{224,1... | collective-permute-start | bytes 208904 | tf_op jit(solution)/shard_map/ppermute | solution.py:200
  71.2 9.8 %collective-permute-start.3 = (f32[136,128]{1,0:T(8,128)S(1)}, f32[136,128]{1,0:T(8,128)S(1)}, u32[]{:S(2)}, u32[]{:S(2)}) collective-permute-start(f32[136,128]{1,0:T(8,128)S(1)} %get-tuple-element.14), channel_id=1, source_target_pairs={{0,128},{32,160},{64,192},{96,224},{128,0},{160,32},{192,64},{224,... | collective-permute-start | bytes 208904 | tf_op jit(solution)/shard_map/ppermute | solution.py:200
  75.9 7.0 %collective-permute-start.2 = (f32[136,128]{1,0:T(8,128)S(1)}, f32[136,128]{1,0:T(8,128)S(1)}, u32[]{:S(2)}, u32[]{:S(2)}) collective-permute-start(f32[136,128]{1,0:T(8,128)S(1)} %get-tuple-element.15), channel_id=1, source_target_pairs={{0,96},{32,128},{64,160},{96,192},{128,224},{160,0},{192,32},{224,... | collective-permute-start | bytes 208904 | tf_op jit(solution)/shard_map/ppermute | solution.py:200
  78.8 9.1 %collective-permute-start.1 = (f32[136,128]{1,0:T(8,128)S(1)}, f32[136,128]{1,0:T(8,128)S(1)}, u32[]{:S(2)}, u32[]{:S(2)}) collective-permute-start(f32[136,128]{1,0:T(8,128)S(1)} %get-tuple-element.16), channel_id=1, source_target_pairs={{0,64},{32,96},{64,128},{96,160},{128,192},{160,224},{192,0},{224,... | collective-permute-start | bytes 208904 | tf_op jit(solution)/shard_map/ppermute | solution.py:200
  80.1 9.7 %collective-permute-start = (f32[136,128]{1,0:T(8,128)S(1)}, f32[136,128]{1,0:T(8,128)S(1)}, u32[]{:S(2)}, u32[]{:S(2)}) collective-permute-start(f32[136,128]{1,0:T(8,128)S(1)} %get-tuple-element.10), channel_id=1, source_target_pairs={{0,32},{32,64},{64,96},{96,128},{128,160},{160,192},{192,224},{224... | collective-permute-start | bytes 208904 | tf_op jit(solution)/shard_map/ppermute | solution.py:200

commit v10 on v9

--- a/solution.py
+++ b/solution.py
@@ -10,7 +10,7 @@
 IMG = 128
 VOL = 256
 SHIFTS = (-1, 0, 1)
-TK = 8192
+TK = 16384
 TN = 1024
 
 
@@ -99,27 +99,30 @@
     band = pix // groups
     width = band // IMG
 
-    def plane_tiles(j, carry):
-        n0 = pl.multiple_of(j * band, band)
-        summed = jnp.zeros((2 * depth, band), jnp.float32)
+    def plane_tiles(jj, carry):
+        n0 = pl.multiple_of(jj * 2 * band, 2 * band)
+        summed = jnp.zeros((2 * depth, 2 * band), jnp.float32)
         for ai, a in enumerate(SHIFTS):
             start = pl.multiple_of(n0 + IMG * (1 - a), IMG)
             for bi in range(3):
                 summed = summed + jnp.dot(
-                    v_ref[ai * 3 + bi].astype(jnp.bfloat16), ext_ref[bi, :, pl.ds(start, band)],
+                    v_ref[ai * 3 + bi].astype(jnp.bfloat16), ext_ref[bi, :, pl.ds(start, 2 * band)],
                     preferred_element_type=jnp.float32,
                 )
-        plane = summed[0:depth] + summed[depth:2 * depth]
-        before = lax.rem(j + groups - 1, groups)
-        for z in range(depth):
-            for u in range(width):
-                row = z * (width + 1) + u
-                planes_ref[j, pl.ds(row, 1), :] = plane[z:z + 1, u * IMG:(u + 1) * IMG]
-            row = z * (width + 1) + width
-            planes_ref[before, pl.ds(row, 1), :] = plane[z:z + 1, 0:IMG]
+        both = summed[0:depth] + summed[depth:2 * depth]
+        for half in range(2):
+            j = jj * 2 + half
+            plane = both[:, half * band:(half + 1) * band]
+            before = lax.rem(j + groups - 1, groups)
+            for z in range(depth):
+                for u in range(width):
+                    row = z * (width + 1) + u
+                    planes_ref[j, pl.ds(row, 1), :] = plane[z:z + 1, u * IMG:(u + 1) * IMG]
+                row = z * (width + 1) + width
+                planes_ref[before, pl.ds(row, 1), :] = plane[z:z + 1, 0:IMG]
         return carry
 
-    lax.fori_loop(0, groups, plane_tiles, 0)
+    lax.fori_loop(0, groups // 2, plane_tiles, 0)
 
 
 def class_pass(rows_ext, templates, scale_row, energy_col, gain, pix, groups):

time: 91.5 us -> 90.6 us (level)
  Pallas kernels: 10.8 us -> 9.79 us
    pallas_call x1, Pallas kernels: 10.8 us -> 9.79 us  [class_pass(): pl.pallas_call(functools.partial(class_kernel, pix, groups), out_shape=(j...]
where the time goes in v10:
time: 90.6 us; the launch traced here: 90.3 us
  waiting for transfers between devices  37.9 us (42%)
  starting transfers between devices  27.5 us (30%)
  Pallas kernels  9.79 us (11%)
  local copies, waits for them, and re-layouts  8.04 us (9%)
  matrix products  3.39 us (4%)
  other arithmetic  2.73 us (3%)
    all_to_all x1, waiting for transfers between devices, on_device(): lax.all_to_all(outgoing, 'dev', split_axis=1, concat_axis=1, tiled=True)  27.5 us
    ppermute x7, starting transfers between devices, on_device(): mine = mine + lax.ppermute(part, 'grp', pairs)  13.9 us
    pallas_call x1, Pallas kernels, class_pass(): pl.pallas_call(functools.partial(class_kernel, pix, groups), out_shape=(j...  9.79 us
    all_to_all x1, starting transfers between devices, on_device(): lax.all_to_all(outgoing, 'dev', split_axis=1, concat_axis=1, tiled=True)  8.77 us
    ppermute x7, waiting for transfers between devices, on_device(): mine = mine + lax.ppermute(part, 'grp', pairs)  8.65 us
    all_to_all x1, starting transfers between devices, on_device(): lax.all_to_all(stacked, 'dev', split_axis=1, concat_axis=1, tiled=True)  4.9 us
    reshape x1, local copies, waits for them, and re-layouts, on_device(): outgoing = outgoing.reshape(slot_depth, sources, owned_classes * width)  2.95 us
    dot_general x1, matrix products, on_device(): jnp.dot(placing, carried, preferred_element_type=jnp.float32)  1.91 us
  transfers between devices with their start and end apart: 9, of which 5 were waited for; matrix products, arithmetic and copies ran while one was open for 5% of the time, Pallas kernels for 0%

profile of v10, /device:TPU:1, one launch (start us, length us, event | category | flops | bytes accessed | tf_op | source)
XLA Modules:
  0.0 90.3 jit_solution(320852057838829186)
XLA Ops:
  0.6 0.9 %convert_reduce_fusion.1 = (s32[32]{0:T(128)S(1)}, s32[32]{0:T(128)S(1)}) fusion(s32[32]{0:T(128)} %bitcast.51, s32[32]{0:T(128)} %param.9), kind=kLoop, calls=%fused_computation.44 | loop fusion | flops 8128 | bytes 512 | tf_op jit(solution)/shard_map/reduce_sum | solution.py:172
  1.6 0.7 broadcast_in_dim.86
  2.3 1.9 %convolution_convert_fusion = bf16[64,16512]{1,0:T(8,128)(2,1)S(1)} fusion(bf16[32,128]{1,0:T(8,128)(2,1)S(1)} %broadcast_in_dim.86, bf16[32,16384]{1,0:T(8,128)(2,1)} %param.6, s32[32]{0:T(128)S(1)} %get-tuple-element.9), kind=kOutput, calls=%fused_computation.1 | convolution fusion | flops 70805504 | bytes 3170432 | tf_op jit(solution)/shard_map/dot_general | solution.py:181
  4.2 2.9 %copy.15 = bf16[2,32,16512]{2,0,1:T(2,128)(2,1)} copy(bf16[2,32,16512]{2,1,0:T(8,128)(2,1)S(1)} %bitcast.49) | data formatting | bytes 4227072 | tf_op jit(solution)/shard_map/reshape | solution.py:182
  7.1 0.0 copy-start
  7.1 8.8 %all-to-all-start = ((bf16[2,32,16512]{2,0,1:T(2,128)(2,1)}), bf16[2,32,16512]{2,0,1:T(2,128)(2,1)}, u32[]{:S(2)}, u32[]{:S(2)}) async-start(bf16[2,32,16512]{2,0,1:T(2,128)(2,1)} %copy.15), calls=%async_computation | async-start | bytes 4227072 | tf_op jit(solution)/shard_map/all_to_all | solution.py:183
  16.0 0.0 copy-done
  16.0 0.4 multiply_reduce_fusion
  16.4 0.1 copy.17.energy_ref
  16.5 0.1 mul.46
  16.6 0.1 mul.47
  16.7 0.1 add_select_fusion
  16.8 0.1 mul.44
  16.9 0.0 copy-start.1
  16.9 27.5 %all-to-all-done = bf16[2,32,16512]{2,0,1:T(2,128)(2,1)} async-done(((bf16[2,32,16512]{2,0,1:T(2,128)(2,1)}), bf16[2,32,16512]{2,0,1:T(2,128)(2,1)}, u32[]{:S(2)}, u32[]{:S(2)}) %all-to-all-start) | async-done | bytes 2113568 | tf_op jit(solution)/shard_map/all_to_all | solution.py:183
  44.5 1.8 %copy.16 = bf16[2,32,16512]{2,1,0:T(8,128)(2,1)S(1)} copy(bf16[2,32,16512]{2,0,1:T(2,128)(2,1)} %all-to-all-done) | data formatting | bytes 4227072 | tf_op jit(solution)/shard_map/all_to_all | solution.py:183
  46.3 0.1 convert_reduce_fusion
  46.4 0.0 copy-done.1
  46.4 9.8 %shard_map.77 = (f32[8,136,128]{2,1,0:T(8,128)S(1)}, f32[1,64]{1,0:T(1,128)S(1)}) custom-call(bf16[64,16512]{1,0:T(8,128)(2,1)S(1)} %bitcast.46, bf16[48,16384]{1,0:T(8,128)(2,1)S(1)} %bitcast.47, f32[1,64]{1,0:T(1,128)S(1)} %bitcast.48, f32[48,1]{1,0:T(8,128)S(1)} %copy.17.energy_ref, f32[8,48]{1,0:T(8,128)S(1)} %copy-done.1), custom_call_target="tpu_custom_call" | custom-call | flops 1207959552 | bytes 4210688 | tf_op jit(solution)/shard_map/pallas_call | solution.py:138
  56.2 0.1 dynamic-slice_bitcast_fusion.6
  56.2 5.7 %collective-permute-start.6 = (f32[136,128]{1,0:T(8,128)S(1)}, f32[136,128]{1,0:T(8,128)S(1)}, u32[]{:S(2)}, u32[]{:S(2)}) collective-permute-start(f32[136,128]{1,0:T(8,128)S(1)} %get-tuple-element.11), channel_id=1, source_target_pairs={{0,224},{32,0},{64,32},{96,64},{128,96},{160,128},{192,160},{224,1... | collective-permute-start | bytes 208904 | tf_op jit(solution)/shard_map/ppermute | solution.py:203
  61.9 1.2 %collective-permute-start.5 = (f32[136,128]{1,0:T(8,128)S(1)}, f32[136,128]{1,0:T(8,128)S(1)}, u32[]{:S(2)}, u32[]{:S(2)}) collective-permute-start(f32[136,128]{1,0:T(8,128)S(1)} %get-tuple-element.12), channel_id=1, source_target_pairs={{0,192},{32,224},{64,0},{96,32},{128,64},{160,96},{192,128},{224,1... | collective-permute-start | bytes 208904 | tf_op jit(solution)/shard_map/ppermute | solution.py:203
  63.1 0.5 broadcast.332
  63.6 0.7 reduce.5
  64.2 0.1 all_to_all.10
  64.3 0.7 copy.18
  65.0 4.9 %all-to-all-start.1 = ((f32[2,32,1]{0,2,1:T(1,128)}), f32[2,32,1]{0,2,1:T(1,128)S(1)}, u32[]{:S(2)}, u32[]{:S(2)}) async-start(f32[2,32,1]{0,2,1:T(1,128)} %copy.18), calls=%async_computation.1 | async-start | bytes 32768 | tf_op jit(solution)/shard_map/all_to_all | solution.py:192
  69.9 0.4 collective-permute-start.4
  70.4 4.8 %collective-permute-start.3 = (f32[136,128]{1,0:T(8,128)S(1)}, f32[136,128]{1,0:T(8,128)S(1)}, u32[]{:S(2)}, u32[]{:S(2)}) collective-permute-start(f32[136,128]{1,0:T(8,128)S(1)} %get-tuple-element.14), channel_id=1, source_target_pairs={{0,128},{32,160},{64,192},{96,224},{128,0},{160,32},{192,64},{224,... | collective-permute-start | bytes 208904 | tf_op jit(solution)/shard_map/ppermute | solution.py:203
  75.1 0.0 collective-permute-start.2
  75.1 1.8 %all-to-all-done.1 = f32[2,32,1]{0,2,1:T(1,128)S(1)} async-done(((f32[2,32,1]{0,2,1:T(1,128)}), f32[2,32,1]{0,2,1:T(1,128)S(1)}, u32[]{:S(2)}, u32[]{:S(2)}) %all-to-all-start.1) | async-done | bytes 288 | tf_op jit(solution)/shard_map/all_to_all | solution.py:192
  76.9 0.1 copy.19
  77.0 0.1 reshape.276
  77.1 0.7 gather_fusion
  77.8 0.0 collective-permute-done.6
  77.8 1.3 %collective-permute-start.1 = (f32[136,128]{1,0:T(8,128)S(1)}, f32[136,128]{1,0:T(8,128)S(1)}, u32[]{:S(2)}, u32[]{:S(2)}) collective-permute-start(f32[136,128]{1,0:T(8,128)S(1)} %get-tuple-element.16), channel_id=1, source_target_pairs={{0,64},{32,96},{64,128},{96,160},{128,192},{160,224},{192,0},{224,... | collective-permute-start | bytes 208904 | tf_op jit(solution)/shard_map/ppermute | solution.py:203
  79.1 0.0 collective-permute-done.5
  79.1 0.6 collective-permute-start
  79.6 0.5 and_select_fusion
  80.1 0.0 collective-permute-done.4
  80.1 0.0 collective-permute-done.3
  80.1 2.0 %collective-permute-done.2 = f32[136,128]{1,0:T(8,128)S(1)} collective-permute-done((f32[136,128]{1,0:T(8,128)S(1)}, f32[136,128]{1,0:T(8,128)S(1)}, u32[]{:S(2)}, u32[]{:S(2)}) %collective-permute-start.2) | collective-permute-done | bytes 69664 | tf_op jit(solution)/shard_map/ppermute | solution.py:203
  82.1 4.9 %collective-permute-done.1 = f32[136,128]{1,0:T(8,128)S(1)} collective-permute-done((f32[136,128]{1,0:T(8,128)S(1)}, f32[136,128]{1,0:T(8,128)S(1)}, u32[]{:S(2)}, u32[]{:S(2)}) %collective-permute-start.1) | collective-permute-done | bytes 69664 | tf_op jit(solution)/shard_map/ppermute | solution.py:203
  87.0 1.8 %collective-permute-done = f32[136,128]{1,0:T(8,128)S(1)} collective-permute-done((f32[136,128]{1,0:T(8,128)S(1)}, f32[136,128]{1,0:T(8,128)S(1)}, u32[]{:S(2)}, u32[]{:S(2)}) %collective-permute-start) | collective-permute-done | bytes 69664 | tf_op jit(solution)/shard_map/ppermute | solution.py:203
  88.8 0.4 convolution_bitcast_fusion
  89.2 1.1 %fusion.3 = f32[32,8,256]{2,1,0:T(8,128)} fusion(f32[136,256,1]{1,0,2:T(8,128)S(1)} %convolution_bitcast_fusion, f32[8,136]{1,0:T(8,128)S(1)} %mul.47, f32[32,136]{1,0:T(8,128)S(1)} %mul.44), kind=kOutput, calls=%fused_computation.7 | convolution fusion | flops 106989568 | bytes 423168 | tf_op jit(solution)/shard_map/dot_general | solution.py:211
  (8 shorter events, 0.1 us)
Async XLA Ops:
  7.1 8.8 %copy-start = (bf16[1,48,16384]{2,1,0:T(8,128)(2,1)S(1)}, bf16[1,48,16384]{2,1,0:T(8,128)(2,1)}, u32[]{:S(2)}) copy-start(bf16[1,48,16384]{2,1,0:T(8,128)(2,1)} %param.10) | copy-start | bytes 4718596
  7.1 37.3 %all-to-all-start = ((bf16[2,32,16512]{2,0,1:T(2,128)(2,1)}), bf16[2,32,16512]{2,0,1:T(2,128)(2,1)}, u32[]{:S(2)}, u32[]{:S(2)}) async-start(bf16[2,32,16512]{2,0,1:T(2,128)(2,1)} %copy.15), calls=%async_computation | async-start | bytes 4227072 | tf_op jit(solution)/shard_map/all_to_all | solution.py:183
  16.9 29.4 %copy-start.1 = (f32[8,48]{1,0:T(8,128)S(1)}, f32[8,48]{1,0:T(8,128)}, u32[]{:S(2)}) copy-start(f32[8,48]{1,0:T(8,128)} %gain_ref.1) | copy-start | bytes 4612
  56.2 21.5 %collective-permute-start.6 = (f32[136,128]{1,0:T(8,128)S(1)}, f32[136,128]{1,0:T(8,128)S(1)}, u32[]{:S(2)}, u32[]{:S(2)}) collective-permute-start(f32[136,128]{1,0:T(8,128)S(1)} %get-tuple-element.11), channel_id=1, source_target_pairs={{0,224},{32,0},{64,32},{96,64},{128,96},{160,128},{192,160},{224,1... | collective-permute-start | bytes 208904 | tf_op jit(solution)/shard_map/ppermute | solution.py:203
  61.9 17.2 %collective-permute-start.5 = (f32[136,128]{1,0:T(8,128)S(1)}, f32[136,128]{1,0:T(8,128)S(1)}, u32[]{:S(2)}, u32[]{:S(2)}) collective-permute-start(f32[136,128]{1,0:T(8,128)S(1)} %get-tuple-element.12), channel_id=1, source_target_pairs={{0,192},{32,224},{64,0},{96,32},{128,64},{160,96},{192,128},{224,1... | collective-permute-start | bytes 208904 | tf_op jit(solution)/shard_map/ppermute | solution.py:203
  65.0 11.9 %all-to-all-start.1 = ((f32[2,32,1]{0,2,1:T(1,128)}), f32[2,32,1]{0,2,1:T(1,128)S(1)}, u32[]{:S(2)}, u32[]{:S(2)}) async-start(f32[2,32,1]{0,2,1:T(1,128)} %copy.18), calls=%async_computation.1 | async-start | bytes 32768 | tf_op jit(solution)/shard_map/all_to_all | solution.py:192
  69.9 10.2 %collective-permute-start.4 = (f32[136,128]{1,0:T(8,128)S(1)}, f32[136,128]{1,0:T(8,128)S(1)}, u32[]{:S(2)}, u32[]{:S(2)}) collective-permute-start(f32[136,128]{1,0:T(8,128)S(1)} %get-tuple-element.13), channel_id=1, source_target_pairs={{0,160},{32,192},{64,224},{96,0},{128,32},{160,64},{192,96},{224,1... | collective-permute-start | bytes 208904 | tf_op jit(solution)/shard_map/ppermute | solution.py:203
  70.4 9.8 %collective-permute-start.3 = (f32[136,128]{1,0:T(8,128)S(1)}, f32[136,128]{1,0:T(8,128)S(1)}, u32[]{:S(2)}, u32[]{:S(2)}) collective-permute-start(f32[136,128]{1,0:T(8,128)S(1)} %get-tuple-element.14), channel_id=1, source_target_pairs={{0,128},{32,160},{64,192},{96,224},{128,0},{160,32},{192,64},{224,... | collective-permute-start | bytes 208904 | tf_op jit(solution)/shard_map/ppermute | solution.py:203
  75.1 7.0 %collective-permute-start.2 = (f32[136,128]{1,0:T(8,128)S(1)}, f32[136,128]{1,0:T(8,128)S(1)}, u32[]{:S(2)}, u32[]{:S(2)}) collective-permute-start(f32[136,128]{1,0:T(8,128)S(1)} %get-tuple-element.15), channel_id=1, source_target_pairs={{0,96},{32,128},{64,160},{96,192},{128,224},{160,0},{192,32},{224,... | collective-permute-start | bytes 208904 | tf_op jit(solution)/shard_map/ppermute | solution.py:203
  77.8 9.2 %collective-permute-start.1 = (f32[136,128]{1,0:T(8,128)S(1)}, f32[136,128]{1,0:T(8,128)S(1)}, u32[]{:S(2)}, u32[]{:S(2)}) collective-permute-start(f32[136,128]{1,0:T(8,128)S(1)} %get-tuple-element.16), channel_id=1, source_target_pairs={{0,64},{32,96},{64,128},{96,160},{128,192},{160,224},{192,0},{224,... | collective-permute-start | bytes 208904 | tf_op jit(solution)/shard_map/ppermute | solution.py:203
  79.1 9.7 %collective-permute-start = (f32[136,128]{1,0:T(8,128)S(1)}, f32[136,128]{1,0:T(8,128)S(1)}, u32[]{:S(2)}, u32[]{:S(2)}) collective-permute-start(f32[136,128]{1,0:T(8,128)S(1)} %get-tuple-element.10), channel_id=1, source_target_pairs={{0,32},{32,64},{64,96},{96,128},{128,160},{160,192},{192,224},{224... | collective-permute-start | bytes 208904 | tf_op jit(solution)/shard_map/ppermute | solution.py:203

commit v11 on v10

--- a/solution.py
+++ b/solution.py
@@ -202,13 +202,13 @@
         pairs = [(g, (g + step) % groups) for g in range(groups)]
         mine = mine + lax.ppermute(part, "grp", pairs)
     interp = upsample_table(VOL, IMG)
-    across = jnp.dot(mine, interp.T, precision=lax.Precision.HIGHEST)
+    across = jnp.dot(mine, interp.T, precision=lax.Precision.HIGH)
     rows_table = local_table(2 * band, band + 1)
     eye = jnp.eye(depth, dtype=jnp.float32)
     block = (rows_table[:, None, None, :] * eye[None, :, :, None]).reshape(
         2 * band * depth, depth * (band + 1)
     )
-    volume = jnp.dot(block, across, precision=lax.Precision.HIGHEST).reshape(2 * band, depth, VOL)
+    volume = jnp.dot(block, across, precision=lax.Precision.HIGH).reshape(2 * band, depth, VOL)
     return (volume, particle_evidence)
 
 

time: 90.6 us -> 90.4 us (level)
  no operation moved by 1% of the time
where the time goes in v11:
time: 90.4 us; the launch traced here: 90.1 us
  waiting for transfers between devices  37.9 us (42%)
  starting transfers between devices  27.5 us (30%)
  Pallas kernels  9.79 us (11%)
  local copies, waits for them, and re-layouts  8.04 us (9%)
  matrix products  3.25 us (4%)
  other arithmetic  2.73 us (3%)
    all_to_all x1, waiting for transfers between devices, on_device(): lax.all_to_all(outgoing, 'dev', split_axis=1, concat_axis=1, tiled=True)  27.5 us
    ppermute x7, starting transfers between devices, on_device(): mine = mine + lax.ppermute(part, 'grp', pairs)  13.9 us
    pallas_call x1, Pallas kernels, class_pass(): pl.pallas_call(functools.partial(class_kernel, pix, groups), out_shape=(j...  9.79 us
    all_to_all x1, starting transfers between devices, on_device(): lax.all_to_all(outgoing, 'dev', split_axis=1, concat_axis=1, tiled=True)  8.77 us
    ppermute x7, waiting for transfers between devices, on_device(): mine = mine + lax.ppermute(part, 'grp', pairs)  8.65 us
    all_to_all x1, starting transfers between devices, on_device(): lax.all_to_all(stacked, 'dev', split_axis=1, concat_axis=1, tiled=True)  4.9 us
    reshape x1, local copies, waits for them, and re-layouts, on_device(): outgoing = outgoing.reshape(slot_depth, sources, owned_classes * width)  2.95 us
    dot_general x1, matrix products, on_device(): jnp.dot(placing, carried, preferred_element_type=jnp.float32)  1.91 us
  transfers between devices with their start and end apart: 9, of which 5 were waited for; matrix products, arithmetic and copies ran while one was open for 5% of the time, Pallas kernels for 0%

profile of v11, /device:TPU:1, one launch (start us, length us, event | category | flops | bytes accessed | tf_op | source)
XLA Modules:
  0.0 90.1 jit_solution(15881758416429830348)
XLA Ops:
  0.6 0.9 %convert_reduce_fusion.1 = (s32[32]{0:T(128)S(1)}, s32[32]{0:T(128)S(1)}) fusion(s32[32]{0:T(128)} %bitcast.51, s32[32]{0:T(128)} %param.9), kind=kLoop, calls=%fused_computation.44 | loop fusion | flops 8128 | bytes 512 | tf_op jit(solution)/shard_map/reduce_sum | solution.py:172
  1.6 0.7 broadcast_in_dim.86
  2.3 1.9 %convolution_convert_fusion = bf16[64,16512]{1,0:T(8,128)(2,1)S(1)} fusion(bf16[32,128]{1,0:T(8,128)(2,1)S(1)} %broadcast_in_dim.86, bf16[32,16384]{1,0:T(8,128)(2,1)} %param.6, s32[32]{0:T(128)S(1)} %get-tuple-element.9), kind=kOutput, calls=%fused_computation.1 | convolution fusion | flops 70805504 | bytes 3170432 | tf_op jit(solution)/shard_map/dot_general | solution.py:181
  4.2 2.9 %copy.15 = bf16[2,32,16512]{2,0,1:T(2,128)(2,1)} copy(bf16[2,32,16512]{2,1,0:T(8,128)(2,1)S(1)} %bitcast.49) | data formatting | bytes 4227072 | tf_op jit(solution)/shard_map/reshape | solution.py:182
  7.1 0.0 copy-start
  7.1 8.8 %all-to-all-start = ((bf16[2,32,16512]{2,0,1:T(2,128)(2,1)}), bf16[2,32,16512]{2,0,1:T(2,128)(2,1)}, u32[]{:S(2)}, u32[]{:S(2)}) async-start(bf16[2,32,16512]{2,0,1:T(2,128)(2,1)} %copy.15), calls=%async_computation | async-start | bytes 4227072 | tf_op jit(solution)/shard_map/all_to_all | solution.py:183
  16.0 0.0 copy-done
  16.0 0.4 multiply_reduce_fusion
  16.4 0.1 copy.17.energy_ref
  16.5 0.1 mul.46
  16.6 0.1 mul.47
  16.7 0.1 add_select_fusion
  16.8 0.1 mul.44
  16.9 0.0 copy-start.1
  16.9 27.5 %all-to-all-done = bf16[2,32,16512]{2,0,1:T(2,128)(2,1)} async-done(((bf16[2,32,16512]{2,0,1:T(2,128)(2,1)}), bf16[2,32,16512]{2,0,1:T(2,128)(2,1)}, u32[]{:S(2)}, u32[]{:S(2)}) %all-to-all-start) | async-done | bytes 2113568 | tf_op jit(solution)/shard_map/all_to_all | solution.py:183
  44.5 1.8 %copy.16 = bf16[2,32,16512]{2,1,0:T(8,128)(2,1)S(1)} copy(bf16[2,32,16512]{2,0,1:T(2,128)(2,1)} %all-to-all-done) | data formatting | bytes 4227072 | tf_op jit(solution)/shard_map/all_to_all | solution.py:183
  46.3 0.1 convert_reduce_fusion
  46.4 0.0 copy-done.1
  46.4 9.8 %shard_map.77 = (f32[8,136,128]{2,1,0:T(8,128)S(1)}, f32[1,64]{1,0:T(1,128)S(1)}) custom-call(bf16[64,16512]{1,0:T(8,128)(2,1)S(1)} %bitcast.46, bf16[48,16384]{1,0:T(8,128)(2,1)S(1)} %bitcast.47, f32[1,64]{1,0:T(1,128)S(1)} %bitcast.48, f32[48,1]{1,0:T(8,128)S(1)} %copy.17.energy_ref, f32[8,48]{1,0:T(8,128)S(1)} %copy-done.1), custom_call_target="tpu_custom_call" | custom-call | flops 1207959552 | bytes 4210688 | tf_op jit(solution)/shard_map/pallas_call | solution.py:138
  56.2 0.1 dynamic-slice_bitcast_fusion.6
  56.2 5.7 %collective-permute-start.6 = (f32[136,128]{1,0:T(8,128)S(1)}, f32[136,128]{1,0:T(8,128)S(1)}, u32[]{:S(2)}, u32[]{:S(2)}) collective-permute-start(f32[136,128]{1,0:T(8,128)S(1)} %get-tuple-element.11), channel_id=1, source_target_pairs={{0,224},{32,0},{64,32},{96,64},{128,96},{160,128},{192,160},{224,1... | collective-permute-start | bytes 208904 | tf_op jit(solution)/shard_map/ppermute | solution.py:203
  61.9 1.2 %collective-permute-start.5 = (f32[136,128]{1,0:T(8,128)S(1)}, f32[136,128]{1,0:T(8,128)S(1)}, u32[]{:S(2)}, u32[]{:S(2)}) collective-permute-start(f32[136,128]{1,0:T(8,128)S(1)} %get-tuple-element.12), channel_id=1, source_target_pairs={{0,192},{32,224},{64,0},{96,32},{128,64},{160,96},{192,128},{224,1... | collective-permute-start | bytes 208904 | tf_op jit(solution)/shard_map/ppermute | solution.py:203
  63.1 0.5 broadcast.332
  63.6 0.7 reduce.5
  64.2 0.1 all_to_all.10
  64.3 0.7 copy.18
  65.0 4.9 %all-to-all-start.1 = ((f32[2,32,1]{0,2,1:T(1,128)}), f32[2,32,1]{0,2,1:T(1,128)S(1)}, u32[]{:S(2)}, u32[]{:S(2)}) async-start(f32[2,32,1]{0,2,1:T(1,128)} %copy.18), calls=%async_computation.1 | async-start | bytes 32768 | tf_op jit(solution)/shard_map/all_to_all | solution.py:192
  69.9 0.4 collective-permute-start.4
  70.4 4.8 %collective-permute-start.3 = (f32[136,128]{1,0:T(8,128)S(1)}, f32[136,128]{1,0:T(8,128)S(1)}, u32[]{:S(2)}, u32[]{:S(2)}) collective-permute-start(f32[136,128]{1,0:T(8,128)S(1)} %get-tuple-element.14), channel_id=1, source_target_pairs={{0,128},{32,160},{64,192},{96,224},{128,0},{160,32},{192,64},{224,... | collective-permute-start | bytes 208904 | tf_op jit(solution)/shard_map/ppermute | solution.py:203
  75.1 0.0 collective-permute-start.2
  75.1 1.8 %all-to-all-done.1 = f32[2,32,1]{0,2,1:T(1,128)S(1)} async-done(((f32[2,32,1]{0,2,1:T(1,128)}), f32[2,32,1]{0,2,1:T(1,128)S(1)}, u32[]{:S(2)}, u32[]{:S(2)}) %all-to-all-start.1) | async-done | bytes 288 | tf_op jit(solution)/shard_map/all_to_all | solution.py:192
  76.9 0.1 copy.19
  77.0 0.1 reshape.276
  77.1 0.7 gather_fusion
  77.8 0.0 collective-permute-done.6
  77.8 1.3 %collective-permute-start.1 = (f32[136,128]{1,0:T(8,128)S(1)}, f32[136,128]{1,0:T(8,128)S(1)}, u32[]{:S(2)}, u32[]{:S(2)}) collective-permute-start(f32[136,128]{1,0:T(8,128)S(1)} %get-tuple-element.16), channel_id=1, source_target_pairs={{0,64},{32,96},{64,128},{96,160},{128,192},{160,224},{192,0},{224,... | collective-permute-start | bytes 208904 | tf_op jit(solution)/shard_map/ppermute | solution.py:203
  79.1 0.0 collective-permute-done.5
  79.1 0.6 collective-permute-start
  79.6 0.5 and_select_fusion
  80.1 0.0 collective-permute-done.4
  80.1 0.0 collective-permute-done.3
  80.1 2.0 %collective-permute-done.2 = f32[136,128]{1,0:T(8,128)S(1)} collective-permute-done((f32[136,128]{1,0:T(8,128)S(1)}, f32[136,128]{1,0:T(8,128)S(1)}, u32[]{:S(2)}, u32[]{:S(2)}) %collective-permute-start.2) | collective-permute-done | bytes 69664 | tf_op jit(solution)/shard_map/ppermute | solution.py:203
  82.1 4.9 %collective-permute-done.1 = f32[136,128]{1,0:T(8,128)S(1)} collective-permute-done((f32[136,128]{1,0:T(8,128)S(1)}, f32[136,128]{1,0:T(8,128)S(1)}, u32[]{:S(2)}, u32[]{:S(2)}) %collective-permute-start.1) | collective-permute-done | bytes 69664 | tf_op jit(solution)/shard_map/ppermute | solution.py:203
  87.0 1.8 %collective-permute-done = f32[136,128]{1,0:T(8,128)S(1)} collective-permute-done((f32[136,128]{1,0:T(8,128)S(1)}, f32[136,128]{1,0:T(8,128)S(1)}, u32[]{:S(2)}, u32[]{:S(2)}) %collective-permute-start) | collective-permute-done | bytes 69664 | tf_op jit(solution)/shard_map/ppermute | solution.py:203
  88.8 0.4 convolution_bitcast_fusion
  89.2 1.0 %fusion.3 = f32[32,8,256]{2,1,0:T(8,128)} fusion(f32[136,256,1]{1,0,2:T(8,128)S(1)} %convolution_bitcast_fusion, f32[8,136]{1,0:T(8,128)S(1)} %mul.47, f32[32,136]{1,0:T(8,128)S(1)} %mul.44), kind=kOutput, calls=%fused_computation.7 | convolution fusion | flops 53512192 | bytes 423168 | tf_op jit(solution)/shard_map/dot_general | solution.py:211
  (8 shorter events, 0.1 us)
Async XLA Ops:
  7.1 8.8 %copy-start = (bf16[1,48,16384]{2,1,0:T(8,128)(2,1)S(1)}, bf16[1,48,16384]{2,1,0:T(8,128)(2,1)}, u32[]{:S(2)}) copy-start(bf16[1,48,16384]{2,1,0:T(8,128)(2,1)} %param.10) | copy-start | bytes 4718596
  7.1 37.3 %all-to-all-start = ((bf16[2,32,16512]{2,0,1:T(2,128)(2,1)}), bf16[2,32,16512]{2,0,1:T(2,128)(2,1)}, u32[]{:S(2)}, u32[]{:S(2)}) async-start(bf16[2,32,16512]{2,0,1:T(2,128)(2,1)} %copy.15), calls=%async_computation | async-start | bytes 4227072 | tf_op jit(solution)/shard_map/all_to_all | solution.py:183
  16.9 29.4 %copy-start.1 = (f32[8,48]{1,0:T(8,128)S(1)}, f32[8,48]{1,0:T(8,128)}, u32[]{:S(2)}) copy-start(f32[8,48]{1,0:T(8,128)} %gain_ref.1) | copy-start | bytes 4612
  56.2 21.5 %collective-permute-start.6 = (f32[136,128]{1,0:T(8,128)S(1)}, f32[136,128]{1,0:T(8,128)S(1)}, u32[]{:S(2)}, u32[]{:S(2)}) collective-permute-start(f32[136,128]{1,0:T(8,128)S(1)} %get-tuple-element.11), channel_id=1, source_target_pairs={{0,224},{32,0},{64,32},{96,64},{128,96},{160,128},{192,160},{224,1... | collective-permute-start | bytes 208904 | tf_op jit(solution)/shard_map/ppermute | solution.py:203
  61.9 17.2 %collective-permute-start.5 = (f32[136,128]{1,0:T(8,128)S(1)}, f32[136,128]{1,0:T(8,128)S(1)}, u32[]{:S(2)}, u32[]{:S(2)}) collective-permute-start(f32[136,128]{1,0:T(8,128)S(1)} %get-tuple-element.12), channel_id=1, source_target_pairs={{0,192},{32,224},{64,0},{96,32},{128,64},{160,96},{192,128},{224,1... | collective-permute-start | bytes 208904 | tf_op jit(solution)/shard_map/ppermute | solution.py:203
  65.0 11.9 %all-to-all-start.1 = ((f32[2,32,1]{0,2,1:T(1,128)}), f32[2,32,1]{0,2,1:T(1,128)S(1)}, u32[]{:S(2)}, u32[]{:S(2)}) async-start(f32[2,32,1]{0,2,1:T(1,128)} %copy.18), calls=%async_computation.1 | async-start | bytes 32768 | tf_op jit(solution)/shard_map/all_to_all | solution.py:192
  69.9 10.2 %collective-permute-start.4 = (f32[136,128]{1,0:T(8,128)S(1)}, f32[136,128]{1,0:T(8,128)S(1)}, u32[]{:S(2)}, u32[]{:S(2)}) collective-permute-start(f32[136,128]{1,0:T(8,128)S(1)} %get-tuple-element.13), channel_id=1, source_target_pairs={{0,160},{32,192},{64,224},{96,0},{128,32},{160,64},{192,96},{224,1... | collective-permute-start | bytes 208904 | tf_op jit(solution)/shard_map/ppermute | solution.py:203
  70.4 9.8 %collective-permute-start.3 = (f32[136,128]{1,0:T(8,128)S(1)}, f32[136,128]{1,0:T(8,128)S(1)}, u32[]{:S(2)}, u32[]{:S(2)}) collective-permute-start(f32[136,128]{1,0:T(8,128)S(1)} %get-tuple-element.14), channel_id=1, source_target_pairs={{0,128},{32,160},{64,192},{96,224},{128,0},{160,32},{192,64},{224,... | collective-permute-start | bytes 208904 | tf_op jit(solution)/shard_map/ppermute | solution.py:203
  75.1 7.0 %collective-permute-start.2 = (f32[136,128]{1,0:T(8,128)S(1)}, f32[136,128]{1,0:T(8,128)S(1)}, u32[]{:S(2)}, u32[]{:S(2)}) collective-permute-start(f32[136,128]{1,0:T(8,128)S(1)} %get-tuple-element.15), channel_id=1, source_target_pairs={{0,96},{32,128},{64,160},{96,192},{128,224},{160,0},{192,32},{224,... | collective-permute-start | bytes 208904 | tf_op jit(solution)/shard_map/ppermute | solution.py:203
  77.8 9.2 %collective-permute-start.1 = (f32[136,128]{1,0:T(8,128)S(1)}, f32[136,128]{1,0:T(8,128)S(1)}, u32[]{:S(2)}, u32[]{:S(2)}) collective-permute-start(f32[136,128]{1,0:T(8,128)S(1)} %get-tuple-element.16), channel_id=1, source_target_pairs={{0,64},{32,96},{64,128},{96,160},{128,192},{160,224},{192,0},{224,... | collective-permute-start | bytes 208904 | tf_op jit(solution)/shard_map/ppermute | solution.py:203
  79.1 9.7 %collective-permute-start = (f32[136,128]{1,0:T(8,128)S(1)}, f32[136,128]{1,0:T(8,128)S(1)}, u32[]{:S(2)}, u32[]{:S(2)}) collective-permute-start(f32[136,128]{1,0:T(8,128)S(1)} %get-tuple-element.10), channel_id=1, source_target_pairs={{0,32},{32,64},{64,96},{96,128},{128,160},{160,192},{192,224},{224... | collective-permute-start | bytes 208904 | tf_op jit(solution)/shard_map/ppermute | solution.py:203

commit v12 on v11

--- a/solution.py
+++ b/solution.py
@@ -170,26 +170,23 @@
     ordinal = jnp.arange(local_count, dtype=jnp.int32)
     earlier = (labels[:, None] == labels[None, :]) & (ordinal[None, :] < ordinal[:, None])
     arrival = jnp.sum(earlier, axis=1)
-    slot_index = arrival * classes + position
+    slot_index = position * slot_depth + arrival
     total_slots = classes * slot_depth
-    placing = (jnp.arange(total_slots, dtype=jnp.int32)[:, None] == slot_index[None, :]).astype(
-        jnp.bfloat16
-    )
     extra = jnp.broadcast_to(particle_precision[:, None], (local_count, IMG))
     carried = jnp.concatenate([particles, extra], axis=1)
     width = pix + IMG
-    outgoing = jnp.dot(placing, carried, preferred_element_type=jnp.float32).astype(jnp.bfloat16)
-    outgoing = outgoing.reshape(slot_depth, sources, owned_classes * width)
-    arrived = lax.all_to_all(outgoing, "dev", split_axis=1, concat_axis=1, tiled=True)
-    rows_ext = arrived.reshape(slot_depth * sources, width)
-    scale_row = rows_ext[:, pix].astype(jnp.float32).reshape(1, slot_depth * sources)
+    outgoing = jnp.zeros((classes, slot_depth, width), carried.dtype)
+    outgoing = outgoing.at[position, arrival].set(carried, unique_indices=True)
+    arrived = lax.all_to_all(outgoing, "dev", split_axis=0, concat_axis=0, tiled=True)
+    rows_ext = arrived.reshape(sources * slot_depth, width)
+    scale_row = rows_ext[:, pix].astype(jnp.float32).reshape(1, sources * slot_depth)
     templates = references[0]
     energy_col = jnp.sum(jnp.square(templates.astype(jnp.float32)), axis=1).reshape(-1, 1)
     windows, class_evidence = class_pass(
         rows_ext, templates, scale_row, energy_col, insert_weights, pix, groups
     )
-    stacked = class_evidence.reshape(slot_depth, sources)
-    returned = lax.all_to_all(stacked, "dev", split_axis=1, concat_axis=1, tiled=True).reshape(
+    stacked = class_evidence.reshape(sources, slot_depth)
+    returned = lax.all_to_all(stacked, "dev", split_axis=0, concat_axis=0, tiled=True).reshape(
         total_slots
     )
     particle_evidence = jnp.take(returned, slot_index)

time: 90.4 us -> 116 us (1.28)
  local copies, waits for them, and re-layouts: 8.04 us -> 33.4 us
  other arithmetic: 2.73 us -> 4.72 us
  matrix products: 3.25 us -> 1.34 us
    scatter x0 -> x1, local copies, waits for them, and re-layouts: none -> 23.6 us  [on_device(): outgoing = outgoing.at[position, arrival].set(carried, unique_indices=True)]
    broadcast_in_dim x0 -> x1, local copies, waits for them, and re-layouts: none -> 2.4 us  [on_device(): outgoing = jnp.zeros((classes, slot_depth, width), carried.dtype)]
    all_to_all x4 -> x1, local copies, waits for them, and re-layouts: 2.66 us -> 0.71 us  [on_device(): lax.all_to_all(stacked, 'dev', split_axis=0, concat_axis=0, tiled=True)]
    dot_general x1 -> x0, matrix products: 1.91 us -> none  [on_device(): jnp.dot(placing, carried, preferred_element_type=jnp.float32)]
    unnamed x4 -> x6, local copies, waits for them, and re-layouts: 0.01 us -> 1.41 us
    concatenate x0 -> x1, other arithmetic: none -> 1.3 us  [on_device(): carried = jnp.concatenate([particles, extra], axis=1)]
  transfers between devices with their start and end apart: 9 -> 9, of which waited for: 5 -> 5; matrix products, arithmetic and copies ran while one was open for 5% -> 4% of each run, Pallas kernels for 0% -> 0%
where the time goes in v12:
time: 116 us; the launch traced here: 115 us
  waiting for transfers between devices  37.6 us (32%)
  local copies, waits for them, and re-layouts  33.4 us (29%)
  starting transfers between devices  27.3 us (24%)
  Pallas kernels  9.79 us (8%)
  other arithmetic  4.72 us (4%)
  matrix products  1.34 us (1%)
    all_to_all x1, waiting for transfers between devices, on_device(): lax.all_to_all(outgoing, 'dev', split_axis=0, concat_axis=0, tiled=True)  27.5 us
    scatter x1, local copies, waits for them, and re-layouts, on_device(): outgoing = outgoing.at[position, arrival].set(carried, unique_indices=True)  23.6 us
    ppermute x7, starting transfers between devices, on_device(): mine = mine + lax.ppermute(part, 'grp', pairs)  13.5 us
    pallas_call x1, Pallas kernels, class_pass(): pl.pallas_call(functools.partial(class_kernel, pix, groups), out_shape=(j...  9.79 us
    all_to_all x1, starting transfers between devices, on_device(): lax.all_to_all(outgoing, 'dev', split_axis=0, concat_axis=0, tiled=True)  8.83 us
    ppermute x7, waiting for transfers between devices, on_device(): mine = mine + lax.ppermute(part, 'grp', pairs)  8.21 us
    all_to_all x1, starting transfers between devices, on_device(): lax.all_to_all(stacked, 'dev', split_axis=0, concat_axis=0, tiled=True)  4.92 us
    reshape x1, local copies, waits for them, and re-layouts, on_device(): rows_ext = arrived.reshape(sources * slot_depth, width)  2.75 us
  transfers between devices with their start and end apart: 9, of which 5 were waited for; matrix products, arithmetic and copies ran while one was open for 4% of the time, Pallas kernels for 0%

profile of v12, /device:TPU:1, one launch (start us, length us, event | category | flops | bytes accessed | tf_op | source)
XLA Modules:
  0.0 114.9 jit_solution(2268628022881857063)
XLA Ops:
  0.6 0.9 select_reduce_fusion
  1.6 0.7 broadcast_in_dim.90
  2.3 1.3 %pad_maximum_fusion = bf16[32,16512]{1,0:T(8,128)(2,1)S(1)} fusion(bf16[32,128]{1,0:T(8,128)(2,1)S(1)} %broadcast_in_dim.90, bf16[32,16384]{1,0:T(8,128)(2,1)} %param.6), kind=kLoop, calls=%fused_computation.4 | loop fusion | flops 2113536 | bytes 2113536 | tf_op jit(solution)/shard_map/concatenate | solution.py:176
  3.6 2.4 %broadcast_in_dim.87 = bf16[32,2,16512]{2,1,0:T(2,128)(2,1)} broadcast(bf16[]{:T(256)} %constant.132.clone.1), dimensions={} | broadcast | bytes 2113538 | tf_op jit(solution)/shard_map/broadcast_in_dim | solution.py:178
  6.0 23.6 %scatter_fusion = bf16[32,2,16512]{2,1,0:T(2,128)(2,1)} fusion(bf16[32,2,16512]{2,1,0:T(2,128)(2,1)} %broadcast_in_dim.87, s32[32]{0:T(128)S(1)} %get-tuple-element.16, bf16[32,16512]{1,0:T(8,128)(2,1)S(1)} %pad_maximum_fusion), kind=kCustom, calls=%fused_computation.1 | custom fusion | bytes 3170560 | tf_op jit(solution)/shard_map/scatter | solution.py:179
  29.6 0.0 copy-start
  29.6 8.8 %all-to-all-start = ((bf16[32,2,16512]{2,1,0:T(2,128)(2,1)}), bf16[32,2,16512]{2,1,0:T(2,128)(2,1)}, u32[]{:S(2)}, u32[]{:S(2)}) async-start(bf16[32,2,16512]{2,1,0:T(2,128)(2,1)} %scatter_fusion), calls=%async_computation | async-start | bytes 4227072 | tf_op jit(solution)/shard_map/all_to_all | solution.py:180
  38.5 0.0 copy-done
  38.5 0.4 multiply_reduce_fusion
  38.9 0.1 copy.12.energy_ref
  39.0 0.1 mul.40
  39.1 0.1 mul.41
  39.2 0.1 add_select_fusion
  39.3 0.1 mul.38
  39.5 0.0 copy-start.2
  39.5 27.5 %all-to-all-done = bf16[32,2,16512]{2,1,0:T(2,128)(2,1)} async-done(((bf16[32,2,16512]{2,1,0:T(2,128)(2,1)}), bf16[32,2,16512]{2,1,0:T(2,128)(2,1)}, u32[]{:S(2)}, u32[]{:S(2)}) %all-to-all-start) | async-done | bytes 2113568 | tf_op jit(solution)/shard_map/all_to_all | solution.py:180
  67.0 2.7 %reshape.287.rows_ref = bf16[64,16512]{1,0:T(8,128)(2,1)S(1)} reshape(bf16[32,2,16512]{2,1,0:T(2,128)(2,1)} %all-to-all-done) | data formatting | bytes 4227072 | tf_op jit(solution)/shard_map/reshape | solution.py:181
  69.8 0.1 convert_reduce_fusion
  69.9 0.0 copy-done.2
  69.9 0.0 copy-start.1
  69.9 1.4 %copy-done.1 = bf16[1,48,16384]{2,1,0:T(8,128)(2,1)S(1)} copy-done((bf16[1,48,16384]{2,1,0:T(8,128)(2,1)S(1)}, bf16[1,48,16384]{2,1,0:T(8,128)(2,1)}, u32[]{:S(2)}) %copy-start.1) | copy-done | bytes 1572888
  71.3 9.8 %shard_map.77 = (f32[8,136,128]{2,1,0:T(8,128)S(1)}, f32[1,64]{1,0:T(1,128)S(1)}) custom-call(bf16[64,16512]{1,0:T(8,128)(2,1)S(1)} %reshape.287.rows_ref, bf16[48,16384]{1,0:T(8,128)(2,1)S(1)} %bitcast.56, f32[1,64]{1,0:T(1,128)S(1)} %bitcast.57, f32[48,1]{1,0:T(8,128)S(1)} %copy.12.energy_ref, f32[8,48]{1,0:T(8,128)S(1)} %copy-done.2), custom_call_target="tpu_custom_call" | custom-call | flops 1207959552 | bytes 4210688 | tf_op jit(solution)/shard_map/pallas_call | solution.py:138
  81.1 0.1 dynamic-slice_bitcast_fusion.6
  81.1 5.6 %collective-permute-start.6 = (f32[136,128]{1,0:T(8,128)S(1)}, f32[136,128]{1,0:T(8,128)S(1)}, u32[]{:S(2)}, u32[]{:S(2)}) collective-permute-start(f32[136,128]{1,0:T(8,128)S(1)} %get-tuple-element.9), channel_id=1, source_target_pairs={{0,224},{32,0},{64,32},{96,64},{128,96},{160,128},{192,160},{224,1... | collective-permute-start | bytes 208904 | tf_op jit(solution)/shard_map/ppermute | solution.py:200
  86.7 1.1 %collective-permute-start.5 = (f32[136,128]{1,0:T(8,128)S(1)}, f32[136,128]{1,0:T(8,128)S(1)}, u32[]{:S(2)}, u32[]{:S(2)}) collective-permute-start(f32[136,128]{1,0:T(8,128)S(1)} %get-tuple-element.10), channel_id=1, source_target_pairs={{0,192},{32,224},{64,0},{96,32},{128,64},{160,96},{192,128},{224,1... | collective-permute-start | bytes 208904 | tf_op jit(solution)/shard_map/ppermute | solution.py:200
  87.9 0.5 broadcast.379
  88.4 0.7 reduce.8
  89.0 0.7 all_to_all.10
  89.7 4.9 %all-to-all-start.1 = ((f32[32,1,2]{2,1,0:T(1,128)}), f32[32,1,2]{2,1,0:T(1,128)S(1)}, u32[]{:S(2)}, u32[]{:S(2)}) async-start(f32[32,1,2]{2,1,0:T(1,128)} %bitcast.15), calls=%async_computation.1 | async-start | bytes 32768 | tf_op jit(solution)/shard_map/all_to_all | solution.py:189
  94.7 0.3 collective-permute-start.4
  95.0 4.8 %collective-permute-start.3 = (f32[136,128]{1,0:T(8,128)S(1)}, f32[136,128]{1,0:T(8,128)S(1)}, u32[]{:S(2)}, u32[]{:S(2)}) collective-permute-start(f32[136,128]{1,0:T(8,128)S(1)} %get-tuple-element.12), channel_id=1, source_target_pairs={{0,128},{32,160},{64,192},{96,224},{128,0},{160,32},{192,64},{224,... | collective-permute-start | bytes 208904 | tf_op jit(solution)/shard_map/ppermute | solution.py:200
  99.8 0.0 collective-permute-start.2
  99.8 1.9 %all-to-all-done.1 = f32[32,1,2]{2,1,0:T(1,128)S(1)} async-done(((f32[32,1,2]{2,1,0:T(1,128)}), f32[32,1,2]{2,1,0:T(1,128)S(1)}, u32[]{:S(2)}, u32[]{:S(2)}) %all-to-all-start.1) | async-done | bytes 288 | tf_op jit(solution)/shard_map/all_to_all | solution.py:189
  101.6 0.7 reduce.9
  102.3 0.1 reshape.289
  102.4 0.7 gather_fusion
  103.1 0.0 collective-permute-done.6
  103.1 1.3 %collective-permute-start.1 = (f32[136,128]{1,0:T(8,128)S(1)}, f32[136,128]{1,0:T(8,128)S(1)}, u32[]{:S(2)}, u32[]{:S(2)}) collective-permute-start(f32[136,128]{1,0:T(8,128)S(1)} %get-tuple-element.14), channel_id=1, source_target_pairs={{0,64},{32,96},{64,128},{96,160},{128,192},{160,224},{192,0},{224,... | collective-permute-start | bytes 208904 | tf_op jit(solution)/shard_map/ppermute | solution.py:200
  104.4 0.0 collective-permute-done.5
  104.4 0.4 collective-permute-start
  104.9 0.5 and_select_fusion
  105.4 0.0 collective-permute-done.4
  105.4 0.0 collective-permute-done.3
  105.4 1.8 %collective-permute-done.2 = f32[136,128]{1,0:T(8,128)S(1)} collective-permute-done((f32[136,128]{1,0:T(8,128)S(1)}, f32[136,128]{1,0:T(8,128)S(1)}, u32[]{:S(2)}, u32[]{:S(2)}) %collective-permute-start.2) | collective-permute-done | bytes 69664 | tf_op jit(solution)/shard_map/ppermute | solution.py:200
  107.2 4.7 %collective-permute-done.1 = f32[136,128]{1,0:T(8,128)S(1)} collective-permute-done((f32[136,128]{1,0:T(8,128)S(1)}, f32[136,128]{1,0:T(8,128)S(1)}, u32[]{:S(2)}, u32[]{:S(2)}) %collective-permute-start.1) | collective-permute-done | bytes 69664 | tf_op jit(solution)/shard_map/ppermute | solution.py:200
  111.9 1.7 %collective-permute-done = f32[136,128]{1,0:T(8,128)S(1)} collective-permute-done((f32[136,128]{1,0:T(8,128)S(1)}, f32[136,128]{1,0:T(8,128)S(1)}, u32[]{:S(2)}, u32[]{:S(2)}) %collective-permute-start) | collective-permute-done | bytes 69664 | tf_op jit(solution)/shard_map/ppermute | solution.py:200
  113.6 0.4 convolution_bitcast_fusion
  114.0 1.0 fusion
  (8 shorter events, 0.1 us)
Async XLA Ops:
  29.6 8.9 %copy-start = (bf16[1,48,16384]{2,1,0:T(8,128)(2,1)S(1)}, bf16[1,48,16384]{2,1,0:T(8,128)(2,1)}, u32[]{:S(2)}) copy-start(bf16[1,48,16384]{2,1,0:T(8,128)(2,1)} %param.10) | copy-start | bytes 4718596
  29.6 37.4 %all-to-all-start = ((bf16[32,2,16512]{2,1,0:T(2,128)(2,1)}), bf16[32,2,16512]{2,1,0:T(2,128)(2,1)}, u32[]{:S(2)}, u32[]{:S(2)}) async-start(bf16[32,2,16512]{2,1,0:T(2,128)(2,1)} %scatter_fusion), calls=%async_computation | async-start | bytes 4227072 | tf_op jit(solution)/shard_map/all_to_all | solution.py:180
  39.5 30.4 %copy-start.2 = (f32[8,48]{1,0:T(8,128)S(1)}, f32[8,48]{1,0:T(8,128)}, u32[]{:S(2)}) copy-start(f32[8,48]{1,0:T(8,128)} %gain_ref.1) | copy-start | bytes 4612
  69.9 1.4 %copy-start.1 = (bf16[1,48,16384]{2,1,0:T(8,128)(2,1)S(1)}, bf16[1,48,16384]{2,1,0:T(8,128)(2,1)}, u32[]{:S(2)}) copy-start(bf16[1,48,16384]{2,1,0:T(8,128)(2,1)} %param.10) | copy-start | bytes 4718596
  81.1 22.0 %collective-permute-start.6 = (f32[136,128]{1,0:T(8,128)S(1)}, f32[136,128]{1,0:T(8,128)S(1)}, u32[]{:S(2)}, u32[]{:S(2)}) collective-permute-start(f32[136,128]{1,0:T(8,128)S(1)} %get-tuple-element.9), channel_id=1, source_target_pairs={{0,224},{32,0},{64,32},{96,64},{128,96},{160,128},{192,160},{224,1... | collective-permute-start | bytes 208904 | tf_op jit(solution)/shard_map/ppermute | solution.py:200
  86.7 17.7 %collective-permute-start.5 = (f32[136,128]{1,0:T(8,128)S(1)}, f32[136,128]{1,0:T(8,128)S(1)}, u32[]{:S(2)}, u32[]{:S(2)}) collective-permute-start(f32[136,128]{1,0:T(8,128)S(1)} %get-tuple-element.10), channel_id=1, source_target_pairs={{0,192},{32,224},{64,0},{96,32},{128,64},{160,96},{192,128},{224,1... | collective-permute-start | bytes 208904 | tf_op jit(solution)/shard_map/ppermute | solution.py:200
  89.7 11.9 %all-to-all-start.1 = ((f32[32,1,2]{2,1,0:T(1,128)}), f32[32,1,2]{2,1,0:T(1,128)S(1)}, u32[]{:S(2)}, u32[]{:S(2)}) async-start(f32[32,1,2]{2,1,0:T(1,128)} %bitcast.15), calls=%async_computation.1 | async-start | bytes 32768 | tf_op jit(solution)/shard_map/all_to_all | solution.py:189
  94.7 10.7 %collective-permute-start.4 = (f32[136,128]{1,0:T(8,128)S(1)}, f32[136,128]{1,0:T(8,128)S(1)}, u32[]{:S(2)}, u32[]{:S(2)}) collective-permute-start(f32[136,128]{1,0:T(8,128)S(1)} %get-tuple-element.11), channel_id=1, source_target_pairs={{0,160},{32,192},{64,224},{96,0},{128,32},{160,64},{192,96},{224,1... | collective-permute-start | bytes 208904 | tf_op jit(solution)/shard_map/ppermute | solution.py:200
  95.0 10.4 %collective-permute-start.3 = (f32[136,128]{1,0:T(8,128)S(1)}, f32[136,128]{1,0:T(8,128)S(1)}, u32[]{:S(2)}, u32[]{:S(2)}) collective-permute-start(f32[136,128]{1,0:T(8,128)S(1)} %get-tuple-element.12), channel_id=1, source_target_pairs={{0,128},{32,160},{64,192},{96,224},{128,0},{160,32},{192,64},{224,... | collective-permute-start | bytes 208904 | tf_op jit(solution)/shard_map/ppermute | solution.py:200
  99.8 7.4 %collective-permute-start.2 = (f32[136,128]{1,0:T(8,128)S(1)}, f32[136,128]{1,0:T(8,128)S(1)}, u32[]{:S(2)}, u32[]{:S(2)}) collective-permute-start(f32[136,128]{1,0:T(8,128)S(1)} %get-tuple-element.13), channel_id=1, source_target_pairs={{0,96},{32,128},{64,160},{96,192},{128,224},{160,0},{192,32},{224,... | collective-permute-start | bytes 208904 | tf_op jit(solution)/shard_map/ppermute | solution.py:200
  103.1 8.7 %collective-permute-start.1 = (f32[136,128]{1,0:T(8,128)S(1)}, f32[136,128]{1,0:T(8,128)S(1)}, u32[]{:S(2)}, u32[]{:S(2)}) collective-permute-start(f32[136,128]{1,0:T(8,128)S(1)} %get-tuple-element.14), channel_id=1, source_target_pairs={{0,64},{32,96},{64,128},{96,160},{128,192},{160,224},{192,0},{224,... | collective-permute-start | bytes 208904 | tf_op jit(solution)/shard_map/ppermute | solution.py:200
  104.4 9.2 %collective-permute-start = (f32[136,128]{1,0:T(8,128)S(1)}, f32[136,128]{1,0:T(8,128)S(1)}, u32[]{:S(2)}, u32[]{:S(2)}) collective-permute-start(f32[136,128]{1,0:T(8,128)S(1)} %get-tuple-element.8), channel_id=1, source_target_pairs={{0,32},{32,64},{64,96},{96,128},{128,160},{160,192},{192,224},{224... | collective-permute-start | bytes 208904 | tf_op jit(solution)/shard_map/ppermute | solution.py:200

commit v13 on v11

--- a/solution.py
+++ b/solution.py
@@ -192,6 +192,7 @@
     returned = lax.all_to_all(stacked, "dev", split_axis=1, concat_axis=1, tiled=True).reshape(
         total_slots
     )
+    windows, returned = lax.optimization_barrier((windows, returned))
     particle_evidence = jnp.take(returned, slot_index)
     depth = insert_weights.shape[0]
     band = IMG // groups

time: 90.4 us -> 95.5 us (1.056)
  waiting for transfers between devices: 37.9 us -> 42 us
  starting transfers between devices: 27.5 us -> 28.5 us
    all_to_all x1, waiting for transfers between devices: 1.78 us -> 6.96 us  [on_device(): lax.all_to_all(stacked, 'dev', split_axis=1, concat_axis=1, tiled=True)]
    ppermute x7, starting transfers between devices: 13.9 us -> 15.4 us  [on_device(): mine = mine + lax.ppermute(part, 'grp', pairs)]
    ppermute x7, waiting for transfers between devices: 8.65 us -> 7.54 us  [on_device(): mine = mine + lax.ppermute(part, 'grp', pairs)]
  transfers between devices with their start and end apart: 9 -> 9, of which waited for: 5 -> 5; matrix products, arithmetic and copies ran while one was open for 5% -> 2% of each run, Pallas kernels for 0% -> 0%
where the time goes in v13:
time: 95.5 us; the launch traced here: 95.2 us
  waiting for transfers between devices  42 us (44%)
  starting transfers between devices  28.5 us (30%)
  Pallas kernels  9.79 us (10%)
  local copies, waits for them, and re-layouts  8.03 us (8%)
  matrix products  3.25 us (3%)
  other arithmetic  2.73 us (3%)
    all_to_all x1, waiting for transfers between devices, on_device(): lax.all_to_all(outgoing, 'dev', split_axis=1, concat_axis=1, tiled=True)  27.5 us
    ppermute x7, starting transfers between devices, on_device(): mine = mine + lax.ppermute(part, 'grp', pairs)  15.4 us
    pallas_call x1, Pallas kernels, class_pass(): pl.pallas_call(functools.partial(class_kernel, pix, groups), out_shape=(j...  9.79 us
    all_to_all x1, starting transfers between devices, on_device(): lax.all_to_all(outgoing, 'dev', split_axis=1, concat_axis=1, tiled=True)  8.77 us
    ppermute x7, waiting for transfers between devices, on_device(): mine = mine + lax.ppermute(part, 'grp', pairs)  7.54 us
    all_to_all x1, waiting for transfers between devices, on_device(): lax.all_to_all(stacked, 'dev', split_axis=1, concat_axis=1, tiled=True)  6.96 us
    all_to_all x1, starting transfers between devices, on_device(): lax.all_to_all(stacked, 'dev', split_axis=1, concat_axis=1, tiled=True)  4.35 us
    reshape x1, local copies, waits for them, and re-layouts, on_device(): outgoing = outgoing.reshape(slot_depth, sources, owned_classes * width)  2.95 us
  transfers between devices with their start and end apart: 9, of which 5 were waited for; matrix products, arithmetic and copies ran while one was open for 2% of the time, Pallas kernels for 0%

profile of v13, /device:TPU:1, one launch (start us, length us, event | category | flops | bytes accessed | tf_op | source)
XLA Modules:
  0.0 95.2 jit_solution(9186178552861789853)
XLA Ops:
  0.6 0.9 convert_reduce_fusion.1
  1.6 0.7 broadcast_in_dim.86
  2.3 1.9 %convolution_convert_fusion = bf16[64,16512]{1,0:T(8,128)(2,1)S(1)} fusion(bf16[32,128]{1,0:T(8,128)(2,1)S(1)} %broadcast_in_dim.86, bf16[32,16384]{1,0:T(8,128)(2,1)} %param.6, s32[32]{0:T(128)S(1)} %get-tuple-element.13), kind=kOutput, calls=%fused_computation.1 | convolution fusion | flops 70805504 | bytes 3170432 | tf_op jit(solution)/shard_map/dot_general | solution.py:181
  4.2 2.9 %copy.15 = bf16[2,32,16512]{2,0,1:T(2,128)(2,1)} copy(bf16[2,32,16512]{2,1,0:T(8,128)(2,1)S(1)} %bitcast.49) | data formatting | bytes 4227072 | tf_op jit(solution)/shard_map/reshape | solution.py:182
  7.1 0.0 copy-start
  7.1 8.8 %all-to-all-start = ((bf16[2,32,16512]{2,0,1:T(2,128)(2,1)}), bf16[2,32,16512]{2,0,1:T(2,128)(2,1)}, u32[]{:S(2)}, u32[]{:S(2)}) async-start(bf16[2,32,16512]{2,0,1:T(2,128)(2,1)} %copy.15), calls=%async_computation | async-start | bytes 4227072 | tf_op jit(solution)/shard_map/all_to_all | solution.py:183
  16.0 0.0 copy-done
  16.0 0.4 multiply_reduce_fusion
  16.4 0.1 copy.17.energy_ref
  16.5 0.1 mul.46
  16.6 0.1 mul.47
  16.7 0.1 add_select_fusion
  16.8 0.1 mul.44
  16.9 0.0 copy-start.1
  16.9 27.5 %all-to-all-done = bf16[2,32,16512]{2,0,1:T(2,128)(2,1)} async-done(((bf16[2,32,16512]{2,0,1:T(2,128)(2,1)}), bf16[2,32,16512]{2,0,1:T(2,128)(2,1)}, u32[]{:S(2)}, u32[]{:S(2)}) %all-to-all-start) | async-done | bytes 2113568 | tf_op jit(solution)/shard_map/all_to_all | solution.py:183
  44.5 1.8 %copy.16 = bf16[2,32,16512]{2,1,0:T(8,128)(2,1)S(1)} copy(bf16[2,32,16512]{2,0,1:T(2,128)(2,1)} %all-to-all-done) | data formatting | bytes 4227072 | tf_op jit(solution)/shard_map/all_to_all | solution.py:183
  46.3 0.1 convert_reduce_fusion
  46.4 0.0 copy-done.1
  46.4 9.8 %shard_map.77 = (f32[8,136,128]{2,1,0:T(8,128)S(1)}, f32[1,64]{1,0:T(1,128)S(1)}) custom-call(bf16[64,16512]{1,0:T(8,128)(2,1)S(1)} %bitcast.46, bf16[48,16384]{1,0:T(8,128)(2,1)S(1)} %bitcast.47, f32[1,64]{1,0:T(1,128)S(1)} %bitcast.48, f32[48,1]{1,0:T(8,128)S(1)} %copy.17.energy_ref, f32[8,48]{1,0:T(8,128)S(1)} %copy-done.1), custom_call_target="tpu_custom_call" | custom-call | flops 1207959552 | bytes 4210688 | tf_op jit(solution)/shard_map/pallas_call | solution.py:138
  56.2 0.5 broadcast.332
  56.7 0.7 reduce.5
  57.4 0.1 all_to_all.10
  57.4 0.7 copy.18
  58.1 4.4 %all-to-all-start.1 = ((f32[2,32,1]{0,2,1:T(1,128)}), f32[2,32,1]{0,2,1:T(1,128)S(1)}, u32[]{:S(2)}, u32[]{:S(2)}) async-start(f32[2,32,1]{0,2,1:T(1,128)} %copy.18), calls=%async_computation.1 | async-start | bytes 32768 | tf_op jit(solution)/shard_map/all_to_all | solution.py:192
  62.5 7.0 %all-to-all-done.1 = f32[2,32,1]{0,2,1:T(1,128)S(1)} async-done(((f32[2,32,1]{0,2,1:T(1,128)}), f32[2,32,1]{0,2,1:T(1,128)S(1)}, u32[]{:S(2)}, u32[]{:S(2)}) %all-to-all-start.1) | async-done | bytes 288 | tf_op jit(solution)/shard_map/all_to_all | solution.py:192
  69.5 0.1 copy.19
  69.5 0.1 reshape.276
  69.7 5.7 %collective-permute-start.6 = (f32[136,128]{1,0:T(8,128)S(1)}, f32[136,128]{1,0:T(8,128)S(1)}, u32[]{:S(2)}, u32[]{:S(2)}) collective-permute-start(f32[136,128]{1,0:T(8,128)S(1)} %get-tuple-element.15), channel_id=1, source_target_pairs={{0,224},{32,0},{64,32},{96,64},{128,96},{160,128},{192,160},{224,1... | collective-permute-start | bytes 208904 | tf_op jit(solution)/shard_map/ppermute | solution.py:204
  75.3 1.2 %collective-permute-start.5 = (f32[136,128]{1,0:T(8,128)S(1)}, f32[136,128]{1,0:T(8,128)S(1)}, u32[]{:S(2)}, u32[]{:S(2)}) collective-permute-start(f32[136,128]{1,0:T(8,128)S(1)} %get-tuple-element.16), channel_id=1, source_target_pairs={{0,192},{32,224},{64,0},{96,32},{128,64},{160,96},{192,128},{224,1... | collective-permute-start | bytes 208904 | tf_op jit(solution)/shard_map/ppermute | solution.py:204
  76.5 0.7 collective-permute-start.4
  77.2 4.2 %collective-permute-start.3 = (f32[136,128]{1,0:T(8,128)S(1)}, f32[136,128]{1,0:T(8,128)S(1)}, u32[]{:S(2)}, u32[]{:S(2)}) collective-permute-start(f32[136,128]{1,0:T(8,128)S(1)} %get-tuple-element.18), channel_id=1, source_target_pairs={{0,128},{32,160},{64,192},{96,224},{128,0},{160,32},{192,64},{224,... | collective-permute-start | bytes 208904 | tf_op jit(solution)/shard_map/ppermute | solution.py:204
  81.4 0.0 collective-permute-start.2
  81.4 0.7 gather_fusion
  82.1 0.0 collective-permute-done.6
  82.1 2.2 %collective-permute-start.1 = (f32[136,128]{1,0:T(8,128)S(1)}, f32[136,128]{1,0:T(8,128)S(1)}, u32[]{:S(2)}, u32[]{:S(2)}) collective-permute-start(f32[136,128]{1,0:T(8,128)S(1)} %get-tuple-element.20), channel_id=1, source_target_pairs={{0,64},{32,96},{64,128},{96,160},{128,192},{160,224},{192,0},{224,... | collective-permute-start | bytes 208904 | tf_op jit(solution)/shard_map/ppermute | solution.py:204
  84.4 0.0 collective-permute-done.5
  84.4 1.4 %collective-permute-start = (f32[136,128]{1,0:T(8,128)S(1)}, f32[136,128]{1,0:T(8,128)S(1)}, u32[]{:S(2)}, u32[]{:S(2)}) collective-permute-start(f32[136,128]{1,0:T(8,128)S(1)} %get-tuple-element.14), channel_id=1, source_target_pairs={{0,32},{32,64},{64,96},{96,128},{128,160},{160,192},{192,224},{224... | collective-permute-start | bytes 208904 | tf_op jit(solution)/shard_map/ppermute | solution.py:204
  85.8 0.5 and_select_fusion
  86.3 0.0 collective-permute-done.4
  86.3 0.0 collective-permute-done.3
  86.3 1.7 %collective-permute-done.2 = f32[136,128]{1,0:T(8,128)S(1)} collective-permute-done((f32[136,128]{1,0:T(8,128)S(1)}, f32[136,128]{1,0:T(8,128)S(1)}, u32[]{:S(2)}, u32[]{:S(2)}) %collective-permute-start.2) | collective-permute-done | bytes 69664 | tf_op jit(solution)/shard_map/ppermute | solution.py:204
  88.0 5.5 %collective-permute-done.1 = f32[136,128]{1,0:T(8,128)S(1)} collective-permute-done((f32[136,128]{1,0:T(8,128)S(1)}, f32[136,128]{1,0:T(8,128)S(1)}, u32[]{:S(2)}, u32[]{:S(2)}) %collective-permute-start.1) | collective-permute-done | bytes 69664 | tf_op jit(solution)/shard_map/ppermute | solution.py:204
  93.5 0.4 collective-permute-done
  93.8 0.4 convolution_bitcast_fusion
  94.2 1.0 %fusion.3 = f32[32,8,256]{2,1,0:T(8,128)} fusion(f32[136,256,1]{1,0,2:T(8,128)S(1)} %convolution_bitcast_fusion, f32[8,136]{1,0:T(8,128)S(1)} %mul.47, f32[32,136]{1,0:T(8,128)S(1)} %mul.44), kind=kOutput, calls=%fused_computation.7 | convolution fusion | flops 53512192 | bytes 423168 | tf_op jit(solution)/shard_map/dot_general | solution.py:212
  (9 shorter events, 0.1 us)
Async XLA Ops:
  7.1 8.8 %copy-start = (bf16[1,48,16384]{2,1,0:T(8,128)(2,1)S(1)}, bf16[1,48,16384]{2,1,0:T(8,128)(2,1)}, u32[]{:S(2)}) copy-start(bf16[1,48,16384]{2,1,0:T(8,128)(2,1)} %param.10) | copy-start | bytes 4718596
  7.1 37.3 %all-to-all-start = ((bf16[2,32,16512]{2,0,1:T(2,128)(2,1)}), bf16[2,32,16512]{2,0,1:T(2,128)(2,1)}, u32[]{:S(2)}, u32[]{:S(2)}) async-start(bf16[2,32,16512]{2,0,1:T(2,128)(2,1)} %copy.15), calls=%async_computation | async-start | bytes 4227072 | tf_op jit(solution)/shard_map/all_to_all | solution.py:183
  16.9 29.5 %copy-start.1 = (f32[8,48]{1,0:T(8,128)S(1)}, f32[8,48]{1,0:T(8,128)}, u32[]{:S(2)}) copy-start(f32[8,48]{1,0:T(8,128)} %gain_ref.1) | copy-start | bytes 4612
  58.1 11.3 %all-to-all-start.1 = ((f32[2,32,1]{0,2,1:T(1,128)}), f32[2,32,1]{0,2,1:T(1,128)S(1)}, u32[]{:S(2)}, u32[]{:S(2)}) async-start(f32[2,32,1]{0,2,1:T(1,128)} %copy.18), calls=%async_computation.1 | async-start | bytes 32768 | tf_op jit(solution)/shard_map/all_to_all | solution.py:192
  69.7 12.5 %collective-permute-start.6 = (f32[136,128]{1,0:T(8,128)S(1)}, f32[136,128]{1,0:T(8,128)S(1)}, u32[]{:S(2)}, u32[]{:S(2)}) collective-permute-start(f32[136,128]{1,0:T(8,128)S(1)} %get-tuple-element.15), channel_id=1, source_target_pairs={{0,224},{32,0},{64,32},{96,64},{128,96},{160,128},{192,160},{224,1... | collective-permute-start | bytes 208904 | tf_op jit(solution)/shard_map/ppermute | solution.py:204
  75.3 9.1 %collective-permute-start.5 = (f32[136,128]{1,0:T(8,128)S(1)}, f32[136,128]{1,0:T(8,128)S(1)}, u32[]{:S(2)}, u32[]{:S(2)}) collective-permute-start(f32[136,128]{1,0:T(8,128)S(1)} %get-tuple-element.16), channel_id=1, source_target_pairs={{0,192},{32,224},{64,0},{96,32},{128,64},{160,96},{192,128},{224,1... | collective-permute-start | bytes 208904 | tf_op jit(solution)/shard_map/ppermute | solution.py:204
  76.5 9.8 %collective-permute-start.4 = (f32[136,128]{1,0:T(8,128)S(1)}, f32[136,128]{1,0:T(8,128)S(1)}, u32[]{:S(2)}, u32[]{:S(2)}) collective-permute-start(f32[136,128]{1,0:T(8,128)S(1)} %get-tuple-element.17), channel_id=1, source_target_pairs={{0,160},{32,192},{64,224},{96,0},{128,32},{160,64},{192,96},{224,1... | collective-permute-start | bytes 208904 | tf_op jit(solution)/shard_map/ppermute | solution.py:204
  77.2 9.1 %collective-permute-start.3 = (f32[136,128]{1,0:T(8,128)S(1)}, f32[136,128]{1,0:T(8,128)S(1)}, u32[]{:S(2)}, u32[]{:S(2)}) collective-permute-start(f32[136,128]{1,0:T(8,128)S(1)} %get-tuple-element.18), channel_id=1, source_target_pairs={{0,128},{32,160},{64,192},{96,224},{128,0},{160,32},{192,64},{224,... | collective-permute-start | bytes 208904 | tf_op jit(solution)/shard_map/ppermute | solution.py:204
  81.4 6.5 %collective-permute-start.2 = (f32[136,128]{1,0:T(8,128)S(1)}, f32[136,128]{1,0:T(8,128)S(1)}, u32[]{:S(2)}, u32[]{:S(2)}) collective-permute-start(f32[136,128]{1,0:T(8,128)S(1)} %get-tuple-element.19), channel_id=1, source_target_pairs={{0,96},{32,128},{64,160},{96,192},{128,224},{160,0},{192,32},{224,... | collective-permute-start | bytes 208904 | tf_op jit(solution)/shard_map/ppermute | solution.py:204
  82.1 11.3 %collective-permute-start.1 = (f32[136,128]{1,0:T(8,128)S(1)}, f32[136,128]{1,0:T(8,128)S(1)}, u32[]{:S(2)}, u32[]{:S(2)}) collective-permute-start(f32[136,128]{1,0:T(8,128)S(1)} %get-tuple-element.20), channel_id=1, source_target_pairs={{0,64},{32,96},{64,128},{96,160},{128,192},{160,224},{192,0},{224,... | collective-permute-start | bytes 208904 | tf_op jit(solution)/shard_map/ppermute | solution.py:204
  84.4 9.4 %collective-permute-start = (f32[136,128]{1,0:T(8,128)S(1)}, f32[136,128]{1,0:T(8,128)S(1)}, u32[]{:S(2)}, u32[]{:S(2)}) collective-permute-start(f32[136,128]{1,0:T(8,128)S(1)} %get-tuple-element.14), channel_id=1, source_target_pairs={{0,32},{32,64},{64,96},{96,128},{128,160},{160,192},{192,224},{224... | collective-permute-start | bytes 208904 | tf_op jit(solution)/shard_map/ppermute | solution.py:204

commit v14 on v11

--- a/solution.py
+++ b/solution.py
@@ -164,9 +164,7 @@
     slot_depth = max(2, 2 * local_count // classes)
     labels = particle_class[:, 0]
     catalog = jnp.arange(classes, dtype=jnp.int32)
-    position = jnp.sum(
-        jnp.where(labels[:, None] == catalog[None, :], class_owner[None, :], 0), axis=1
-    )
+    position = jnp.take(class_owner, labels, mode="clip")
     ordinal = jnp.arange(local_count, dtype=jnp.int32)
     earlier = (labels[:, None] == labels[None, :]) & (ordinal[None, :] < ordinal[:, None])
     arrival = jnp.sum(earlier, axis=1)
@@ -175,7 +173,7 @@
     placing = (jnp.arange(total_slots, dtype=jnp.int32)[:, None] == slot_index[None, :]).astype(
         jnp.bfloat16
     )
-    extra = jnp.broadcast_to(particle_precision[:, None], (local_count, IMG))
+    extra = jnp.pad(particle_precision[:, None], ((0, 0), (0, IMG - 1)))
     carried = jnp.concatenate([particles, extra], axis=1)
     width = pix + IMG
     outgoing = jnp.dot(placing, carried, preferred_element_type=jnp.float32).astype(jnp.bfloat16)

time: 90.4 us -> 91.9 us (1.017)
  transfers between devices with their start and end apart: 9 -> 9, of which waited for: 5 -> 5; matrix products, arithmetic and copies ran while one was open for 5% -> 4% of each run, Pallas kernels for 0% -> 0%
where the time goes in v14:
time: 91.9 us; the launch traced here: 91.5 us
  waiting for transfers between devices  37.9 us (41%)
  starting transfers between devices  27.5 us (30%)
  Pallas kernels  9.8 us (11%)
  local copies, waits for them, and re-layouts  8.78 us (10%)
  other arithmetic  3.39 us (4%)
  matrix products  3.25 us (4%)
    all_to_all x1, waiting for transfers between devices, on_device(): lax.all_to_all(outgoing, 'dev', split_axis=1, concat_axis=1, tiled=True)  27.5 us
    ppermute x7, starting transfers between devices, on_device(): mine = mine + lax.ppermute(part, 'grp', pairs)  13.8 us
    pallas_call x1, Pallas kernels, class_pass(): pl.pallas_call(functools.partial(class_kernel, pix, groups), out_shape=(j...  9.8 us
    all_to_all x1, starting transfers between devices, on_device(): lax.all_to_all(outgoing, 'dev', split_axis=1, concat_axis=1, tiled=True)  8.77 us
    ppermute x7, waiting for transfers between devices, on_device(): mine = mine + lax.ppermute(part, 'grp', pairs)  8.63 us
    all_to_all x1, starting transfers between devices, on_device(): lax.all_to_all(stacked, 'dev', split_axis=1, concat_axis=1, tiled=True)  4.91 us
    reshape x1, local copies, waits for them, and re-layouts, on_device(): outgoing = outgoing.reshape(slot_depth, sources, owned_classes * width)  2.95 us
    dot_general x1, matrix products, on_device(): jnp.dot(placing, carried, preferred_element_type=jnp.float32)  1.91 us
  transfers between devices with their start and end apart: 9, of which 5 were waited for; matrix products, arithmetic and copies ran while one was open for 4% of the time, Pallas kernels for 0%

profile of v14, /device:TPU:1, one launch (start us, length us, event | category | flops | bytes accessed | tf_op | source)
XLA Modules:
  0.0 91.5 jit_solution(5943874680763808025)
XLA Ops:
  0.6 0.0 copy-start
  0.6 0.7 pad_clamp_fusion.1
  1.3 0.9 convert_reduce_fusion.1
  2.2 0.8 copy.24
  3.0 0.0 copy-done
  3.0 0.7 gather_fusion
  3.7 1.9 %convolution_convert_fusion = bf16[64,16512]{1,0:T(8,128)(2,1)S(1)} fusion(bf16[32,1]{1,0:T(8,128)(2,1)S(1)} %copy.24, bf16[32,16384]{1,0:T(8,128)(2,1)} %param.6, s32[32]{0:T(128)S(1)} %get-tuple-element.7), kind=kOutput, calls=%fused_computation.2 | convolution fusion | flops 71862272 | bytes 3162304 | tf_op jit(solution)/shard_map/dot_general | solution.py:179
  5.6 3.0 %copy.19 = bf16[2,32,16512]{2,0,1:T(2,128)(2,1)} copy(bf16[2,32,16512]{2,1,0:T(8,128)(2,1)S(1)} %bitcast.50) | data formatting | bytes 4227072 | tf_op jit(solution)/shard_map/reshape | solution.py:180
  8.6 8.8 %all-to-all-start = ((bf16[2,32,16512]{2,0,1:T(2,128)(2,1)}), bf16[2,32,16512]{2,0,1:T(2,128)(2,1)}, u32[]{:S(2)}, u32[]{:S(2)}) async-start(bf16[2,32,16512]{2,0,1:T(2,128)(2,1)} %copy.19), calls=%async_computation | async-start | bytes 4227072 | tf_op jit(solution)/shard_map/all_to_all | solution.py:181
  17.4 0.0 copy-done.1
  17.4 0.4 multiply_reduce_fusion
  17.8 0.1 copy.21.energy_ref
  17.9 0.1 mul.46
  18.0 0.1 mul.47
  18.1 0.1 add_select_fusion
  18.2 0.1 mul.44
  18.4 0.0 copy-start.2
  18.4 27.5 %all-to-all-done = bf16[2,32,16512]{2,0,1:T(2,128)(2,1)} async-done(((bf16[2,32,16512]{2,0,1:T(2,128)(2,1)}), bf16[2,32,16512]{2,0,1:T(2,128)(2,1)}, u32[]{:S(2)}, u32[]{:S(2)}) %all-to-all-start) | async-done | bytes 2113568 | tf_op jit(solution)/shard_map/all_to_all | solution.py:181
  45.9 1.8 %copy.20 = bf16[2,32,16512]{2,1,0:T(8,128)(2,1)S(1)} copy(bf16[2,32,16512]{2,0,1:T(2,128)(2,1)} %all-to-all-done) | data formatting | bytes 4227072 | tf_op jit(solution)/shard_map/all_to_all | solution.py:181
  47.7 0.1 convert_reduce_fusion
  47.8 9.8 %shard_map.77 = (f32[8,136,128]{2,1,0:T(8,128)S(1)}, f32[1,64]{1,0:T(1,128)S(1)}) custom-call(bf16[64,16512]{1,0:T(8,128)(2,1)S(1)} %bitcast.47, bf16[48,16384]{1,0:T(8,128)(2,1)S(1)} %bitcast.48, f32[1,64]{1,0:T(1,128)S(1)} %bitcast.49, f32[48,1]{1,0:T(8,128)S(1)} %copy.21.energy_ref, f32[8,48]{1,0:T(8,128)S(1)} %copy-done.2), custom_call_target="tpu_custom_call" | custom-call | flops 1207959552 | bytes 4210688 | tf_op jit(solution)/shard_map/pallas_call | solution.py:138
  57.6 0.1 dynamic-slice_bitcast_fusion.6
  57.7 5.7 %collective-permute-start.6 = (f32[136,128]{1,0:T(8,128)S(1)}, f32[136,128]{1,0:T(8,128)S(1)}, u32[]{:S(2)}, u32[]{:S(2)}) collective-permute-start(f32[136,128]{1,0:T(8,128)S(1)} %get-tuple-element.9), channel_id=1, source_target_pairs={{0,224},{32,0},{64,32},{96,64},{128,96},{160,128},{192,160},{224,1... | collective-permute-start | bytes 208904 | tf_op jit(solution)/shard_map/ppermute | solution.py:201
  63.3 1.2 %collective-permute-start.5 = (f32[136,128]{1,0:T(8,128)S(1)}, f32[136,128]{1,0:T(8,128)S(1)}, u32[]{:S(2)}, u32[]{:S(2)}) collective-permute-start(f32[136,128]{1,0:T(8,128)S(1)} %get-tuple-element.10), channel_id=1, source_target_pairs={{0,192},{32,224},{64,0},{96,32},{128,64},{160,96},{192,128},{224,1... | collective-permute-start | bytes 208904 | tf_op jit(solution)/shard_map/ppermute | solution.py:201
  64.5 0.5 broadcast.346
  65.0 0.7 reduce.5
  65.7 0.1 all_to_all.10
  65.7 0.7 copy.22
  66.4 4.9 %all-to-all-start.1 = ((f32[2,32,1]{0,2,1:T(1,128)}), f32[2,32,1]{0,2,1:T(1,128)S(1)}, u32[]{:S(2)}, u32[]{:S(2)}) async-start(f32[2,32,1]{0,2,1:T(1,128)} %copy.22), calls=%async_computation.1 | async-start | bytes 32768 | tf_op jit(solution)/shard_map/all_to_all | solution.py:190
  71.4 0.4 collective-permute-start.4
  71.8 4.8 %collective-permute-start.3 = (f32[136,128]{1,0:T(8,128)S(1)}, f32[136,128]{1,0:T(8,128)S(1)}, u32[]{:S(2)}, u32[]{:S(2)}) collective-permute-start(f32[136,128]{1,0:T(8,128)S(1)} %get-tuple-element.12), channel_id=1, source_target_pairs={{0,128},{32,160},{64,192},{96,224},{128,0},{160,32},{192,64},{224,... | collective-permute-start | bytes 208904 | tf_op jit(solution)/shard_map/ppermute | solution.py:201
  76.6 0.0 collective-permute-start.2
  76.6 1.8 %all-to-all-done.1 = f32[2,32,1]{0,2,1:T(1,128)S(1)} async-done(((f32[2,32,1]{0,2,1:T(1,128)}), f32[2,32,1]{0,2,1:T(1,128)S(1)}, u32[]{:S(2)}, u32[]{:S(2)}) %all-to-all-start.1) | async-done | bytes 288 | tf_op jit(solution)/shard_map/all_to_all | solution.py:190
  78.3 0.1 copy.23
  78.4 0.1 reshape.274
  78.5 0.7 gather_fusion.1
  79.2 0.0 collective-permute-done.6
  79.2 1.3 %collective-permute-start.1 = (f32[136,128]{1,0:T(8,128)S(1)}, f32[136,128]{1,0:T(8,128)S(1)}, u32[]{:S(2)}, u32[]{:S(2)}) collective-permute-start(f32[136,128]{1,0:T(8,128)S(1)} %get-tuple-element.14), channel_id=1, source_target_pairs={{0,64},{32,96},{64,128},{96,160},{128,192},{160,224},{192,0},{224,... | collective-permute-start | bytes 208904 | tf_op jit(solution)/shard_map/ppermute | solution.py:201
  80.5 0.0 collective-permute-done.5
  80.5 0.6 collective-permute-start
  81.0 0.5 and_select_fusion
  81.6 0.0 collective-permute-done.4
  81.6 0.0 collective-permute-done.3
  81.6 2.0 %collective-permute-done.2 = f32[136,128]{1,0:T(8,128)S(1)} collective-permute-done((f32[136,128]{1,0:T(8,128)S(1)}, f32[136,128]{1,0:T(8,128)S(1)}, u32[]{:S(2)}, u32[]{:S(2)}) %collective-permute-start.2) | collective-permute-done | bytes 69664 | tf_op jit(solution)/shard_map/ppermute | solution.py:201
  83.5 4.9 %collective-permute-done.1 = f32[136,128]{1,0:T(8,128)S(1)} collective-permute-done((f32[136,128]{1,0:T(8,128)S(1)}, f32[136,128]{1,0:T(8,128)S(1)}, u32[]{:S(2)}, u32[]{:S(2)}) %collective-permute-start.1) | collective-permute-done | bytes 69664 | tf_op jit(solution)/shard_map/ppermute | solution.py:201
  88.4 1.7 %collective-permute-done = f32[136,128]{1,0:T(8,128)S(1)} collective-permute-done((f32[136,128]{1,0:T(8,128)S(1)}, f32[136,128]{1,0:T(8,128)S(1)}, u32[]{:S(2)}, u32[]{:S(2)}) %collective-permute-start) | collective-permute-done | bytes 69664 | tf_op jit(solution)/shard_map/ppermute | solution.py:201
  90.2 0.4 convolution_bitcast_fusion
  90.6 1.0 %fusion.7 = f32[32,8,256]{2,1,0:T(8,128)} fusion(f32[136,256,1]{1,0,2:T(8,128)S(1)} %convolution_bitcast_fusion, f32[8,136]{1,0:T(8,128)S(1)} %mul.47, f32[32,136]{1,0:T(8,128)S(1)} %mul.44), kind=kOutput, calls=%fused_computation.12 | convolution fusion | flops 53512192 | bytes 423168 | tf_op jit(solution)/shard_map/dot_general | solution.py:209
  (10 shorter events, 0.1 us)
Async XLA Ops:
  0.6 2.3 %copy-start = (s32[32]{0:T(128)S(1)}, s32[32]{0:T(128)}, u32[]{:S(2)}) copy-start(s32[32]{0:T(128)} %param.9) | copy-start | bytes 388
  8.6 8.8 %copy-start.1 = (bf16[1,48,16384]{2,1,0:T(8,128)(2,1)S(1)}, bf16[1,48,16384]{2,1,0:T(8,128)(2,1)}, u32[]{:S(2)}) copy-start(bf16[1,48,16384]{2,1,0:T(8,128)(2,1)} %param.10) | copy-start | bytes 4718596
  8.6 37.3 %all-to-all-start = ((bf16[2,32,16512]{2,0,1:T(2,128)(2,1)}), bf16[2,32,16512]{2,0,1:T(2,128)(2,1)}, u32[]{:S(2)}, u32[]{:S(2)}) async-start(bf16[2,32,16512]{2,0,1:T(2,128)(2,1)} %copy.19), calls=%async_computation | async-start | bytes 4227072 | tf_op jit(solution)/shard_map/all_to_all | solution.py:181
  18.4 29.4 %copy-start.2 = (f32[8,48]{1,0:T(8,128)S(1)}, f32[8,48]{1,0:T(8,128)}, u32[]{:S(2)}) copy-start(f32[8,48]{1,0:T(8,128)} %gain_ref.1) | copy-start | bytes 4612
  57.7 21.6 %collective-permute-start.6 = (f32[136,128]{1,0:T(8,128)S(1)}, f32[136,128]{1,0:T(8,128)S(1)}, u32[]{:S(2)}, u32[]{:S(2)}) collective-permute-start(f32[136,128]{1,0:T(8,128)S(1)} %get-tuple-element.9), channel_id=1, source_target_pairs={{0,224},{32,0},{64,32},{96,64},{128,96},{160,128},{192,160},{224,1... | collective-permute-start | bytes 208904 | tf_op jit(solution)/shard_map/ppermute | solution.py:201
  63.3 17.2 %collective-permute-start.5 = (f32[136,128]{1,0:T(8,128)S(1)}, f32[136,128]{1,0:T(8,128)S(1)}, u32[]{:S(2)}, u32[]{:S(2)}) collective-permute-start(f32[136,128]{1,0:T(8,128)S(1)} %get-tuple-element.10), channel_id=1, source_target_pairs={{0,192},{32,224},{64,0},{96,32},{128,64},{160,96},{192,128},{224,1... | collective-permute-start | bytes 208904 | tf_op jit(solution)/shard_map/ppermute | solution.py:201
  66.4 11.9 %all-to-all-start.1 = ((f32[2,32,1]{0,2,1:T(1,128)}), f32[2,32,1]{0,2,1:T(1,128)S(1)}, u32[]{:S(2)}, u32[]{:S(2)}) async-start(f32[2,32,1]{0,2,1:T(1,128)} %copy.22), calls=%async_computation.1 | async-start | bytes 32768 | tf_op jit(solution)/shard_map/all_to_all | solution.py:190
  71.4 10.2 %collective-permute-start.4 = (f32[136,128]{1,0:T(8,128)S(1)}, f32[136,128]{1,0:T(8,128)S(1)}, u32[]{:S(2)}, u32[]{:S(2)}) collective-permute-start(f32[136,128]{1,0:T(8,128)S(1)} %get-tuple-element.11), channel_id=1, source_target_pairs={{0,160},{32,192},{64,224},{96,0},{128,32},{160,64},{192,96},{224,1... | collective-permute-start | bytes 208904 | tf_op jit(solution)/shard_map/ppermute | solution.py:201
  71.8 9.8 %collective-permute-start.3 = (f32[136,128]{1,0:T(8,128)S(1)}, f32[136,128]{1,0:T(8,128)S(1)}, u32[]{:S(2)}, u32[]{:S(2)}) collective-permute-start(f32[136,128]{1,0:T(8,128)S(1)} %get-tuple-element.12), channel_id=1, source_target_pairs={{0,128},{32,160},{64,192},{96,224},{128,0},{160,32},{192,64},{224,... | collective-permute-start | bytes 208904 | tf_op jit(solution)/shard_map/ppermute | solution.py:201
  76.6 7.0 %collective-permute-start.2 = (f32[136,128]{1,0:T(8,128)S(1)}, f32[136,128]{1,0:T(8,128)S(1)}, u32[]{:S(2)}, u32[]{:S(2)}) collective-permute-start(f32[136,128]{1,0:T(8,128)S(1)} %get-tuple-element.13), channel_id=1, source_target_pairs={{0,96},{32,128},{64,160},{96,192},{128,224},{160,0},{192,32},{224,... | collective-permute-start | bytes 208904 | tf_op jit(solution)/shard_map/ppermute | solution.py:201
  79.2 9.2 %collective-permute-start.1 = (f32[136,128]{1,0:T(8,128)S(1)}, f32[136,128]{1,0:T(8,128)S(1)}, u32[]{:S(2)}, u32[]{:S(2)}) collective-permute-start(f32[136,128]{1,0:T(8,128)S(1)} %get-tuple-element.14), channel_id=1, source_target_pairs={{0,64},{32,96},{64,128},{96,160},{128,192},{160,224},{192,0},{224,... | collective-permute-start | bytes 208904 | tf_op jit(solution)/shard_map/ppermute | solution.py:201
  80.5 9.7 %collective-permute-start = (f32[136,128]{1,0:T(8,128)S(1)}, f32[136,128]{1,0:T(8,128)S(1)}, u32[]{:S(2)}, u32[]{:S(2)}) collective-permute-start(f32[136,128]{1,0:T(8,128)S(1)} %get-tuple-element.8), channel_id=1, source_target_pairs={{0,32},{32,64},{64,96},{96,128},{128,160},{160,192},{192,224},{224... | collective-permute-start | bytes 208904 | tf_op jit(solution)/shard_map/ppermute | solution.py:201

commit v15 on v11

--- a/solution.py
+++ b/solution.py
@@ -115,9 +115,8 @@
             plane = both[:, half * band:(half + 1) * band]
             before = lax.rem(j + groups - 1, groups)
             for z in range(depth):
-                for u in range(width):
-                    row = z * (width + 1) + u
-                    planes_ref[j, pl.ds(row, 1), :] = plane[z:z + 1, u * IMG:(u + 1) * IMG]
+                row = z * (width + 1)
+                planes_ref[j, pl.ds(row, width), :] = plane[z:z + 1, :].reshape(width, IMG)
                 row = z * (width + 1) + width
                 planes_ref[before, pl.ds(row, 1), :] = plane[z:z + 1, 0:IMG]
         return carry

time: 90.4 us -> 90.4 us (level)
  no operation moved by 1% of the time
where the time goes in v15:
time: 90.4 us; the launch traced here: 90.1 us
  waiting for transfers between devices  37.9 us (42%)
  starting transfers between devices  27.5 us (30%)
  Pallas kernels  9.78 us (11%)
  local copies, waits for them, and re-layouts  8.04 us (9%)
  matrix products  3.24 us (4%)
  other arithmetic  2.73 us (3%)
    all_to_all x1, waiting for transfers between devices, on_device(): lax.all_to_all(outgoing, 'dev', split_axis=1, concat_axis=1, tiled=True)  27.5 us
    ppermute x7, starting transfers between devices, on_device(): mine = mine + lax.ppermute(part, 'grp', pairs)  13.9 us
    pallas_call x1, Pallas kernels, class_pass(): pl.pallas_call(functools.partial(class_kernel, pix, groups), out_shape=(j...  9.78 us
    all_to_all x1, starting transfers between devices, on_device(): lax.all_to_all(outgoing, 'dev', split_axis=1, concat_axis=1, tiled=True)  8.77 us
    ppermute x7, waiting for transfers between devices, on_device(): mine = mine + lax.ppermute(part, 'grp', pairs)  8.63 us
    all_to_all x1, starting transfers between devices, on_device(): lax.all_to_all(stacked, 'dev', split_axis=1, concat_axis=1, tiled=True)  4.9 us
    reshape x1, local copies, waits for them, and re-layouts, on_device(): outgoing = outgoing.reshape(slot_depth, sources, owned_classes * width)  2.95 us
    dot_general x1, matrix products, on_device(): jnp.dot(placing, carried, preferred_element_type=jnp.float32)  1.91 us
  transfers between devices with their start and end apart: 9, of which 5 were waited for; matrix products, arithmetic and copies ran while one was open for 5% of the time, Pallas kernels for 0%

profile of v15, /device:TPU:1, one launch (start us, length us, event | category | flops | bytes accessed | tf_op | source)
XLA Modules:
  0.0 90.1 jit_solution(14049450087340374790)
XLA Ops:
  0.6 0.9 %convert_reduce_fusion.1 = (s32[32]{0:T(128)S(1)}, s32[32]{0:T(128)S(1)}) fusion(s32[32]{0:T(128)} %bitcast.51, s32[32]{0:T(128)} %param.9), kind=kLoop, calls=%fused_computation.44 | loop fusion | flops 8128 | bytes 512 | tf_op jit(solution)/shard_map/reduce_sum | solution.py:171
  1.6 0.7 broadcast_in_dim.86
  2.3 1.9 %convolution_convert_fusion = bf16[64,16512]{1,0:T(8,128)(2,1)S(1)} fusion(bf16[32,128]{1,0:T(8,128)(2,1)S(1)} %broadcast_in_dim.86, bf16[32,16384]{1,0:T(8,128)(2,1)} %param.6, s32[32]{0:T(128)S(1)} %get-tuple-element.9), kind=kOutput, calls=%fused_computation.1 | convolution fusion | flops 70805504 | bytes 3170432 | tf_op jit(solution)/shard_map/dot_general | solution.py:180
  4.2 2.9 %copy.15 = bf16[2,32,16512]{2,0,1:T(2,128)(2,1)} copy(bf16[2,32,16512]{2,1,0:T(8,128)(2,1)S(1)} %bitcast.49) | data formatting | bytes 4227072 | tf_op jit(solution)/shard_map/reshape | solution.py:181
  7.1 0.0 copy-start
  7.1 8.8 %all-to-all-start = ((bf16[2,32,16512]{2,0,1:T(2,128)(2,1)}), bf16[2,32,16512]{2,0,1:T(2,128)(2,1)}, u32[]{:S(2)}, u32[]{:S(2)}) async-start(bf16[2,32,16512]{2,0,1:T(2,128)(2,1)} %copy.15), calls=%async_computation | async-start | bytes 4227072 | tf_op jit(solution)/shard_map/all_to_all | solution.py:182
  16.0 0.0 copy-done
  16.0 0.4 multiply_reduce_fusion
  16.4 0.1 copy.17.energy_ref
  16.5 0.1 mul.46
  16.6 0.1 mul.47
  16.7 0.1 add_select_fusion
  16.8 0.1 mul.44
  16.9 0.0 copy-start.1
  16.9 27.5 %all-to-all-done = bf16[2,32,16512]{2,0,1:T(2,128)(2,1)} async-done(((bf16[2,32,16512]{2,0,1:T(2,128)(2,1)}), bf16[2,32,16512]{2,0,1:T(2,128)(2,1)}, u32[]{:S(2)}, u32[]{:S(2)}) %all-to-all-start) | async-done | bytes 2113568 | tf_op jit(solution)/shard_map/all_to_all | solution.py:182
  44.5 1.8 %copy.16 = bf16[2,32,16512]{2,1,0:T(8,128)(2,1)S(1)} copy(bf16[2,32,16512]{2,0,1:T(2,128)(2,1)} %all-to-all-done) | data formatting | bytes 4227072 | tf_op jit(solution)/shard_map/all_to_all | solution.py:182
  46.3 0.1 convert_reduce_fusion
  46.4 0.0 copy-done.1
  46.4 9.8 %shard_map.77 = (f32[8,136,128]{2,1,0:T(8,128)S(1)}, f32[1,64]{1,0:T(1,128)S(1)}) custom-call(bf16[64,16512]{1,0:T(8,128)(2,1)S(1)} %bitcast.46, bf16[48,16384]{1,0:T(8,128)(2,1)S(1)} %bitcast.47, f32[1,64]{1,0:T(1,128)S(1)} %bitcast.48, f32[48,1]{1,0:T(8,128)S(1)} %copy.17.energy_ref, f32[8,48]{1,0:T(8,128)S(1)} %copy-done.1), custom_call_target="tpu_custom_call" | custom-call | flops 1207959552 | bytes 4210688 | tf_op jit(solution)/shard_map/pallas_call | solution.py:137
  56.2 0.1 dynamic-slice_bitcast_fusion.6
  56.2 5.7 %collective-permute-start.6 = (f32[136,128]{1,0:T(8,128)S(1)}, f32[136,128]{1,0:T(8,128)S(1)}, u32[]{:S(2)}, u32[]{:S(2)}) collective-permute-start(f32[136,128]{1,0:T(8,128)S(1)} %get-tuple-element.11), channel_id=1, source_target_pairs={{0,224},{32,0},{64,32},{96,64},{128,96},{160,128},{192,160},{224,1... | collective-permute-start | bytes 208904 | tf_op jit(solution)/shard_map/ppermute | solution.py:202
  61.9 1.2 %collective-permute-start.5 = (f32[136,128]{1,0:T(8,128)S(1)}, f32[136,128]{1,0:T(8,128)S(1)}, u32[]{:S(2)}, u32[]{:S(2)}) collective-permute-start(f32[136,128]{1,0:T(8,128)S(1)} %get-tuple-element.12), channel_id=1, source_target_pairs={{0,192},{32,224},{64,0},{96,32},{128,64},{160,96},{192,128},{224,1... | collective-permute-start | bytes 208904 | tf_op jit(solution)/shard_map/ppermute | solution.py:202
  63.1 0.5 broadcast.332
  63.6 0.7 reduce.5
  64.2 0.1 all_to_all.10
  64.3 0.7 copy.18
  65.0 4.9 %all-to-all-start.1 = ((f32[2,32,1]{0,2,1:T(1,128)}), f32[2,32,1]{0,2,1:T(1,128)S(1)}, u32[]{:S(2)}, u32[]{:S(2)}) async-start(f32[2,32,1]{0,2,1:T(1,128)} %copy.18), calls=%async_computation.1 | async-start | bytes 32768 | tf_op jit(solution)/shard_map/all_to_all | solution.py:191
  69.9 0.4 collective-permute-start.4
  70.4 4.8 %collective-permute-start.3 = (f32[136,128]{1,0:T(8,128)S(1)}, f32[136,128]{1,0:T(8,128)S(1)}, u32[]{:S(2)}, u32[]{:S(2)}) collective-permute-start(f32[136,128]{1,0:T(8,128)S(1)} %get-tuple-element.14), channel_id=1, source_target_pairs={{0,128},{32,160},{64,192},{96,224},{128,0},{160,32},{192,64},{224,... | collective-permute-start | bytes 208904 | tf_op jit(solution)/shard_map/ppermute | solution.py:202
  75.1 0.0 collective-permute-start.2
  75.1 1.8 %all-to-all-done.1 = f32[2,32,1]{0,2,1:T(1,128)S(1)} async-done(((f32[2,32,1]{0,2,1:T(1,128)}), f32[2,32,1]{0,2,1:T(1,128)S(1)}, u32[]{:S(2)}, u32[]{:S(2)}) %all-to-all-start.1) | async-done | bytes 288 | tf_op jit(solution)/shard_map/all_to_all | solution.py:191
  76.9 0.1 copy.19
  77.0 0.1 reshape.276
  77.1 0.7 gather_fusion
  77.8 0.0 collective-permute-done.6
  77.8 1.3 %collective-permute-start.1 = (f32[136,128]{1,0:T(8,128)S(1)}, f32[136,128]{1,0:T(8,128)S(1)}, u32[]{:S(2)}, u32[]{:S(2)}) collective-permute-start(f32[136,128]{1,0:T(8,128)S(1)} %get-tuple-element.16), channel_id=1, source_target_pairs={{0,64},{32,96},{64,128},{96,160},{128,192},{160,224},{192,0},{224,... | collective-permute-start | bytes 208904 | tf_op jit(solution)/shard_map/ppermute | solution.py:202
  79.0 0.0 collective-permute-done.5
  79.0 0.6 collective-permute-start
  79.6 0.5 and_select_fusion
  80.1 0.0 collective-permute-done.4
  80.1 0.0 collective-permute-done.3
  80.1 2.0 %collective-permute-done.2 = f32[136,128]{1,0:T(8,128)S(1)} collective-permute-done((f32[136,128]{1,0:T(8,128)S(1)}, f32[136,128]{1,0:T(8,128)S(1)}, u32[]{:S(2)}, u32[]{:S(2)}) %collective-permute-start.2) | collective-permute-done | bytes 69664 | tf_op jit(solution)/shard_map/ppermute | solution.py:202
  82.1 4.9 %collective-permute-done.1 = f32[136,128]{1,0:T(8,128)S(1)} collective-permute-done((f32[136,128]{1,0:T(8,128)S(1)}, f32[136,128]{1,0:T(8,128)S(1)}, u32[]{:S(2)}, u32[]{:S(2)}) %collective-permute-start.1) | collective-permute-done | bytes 69664 | tf_op jit(solution)/shard_map/ppermute | solution.py:202
  87.0 1.7 %collective-permute-done = f32[136,128]{1,0:T(8,128)S(1)} collective-permute-done((f32[136,128]{1,0:T(8,128)S(1)}, f32[136,128]{1,0:T(8,128)S(1)}, u32[]{:S(2)}, u32[]{:S(2)}) %collective-permute-start) | collective-permute-done | bytes 69664 | tf_op jit(solution)/shard_map/ppermute | solution.py:202
  88.8 0.4 convolution_bitcast_fusion
  89.1 1.0 %fusion.3 = f32[32,8,256]{2,1,0:T(8,128)} fusion(f32[136,256,1]{1,0,2:T(8,128)S(1)} %convolution_bitcast_fusion, f32[8,136]{1,0:T(8,128)S(1)} %mul.47, f32[32,136]{1,0:T(8,128)S(1)} %mul.44), kind=kOutput, calls=%fused_computation.7 | convolution fusion | flops 53512192 | bytes 423168 | tf_op jit(solution)/shard_map/dot_general | solution.py:210
  (8 shorter events, 0.1 us)
Async XLA Ops:
  7.1 8.8 %copy-start = (bf16[1,48,16384]{2,1,0:T(8,128)(2,1)S(1)}, bf16[1,48,16384]{2,1,0:T(8,128)(2,1)}, u32[]{:S(2)}) copy-start(bf16[1,48,16384]{2,1,0:T(8,128)(2,1)} %param.10) | copy-start | bytes 4718596
  7.1 37.3 %all-to-all-start = ((bf16[2,32,16512]{2,0,1:T(2,128)(2,1)}), bf16[2,32,16512]{2,0,1:T(2,128)(2,1)}, u32[]{:S(2)}, u32[]{:S(2)}) async-start(bf16[2,32,16512]{2,0,1:T(2,128)(2,1)} %copy.15), calls=%async_computation | async-start | bytes 4227072 | tf_op jit(solution)/shard_map/all_to_all | solution.py:182
  16.9 29.4 %copy-start.1 = (f32[8,48]{1,0:T(8,128)S(1)}, f32[8,48]{1,0:T(8,128)}, u32[]{:S(2)}) copy-start(f32[8,48]{1,0:T(8,128)} %gain_ref.1) | copy-start | bytes 4612
  56.2 21.5 %collective-permute-start.6 = (f32[136,128]{1,0:T(8,128)S(1)}, f32[136,128]{1,0:T(8,128)S(1)}, u32[]{:S(2)}, u32[]{:S(2)}) collective-permute-start(f32[136,128]{1,0:T(8,128)S(1)} %get-tuple-element.11), channel_id=1, source_target_pairs={{0,224},{32,0},{64,32},{96,64},{128,96},{160,128},{192,160},{224,1... | collective-permute-start | bytes 208904 | tf_op jit(solution)/shard_map/ppermute | solution.py:202
  61.9 17.2 %collective-permute-start.5 = (f32[136,128]{1,0:T(8,128)S(1)}, f32[136,128]{1,0:T(8,128)S(1)}, u32[]{:S(2)}, u32[]{:S(2)}) collective-permute-start(f32[136,128]{1,0:T(8,128)S(1)} %get-tuple-element.12), channel_id=1, source_target_pairs={{0,192},{32,224},{64,0},{96,32},{128,64},{160,96},{192,128},{224,1... | collective-permute-start | bytes 208904 | tf_op jit(solution)/shard_map/ppermute | solution.py:202
  65.0 11.9 %all-to-all-start.1 = ((f32[2,32,1]{0,2,1:T(1,128)}), f32[2,32,1]{0,2,1:T(1,128)S(1)}, u32[]{:S(2)}, u32[]{:S(2)}) async-start(f32[2,32,1]{0,2,1:T(1,128)} %copy.18), calls=%async_computation.1 | async-start | bytes 32768 | tf_op jit(solution)/shard_map/all_to_all | solution.py:191
  69.9 10.2 %collective-permute-start.4 = (f32[136,128]{1,0:T(8,128)S(1)}, f32[136,128]{1,0:T(8,128)S(1)}, u32[]{:S(2)}, u32[]{:S(2)}) collective-permute-start(f32[136,128]{1,0:T(8,128)S(1)} %get-tuple-element.13), channel_id=1, source_target_pairs={{0,160},{32,192},{64,224},{96,0},{128,32},{160,64},{192,96},{224,1... | collective-permute-start | bytes 208904 | tf_op jit(solution)/shard_map/ppermute | solution.py:202
  70.4 9.8 %collective-permute-start.3 = (f32[136,128]{1,0:T(8,128)S(1)}, f32[136,128]{1,0:T(8,128)S(1)}, u32[]{:S(2)}, u32[]{:S(2)}) collective-permute-start(f32[136,128]{1,0:T(8,128)S(1)} %get-tuple-element.14), channel_id=1, source_target_pairs={{0,128},{32,160},{64,192},{96,224},{128,0},{160,32},{192,64},{224,... | collective-permute-start | bytes 208904 | tf_op jit(solution)/shard_map/ppermute | solution.py:202
  75.1 7.0 %collective-permute-start.2 = (f32[136,128]{1,0:T(8,128)S(1)}, f32[136,128]{1,0:T(8,128)S(1)}, u32[]{:S(2)}, u32[]{:S(2)}) collective-permute-start(f32[136,128]{1,0:T(8,128)S(1)} %get-tuple-element.15), channel_id=1, source_target_pairs={{0,96},{32,128},{64,160},{96,192},{128,224},{160,0},{192,32},{224,... | collective-permute-start | bytes 208904 | tf_op jit(solution)/shard_map/ppermute | solution.py:202
  77.8 9.2 %collective-permute-start.1 = (f32[136,128]{1,0:T(8,128)S(1)}, f32[136,128]{1,0:T(8,128)S(1)}, u32[]{:S(2)}, u32[]{:S(2)}) collective-permute-start(f32[136,128]{1,0:T(8,128)S(1)} %get-tuple-element.16), channel_id=1, source_target_pairs={{0,64},{32,96},{64,128},{96,160},{128,192},{160,224},{192,0},{224,... | collective-permute-start | bytes 208904 | tf_op jit(solution)/shard_map/ppermute | solution.py:202
  79.0 9.7 %collective-permute-start = (f32[136,128]{1,0:T(8,128)S(1)}, f32[136,128]{1,0:T(8,128)S(1)}, u32[]{:S(2)}, u32[]{:S(2)}) collective-permute-start(f32[136,128]{1,0:T(8,128)S(1)} %get-tuple-element.10), channel_id=1, source_target_pairs={{0,32},{32,64},{64,96},{96,128},{128,160},{160,192},{192,224},{224... | collective-permute-start | bytes 208904 | tf_op jit(solution)/shard_map/ppermute | solution.py:202

commit v16 on v11

--- a/solution.py
+++ b/solution.py
@@ -10,7 +10,6 @@
 IMG = 128
 VOL = 256
 SHIFTS = (-1, 0, 1)
-TK = 16384
 TN = 1024
 
 
@@ -56,21 +55,14 @@
     ext_ref[:, :, 0:IMG] = ext_ref[:, :, pix:pix + IMG]
     ext_ref[:, :, pix + IMG:pix + 2 * IMG] = ext_ref[:, :, IMG:2 * IMG]
 
-    acc_ref[...] = jnp.zeros_like(acc_ref)
-
-    def products(j, carry):
-        k0 = pl.multiple_of(j * TK, TK)
-        tile = ref_ref[:, pl.ds(k0, TK)]
-        for ai, a in enumerate(SHIFTS):
-            start = pl.multiple_of(k0 + IMG * (1 - a), IMG)
-            for bi in range(3):
-                moved = ext_ref[bi, :, pl.ds(start, TK)]
-                acc_ref[ai * 3 + bi] += lax.dot_general(
-                    tile, moved, (((1,), (1,)), ((), ())), preferred_element_type=jnp.float32
-                )
-        return carry
-
-    lax.fori_loop(0, pix // TK, products, 0)
+    tile = ref_ref[...]
+    for ai, a in enumerate(SHIFTS):
+        start = IMG * (1 - a)
+        for bi in range(3):
+            moved = ext_ref[bi, :, start:start + pix]
+            acc_ref[ai * 3 + bi] = lax.dot_general(
+                tile, moved, (((1,), (1,)), ((), ())), preferred_element_type=jnp.float32
+            )
 
     scale = scale_ref[...]
     half_energy = 0.5 * energy_ref[...]
@@ -78,17 +70,19 @@
     highest = jnp.max(scores[0], axis=0, keepdims=True)
     for t in range(1, 9):
         highest = jnp.maximum(highest, jnp.max(scores[t], axis=0, keepdims=True))
-    total = jnp.sum(jnp.exp(scores[0] - highest), axis=0, keepdims=True)
+    raised = [jnp.exp(scores[t] - highest) for t in range(9)]
+    total = jnp.sum(raised[0], axis=0, keepdims=True)
     for t in range(1, 9):
-        total = total + jnp.sum(jnp.exp(scores[t] - highest), axis=0, keepdims=True)
+        total = total + jnp.sum(raised[t], axis=0, keepdims=True)
     evidence = highest + jnp.log(total)
+    inverse = 1.0 / total
     evid_ref[...] = evidence
     gain = gain_ref[...]
     gain_hi = gain.astype(jnp.bfloat16)
     gain_lo = (gain - gain_hi.astype(jnp.float32)).astype(jnp.bfloat16)
     depth = gain.shape[0]
     for t in range(9):
-        weights = jnp.exp(scores[t] - evidence).astype(jnp.bfloat16)
+        weights = (raised[t] * inverse).astype(jnp.bfloat16)
         mixed = jnp.dot(gain_hi, weights, preferred_element_type=jnp.float32) + jnp.dot(
             gain_lo, weights, preferred_element_type=jnp.float32
         )

time: 90.4 us -> 90.4 us (level)
  no operation moved by 1% of the time
where the time goes in v16:
time: 90.4 us; the launch traced here: 90.1 us
  waiting for transfers between devices  38.2 us (42%)
  starting transfers between devices  27.2 us (30%)
  Pallas kernels  9.84 us (11%)
  local copies, waits for them, and re-layouts  8.04 us (9%)
  matrix products  3.24 us (4%)
  other arithmetic  2.73 us (3%)
    all_to_all x1, waiting for transfers between devices, on_device(): lax.all_to_all(outgoing, 'dev', split_axis=1, concat_axis=1, tiled=True)  27.5 us
    ppermute x7, starting transfers between devices, on_device(): mine = mine + lax.ppermute(part, 'grp', pairs)  13.5 us
    pallas_call x1, Pallas kernels, class_pass(): pl.pallas_call(functools.partial(class_kernel, pix, groups), out_shape=(j...  9.84 us
    all_to_all x1, starting transfers between devices, on_device(): lax.all_to_all(outgoing, 'dev', split_axis=1, concat_axis=1, tiled=True)  8.77 us
    ppermute x7, waiting for transfers between devices, on_device(): mine = mine + lax.ppermute(part, 'grp', pairs)  8.77 us
    all_to_all x1, starting transfers between devices, on_device(): lax.all_to_all(stacked, 'dev', split_axis=1, concat_axis=1, tiled=True)  4.91 us
    reshape x1, local copies, waits for them, and re-layouts, on_device(): outgoing = outgoing.reshape(slot_depth, sources, owned_classes * width)  2.95 us
    all_to_all x1, waiting for transfers between devices, on_device(): lax.all_to_all(stacked, 'dev', split_axis=1, concat_axis=1, tiled=True)  1.97 us
  transfers between devices with their start and end apart: 9, of which 5 were waited for; matrix products, arithmetic and copies ran while one was open for 5% of the time, Pallas kernels for 0%

profile of v16, /device:TPU:1, one launch (start us, length us, event | category | flops | bytes accessed | tf_op | source)
XLA Modules:
  0.0 90.1 jit_solution(11081526290878395848)
XLA Ops:
  0.6 0.9 %convert_reduce_fusion.1 = (s32[32]{0:T(128)S(1)}, s32[32]{0:T(128)S(1)}) fusion(s32[32]{0:T(128)} %bitcast.51, s32[32]{0:T(128)} %param.9), kind=kLoop, calls=%fused_computation.44 | loop fusion | flops 8128 | bytes 512 | tf_op jit(solution)/shard_map/reduce_sum | solution.py:166
  1.6 0.7 broadcast_in_dim.86
  2.3 1.9 %convolution_convert_fusion = bf16[64,16512]{1,0:T(8,128)(2,1)S(1)} fusion(bf16[32,128]{1,0:T(8,128)(2,1)S(1)} %broadcast_in_dim.86, bf16[32,16384]{1,0:T(8,128)(2,1)} %param.6, s32[32]{0:T(128)S(1)} %get-tuple-element.9), kind=kOutput, calls=%fused_computation.1 | convolution fusion | flops 70805504 | bytes 3170432 | tf_op jit(solution)/shard_map/dot_general | solution.py:175
  4.2 2.9 %copy.15 = bf16[2,32,16512]{2,0,1:T(2,128)(2,1)} copy(bf16[2,32,16512]{2,1,0:T(8,128)(2,1)S(1)} %bitcast.49) | data formatting | bytes 4227072 | tf_op jit(solution)/shard_map/reshape | solution.py:176
  7.1 0.0 copy-start
  7.1 8.8 %all-to-all-start = ((bf16[2,32,16512]{2,0,1:T(2,128)(2,1)}), bf16[2,32,16512]{2,0,1:T(2,128)(2,1)}, u32[]{:S(2)}, u32[]{:S(2)}) async-start(bf16[2,32,16512]{2,0,1:T(2,128)(2,1)} %copy.15), calls=%async_computation | async-start | bytes 4227072 | tf_op jit(solution)/shard_map/all_to_all | solution.py:177
  16.0 0.0 copy-done
  16.0 0.4 multiply_reduce_fusion
  16.4 0.1 copy.17.energy_ref
  16.5 0.1 mul.46
  16.6 0.1 mul.47
  16.7 0.1 add_select_fusion
  16.8 0.1 mul.44
  16.9 0.0 copy-start.1
  16.9 27.5 %all-to-all-done = bf16[2,32,16512]{2,0,1:T(2,128)(2,1)} async-done(((bf16[2,32,16512]{2,0,1:T(2,128)(2,1)}), bf16[2,32,16512]{2,0,1:T(2,128)(2,1)}, u32[]{:S(2)}, u32[]{:S(2)}) %all-to-all-start) | async-done | bytes 2113568 | tf_op jit(solution)/shard_map/all_to_all | solution.py:177
  44.5 1.8 %copy.16 = bf16[2,32,16512]{2,1,0:T(8,128)(2,1)S(1)} copy(bf16[2,32,16512]{2,0,1:T(2,128)(2,1)} %all-to-all-done) | data formatting | bytes 4227072 | tf_op jit(solution)/shard_map/all_to_all | solution.py:177
  46.3 0.1 convert_reduce_fusion
  46.4 0.0 copy-done.1
  46.4 9.8 %shard_map.77 = (f32[8,136,128]{2,1,0:T(8,128)S(1)}, f32[1,64]{1,0:T(1,128)S(1)}) custom-call(bf16[64,16512]{1,0:T(8,128)(2,1)S(1)} %bitcast.46, bf16[48,16384]{1,0:T(8,128)(2,1)S(1)} %bitcast.47, f32[1,64]{1,0:T(1,128)S(1)} %bitcast.48, f32[48,1]{1,0:T(8,128)S(1)} %copy.17.energy_ref, f32[8,48]{1,0:T(8,128)S(1)} %copy-done.1), custom_call_target="tpu_custom_call" | custom-call | flops 1207959552 | bytes 4210688 | tf_op jit(solution)/shard_map/pallas_call | solution.py:132
  56.2 0.1 dynamic-slice_bitcast_fusion.6
  56.3 5.6 %collective-permute-start.6 = (f32[136,128]{1,0:T(8,128)S(1)}, f32[136,128]{1,0:T(8,128)S(1)}, u32[]{:S(2)}, u32[]{:S(2)}) collective-permute-start(f32[136,128]{1,0:T(8,128)S(1)} %get-tuple-element.11), channel_id=1, source_target_pairs={{0,224},{32,0},{64,32},{96,64},{128,96},{160,128},{192,160},{224,1... | collective-permute-start | bytes 208904 | tf_op jit(solution)/shard_map/ppermute | solution.py:197
  61.9 1.2 %collective-permute-start.5 = (f32[136,128]{1,0:T(8,128)S(1)}, f32[136,128]{1,0:T(8,128)S(1)}, u32[]{:S(2)}, u32[]{:S(2)}) collective-permute-start(f32[136,128]{1,0:T(8,128)S(1)} %get-tuple-element.12), channel_id=1, source_target_pairs={{0,192},{32,224},{64,0},{96,32},{128,64},{160,96},{192,128},{224,1... | collective-permute-start | bytes 208904 | tf_op jit(solution)/shard_map/ppermute | solution.py:197
  63.1 0.5 broadcast.332
  63.6 0.7 reduce.5
  64.3 0.1 all_to_all.10
  64.4 0.7 copy.18
  65.1 4.9 %all-to-all-start.1 = ((f32[2,32,1]{0,2,1:T(1,128)}), f32[2,32,1]{0,2,1:T(1,128)S(1)}, u32[]{:S(2)}, u32[]{:S(2)}) async-start(f32[2,32,1]{0,2,1:T(1,128)} %copy.18), calls=%async_computation.1 | async-start | bytes 32768 | tf_op jit(solution)/shard_map/all_to_all | solution.py:186
  70.0 0.2 collective-permute-start.4
  70.2 4.8 %collective-permute-start.3 = (f32[136,128]{1,0:T(8,128)S(1)}, f32[136,128]{1,0:T(8,128)S(1)}, u32[]{:S(2)}, u32[]{:S(2)}) collective-permute-start(f32[136,128]{1,0:T(8,128)S(1)} %get-tuple-element.14), channel_id=1, source_target_pairs={{0,128},{32,160},{64,192},{96,224},{128,0},{160,32},{192,64},{224,... | collective-permute-start | bytes 208904 | tf_op jit(solution)/shard_map/ppermute | solution.py:197
  75.0 0.0 collective-permute-start.2
  75.0 2.0 %all-to-all-done.1 = f32[2,32,1]{0,2,1:T(1,128)S(1)} async-done(((f32[2,32,1]{0,2,1:T(1,128)}), f32[2,32,1]{0,2,1:T(1,128)S(1)}, u32[]{:S(2)}, u32[]{:S(2)}) %all-to-all-start.1) | async-done | bytes 288 | tf_op jit(solution)/shard_map/all_to_all | solution.py:186
  77.0 0.1 copy.19
  77.0 0.1 reshape.276
  77.1 0.7 gather_fusion
  77.8 0.0 collective-permute-done.6
  77.8 1.3 %collective-permute-start.1 = (f32[136,128]{1,0:T(8,128)S(1)}, f32[136,128]{1,0:T(8,128)S(1)}, u32[]{:S(2)}, u32[]{:S(2)}) collective-permute-start(f32[136,128]{1,0:T(8,128)S(1)} %get-tuple-element.16), channel_id=1, source_target_pairs={{0,64},{32,96},{64,128},{96,160},{128,192},{160,224},{192,0},{224,... | collective-permute-start | bytes 208904 | tf_op jit(solution)/shard_map/ppermute | solution.py:197
  79.1 0.0 collective-permute-done.5
  79.1 0.4 collective-permute-start
  79.5 0.5 and_select_fusion
  80.0 0.0 collective-permute-done.4
  80.0 0.0 collective-permute-done.3
  80.0 2.0 %collective-permute-done.2 = f32[136,128]{1,0:T(8,128)S(1)} collective-permute-done((f32[136,128]{1,0:T(8,128)S(1)}, f32[136,128]{1,0:T(8,128)S(1)}, u32[]{:S(2)}, u32[]{:S(2)}) %collective-permute-start.2) | collective-permute-done | bytes 69664 | tf_op jit(solution)/shard_map/ppermute | solution.py:197
  82.0 5.0 %collective-permute-done.1 = f32[136,128]{1,0:T(8,128)S(1)} collective-permute-done((f32[136,128]{1,0:T(8,128)S(1)}, f32[136,128]{1,0:T(8,128)S(1)}, u32[]{:S(2)}, u32[]{:S(2)}) %collective-permute-start.1) | collective-permute-done | bytes 69664 | tf_op jit(solution)/shard_map/ppermute | solution.py:197
  87.0 1.8 %collective-permute-done = f32[136,128]{1,0:T(8,128)S(1)} collective-permute-done((f32[136,128]{1,0:T(8,128)S(1)}, f32[136,128]{1,0:T(8,128)S(1)}, u32[]{:S(2)}, u32[]{:S(2)}) %collective-permute-start) | collective-permute-done | bytes 69664 | tf_op jit(solution)/shard_map/ppermute | solution.py:197
  88.8 0.4 convolution_bitcast_fusion
  89.1 1.0 %fusion.3 = f32[32,8,256]{2,1,0:T(8,128)} fusion(f32[136,256,1]{1,0,2:T(8,128)S(1)} %convolution_bitcast_fusion, f32[8,136]{1,0:T(8,128)S(1)} %mul.47, f32[32,136]{1,0:T(8,128)S(1)} %mul.44), kind=kOutput, calls=%fused_computation.7 | convolution fusion | flops 53512192 | bytes 423168 | tf_op jit(solution)/shard_map/dot_general | solution.py:205
  (8 shorter events, 0.1 us)
Async XLA Ops:
  7.1 8.8 %copy-start = (bf16[1,48,16384]{2,1,0:T(8,128)(2,1)S(1)}, bf16[1,48,16384]{2,1,0:T(8,128)(2,1)}, u32[]{:S(2)}) copy-start(bf16[1,48,16384]{2,1,0:T(8,128)(2,1)} %param.10) | copy-start | bytes 4718596
  7.1 37.3 %all-to-all-start = ((bf16[2,32,16512]{2,0,1:T(2,128)(2,1)}), bf16[2,32,16512]{2,0,1:T(2,128)(2,1)}, u32[]{:S(2)}, u32[]{:S(2)}) async-start(bf16[2,32,16512]{2,0,1:T(2,128)(2,1)} %copy.15), calls=%async_computation | async-start | bytes 4227072 | tf_op jit(solution)/shard_map/all_to_all | solution.py:177
  16.9 29.4 %copy-start.1 = (f32[8,48]{1,0:T(8,128)S(1)}, f32[8,48]{1,0:T(8,128)}, u32[]{:S(2)}) copy-start(f32[8,48]{1,0:T(8,128)} %gain_ref.1) | copy-start | bytes 4612
  56.3 21.5 %collective-permute-start.6 = (f32[136,128]{1,0:T(8,128)S(1)}, f32[136,128]{1,0:T(8,128)S(1)}, u32[]{:S(2)}, u32[]{:S(2)}) collective-permute-start(f32[136,128]{1,0:T(8,128)S(1)} %get-tuple-element.11), channel_id=1, source_target_pairs={{0,224},{32,0},{64,32},{96,64},{128,96},{160,128},{192,160},{224,1... | collective-permute-start | bytes 208904 | tf_op jit(solution)/shard_map/ppermute | solution.py:197
  61.9 17.2 %collective-permute-start.5 = (f32[136,128]{1,0:T(8,128)S(1)}, f32[136,128]{1,0:T(8,128)S(1)}, u32[]{:S(2)}, u32[]{:S(2)}) collective-permute-start(f32[136,128]{1,0:T(8,128)S(1)} %get-tuple-element.12), channel_id=1, source_target_pairs={{0,192},{32,224},{64,0},{96,32},{128,64},{160,96},{192,128},{224,1... | collective-permute-start | bytes 208904 | tf_op jit(solution)/shard_map/ppermute | solution.py:197
  65.1 11.9 %all-to-all-start.1 = ((f32[2,32,1]{0,2,1:T(1,128)}), f32[2,32,1]{0,2,1:T(1,128)S(1)}, u32[]{:S(2)}, u32[]{:S(2)}) async-start(f32[2,32,1]{0,2,1:T(1,128)} %copy.18), calls=%async_computation.1 | async-start | bytes 32768 | tf_op jit(solution)/shard_map/all_to_all | solution.py:186
  70.0 10.0 %collective-permute-start.4 = (f32[136,128]{1,0:T(8,128)S(1)}, f32[136,128]{1,0:T(8,128)S(1)}, u32[]{:S(2)}, u32[]{:S(2)}) collective-permute-start(f32[136,128]{1,0:T(8,128)S(1)} %get-tuple-element.13), channel_id=1, source_target_pairs={{0,160},{32,192},{64,224},{96,0},{128,32},{160,64},{192,96},{224,1... | collective-permute-start | bytes 208904 | tf_op jit(solution)/shard_map/ppermute | solution.py:197
  70.2 9.8 %collective-permute-start.3 = (f32[136,128]{1,0:T(8,128)S(1)}, f32[136,128]{1,0:T(8,128)S(1)}, u32[]{:S(2)}, u32[]{:S(2)}) collective-permute-start(f32[136,128]{1,0:T(8,128)S(1)} %get-tuple-element.14), channel_id=1, source_target_pairs={{0,128},{32,160},{64,192},{96,224},{128,0},{160,32},{192,64},{224,... | collective-permute-start | bytes 208904 | tf_op jit(solution)/shard_map/ppermute | solution.py:197
  75.0 7.0 %collective-permute-start.2 = (f32[136,128]{1,0:T(8,128)S(1)}, f32[136,128]{1,0:T(8,128)S(1)}, u32[]{:S(2)}, u32[]{:S(2)}) collective-permute-start(f32[136,128]{1,0:T(8,128)S(1)} %get-tuple-element.15), channel_id=1, source_target_pairs={{0,96},{32,128},{64,160},{96,192},{128,224},{160,0},{192,32},{224,... | collective-permute-start | bytes 208904 | tf_op jit(solution)/shard_map/ppermute | solution.py:197
  77.8 9.1 %collective-permute-start.1 = (f32[136,128]{1,0:T(8,128)S(1)}, f32[136,128]{1,0:T(8,128)S(1)}, u32[]{:S(2)}, u32[]{:S(2)}) collective-permute-start(f32[136,128]{1,0:T(8,128)S(1)} %get-tuple-element.16), channel_id=1, source_target_pairs={{0,64},{32,96},{64,128},{96,160},{128,192},{160,224},{192,0},{224,... | collective-permute-start | bytes 208904 | tf_op jit(solution)/shard_map/ppermute | solution.py:197
  79.1 9.7 %collective-permute-start = (f32[136,128]{1,0:T(8,128)S(1)}, f32[136,128]{1,0:T(8,128)S(1)}, u32[]{:S(2)}, u32[]{:S(2)}) collective-permute-start(f32[136,128]{1,0:T(8,128)S(1)} %get-tuple-element.10), channel_id=1, source_target_pairs={{0,32},{32,64},{64,96},{96,128},{128,160},{160,192},{192,224},{224... | collective-permute-start | bytes 208904 | tf_op jit(solution)/shard_map/ppermute | solution.py:197

commit v17 on v11

--- a/solution.py
+++ b/solution.py
@@ -87,11 +87,11 @@
     gain_hi = gain.astype(jnp.bfloat16)
     gain_lo = (gain - gain_hi.astype(jnp.float32)).astype(jnp.bfloat16)
     depth = gain.shape[0]
+    stacked = jnp.concatenate([gain_hi, gain_lo], axis=0)
     for t in range(9):
         weights = jnp.exp(scores[t] - evidence).astype(jnp.bfloat16)
-        mixed = jnp.dot(gain_hi, weights, preferred_element_type=jnp.float32) + jnp.dot(
-            gain_lo, weights, preferred_element_type=jnp.float32
-        )
+        pair = jnp.dot(stacked, weights, preferred_element_type=jnp.float32)
+        mixed = pair[0:depth] + pair[depth:2 * depth]
         mixed_hi = mixed.astype(jnp.bfloat16).astype(jnp.float32)
         v_ref[t, 0:depth] = mixed_hi
         v_ref[t, depth:2 * depth] = mixed - mixed_hi

time: 90.4 us -> 90.4 us (level)
  no operation moved by 1% of the time
where the time goes in v17:
time: 90.4 us; the launch traced here: 90.1 us
  waiting for transfers between devices  37.9 us (42%)
  starting transfers between devices  27.5 us (30%)
  Pallas kernels  9.76 us (11%)
  local copies, waits for them, and re-layouts  8.04 us (9%)
  matrix products  3.25 us (4%)
  other arithmetic  2.73 us (3%)
    all_to_all x1, waiting for transfers between devices, on_device(): lax.all_to_all(outgoing, 'dev', split_axis=1, concat_axis=1, tiled=True)  27.5 us
    ppermute x7, starting transfers between devices, on_device(): mine = mine + lax.ppermute(part, 'grp', pairs)  13.8 us
    pallas_call x1, Pallas kernels, class_pass(): pl.pallas_call(functools.partial(class_kernel, pix, groups), out_shape=(j...  9.76 us
    all_to_all x1, starting transfers between devices, on_device(): lax.all_to_all(outgoing, 'dev', split_axis=1, concat_axis=1, tiled=True)  8.77 us
    ppermute x7, waiting for transfers between devices, on_device(): mine = mine + lax.ppermute(part, 'grp', pairs)  8.63 us
    all_to_all x1, starting transfers between devices, on_device(): lax.all_to_all(stacked, 'dev', split_axis=1, concat_axis=1, tiled=True)  4.91 us
    reshape x1, local copies, waits for them, and re-layouts, on_device(): outgoing = outgoing.reshape(slot_depth, sources, owned_classes * width)  2.95 us
    dot_general x1, matrix products, on_device(): jnp.dot(placing, carried, preferred_element_type=jnp.float32)  1.91 us
  transfers between devices with their start and end apart: 9, of which 5 were waited for; matrix products, arithmetic and copies ran while one was open for 5% of the time, Pallas kernels for 0%

profile of v17, /device:TPU:1, one launch (start us, length us, event | category | flops | bytes accessed | tf_op | source)
XLA Modules:
  0.0 90.1 jit_solution(1345444025238833094)
XLA Ops:
  0.6 0.9 %convert_reduce_fusion.1 = (s32[32]{0:T(128)S(1)}, s32[32]{0:T(128)S(1)}) fusion(s32[32]{0:T(128)} %bitcast.51, s32[32]{0:T(128)} %param.9), kind=kLoop, calls=%fused_computation.44 | loop fusion | flops 8128 | bytes 512 | tf_op jit(solution)/shard_map/reduce_sum | solution.py:172
  1.6 0.7 broadcast_in_dim.86
  2.3 1.9 %convolution_convert_fusion = bf16[64,16512]{1,0:T(8,128)(2,1)S(1)} fusion(bf16[32,128]{1,0:T(8,128)(2,1)S(1)} %broadcast_in_dim.86, bf16[32,16384]{1,0:T(8,128)(2,1)} %param.6, s32[32]{0:T(128)S(1)} %get-tuple-element.9), kind=kOutput, calls=%fused_computation.1 | convolution fusion | flops 70805504 | bytes 3170432 | tf_op jit(solution)/shard_map/dot_general | solution.py:181
  4.2 2.9 %copy.15 = bf16[2,32,16512]{2,0,1:T(2,128)(2,1)} copy(bf16[2,32,16512]{2,1,0:T(8,128)(2,1)S(1)} %bitcast.49) | data formatting | bytes 4227072 | tf_op jit(solution)/shard_map/reshape | solution.py:182
  7.1 0.0 copy-start
  7.1 8.8 %all-to-all-start = ((bf16[2,32,16512]{2,0,1:T(2,128)(2,1)}), bf16[2,32,16512]{2,0,1:T(2,128)(2,1)}, u32[]{:S(2)}, u32[]{:S(2)}) async-start(bf16[2,32,16512]{2,0,1:T(2,128)(2,1)} %copy.15), calls=%async_computation | async-start | bytes 4227072 | tf_op jit(solution)/shard_map/all_to_all | solution.py:183
  16.0 0.0 copy-done
  16.0 0.4 multiply_reduce_fusion
  16.4 0.1 copy.17.energy_ref
  16.5 0.1 mul.46
  16.6 0.1 mul.47
  16.7 0.1 add_select_fusion
  16.8 0.1 mul.44
  16.9 0.0 copy-start.1
  16.9 27.5 %all-to-all-done = bf16[2,32,16512]{2,0,1:T(2,128)(2,1)} async-done(((bf16[2,32,16512]{2,0,1:T(2,128)(2,1)}), bf16[2,32,16512]{2,0,1:T(2,128)(2,1)}, u32[]{:S(2)}, u32[]{:S(2)}) %all-to-all-start) | async-done | bytes 2113568 | tf_op jit(solution)/shard_map/all_to_all | solution.py:183
  44.5 1.8 %copy.16 = bf16[2,32,16512]{2,1,0:T(8,128)(2,1)S(1)} copy(bf16[2,32,16512]{2,0,1:T(2,128)(2,1)} %all-to-all-done) | data formatting | bytes 4227072 | tf_op jit(solution)/shard_map/all_to_all | solution.py:183
  46.3 0.1 convert_reduce_fusion
  46.4 0.0 copy-done.1
  46.4 9.8 %shard_map.77 = (f32[8,136,128]{2,1,0:T(8,128)S(1)}, f32[1,64]{1,0:T(1,128)S(1)}) custom-call(bf16[64,16512]{1,0:T(8,128)(2,1)S(1)} %bitcast.46, bf16[48,16384]{1,0:T(8,128)(2,1)S(1)} %bitcast.47, f32[1,64]{1,0:T(1,128)S(1)} %bitcast.48, f32[48,1]{1,0:T(8,128)S(1)} %copy.17.energy_ref, f32[8,48]{1,0:T(8,128)S(1)} %copy-done.1), custom_call_target="tpu_custom_call" | custom-call | flops 1207959552 | bytes 4210688 | tf_op jit(solution)/shard_map/pallas_call | solution.py:138
  56.1 0.1 dynamic-slice_bitcast_fusion.6
  56.2 5.7 %collective-permute-start.6 = (f32[136,128]{1,0:T(8,128)S(1)}, f32[136,128]{1,0:T(8,128)S(1)}, u32[]{:S(2)}, u32[]{:S(2)}) collective-permute-start(f32[136,128]{1,0:T(8,128)S(1)} %get-tuple-element.11), channel_id=1, source_target_pairs={{0,224},{32,0},{64,32},{96,64},{128,96},{160,128},{192,160},{224,1... | collective-permute-start | bytes 208904 | tf_op jit(solution)/shard_map/ppermute | solution.py:203
  61.9 1.2 %collective-permute-start.5 = (f32[136,128]{1,0:T(8,128)S(1)}, f32[136,128]{1,0:T(8,128)S(1)}, u32[]{:S(2)}, u32[]{:S(2)}) collective-permute-start(f32[136,128]{1,0:T(8,128)S(1)} %get-tuple-element.12), channel_id=1, source_target_pairs={{0,192},{32,224},{64,0},{96,32},{128,64},{160,96},{192,128},{224,1... | collective-permute-start | bytes 208904 | tf_op jit(solution)/shard_map/ppermute | solution.py:203
  63.0 0.5 broadcast.332
  63.5 0.7 reduce.5
  64.2 0.1 all_to_all.10
  64.3 0.7 copy.18
  65.0 4.9 %all-to-all-start.1 = ((f32[2,32,1]{0,2,1:T(1,128)}), f32[2,32,1]{0,2,1:T(1,128)S(1)}, u32[]{:S(2)}, u32[]{:S(2)}) async-start(f32[2,32,1]{0,2,1:T(1,128)} %copy.18), calls=%async_computation.1 | async-start | bytes 32768 | tf_op jit(solution)/shard_map/all_to_all | solution.py:192
  69.9 0.4 collective-permute-start.4
  70.3 4.8 %collective-permute-start.3 = (f32[136,128]{1,0:T(8,128)S(1)}, f32[136,128]{1,0:T(8,128)S(1)}, u32[]{:S(2)}, u32[]{:S(2)}) collective-permute-start(f32[136,128]{1,0:T(8,128)S(1)} %get-tuple-element.14), channel_id=1, source_target_pairs={{0,128},{32,160},{64,192},{96,224},{128,0},{160,32},{192,64},{224,... | collective-permute-start | bytes 208904 | tf_op jit(solution)/shard_map/ppermute | solution.py:203
  75.1 0.0 collective-permute-start.2
  75.1 1.8 %all-to-all-done.1 = f32[2,32,1]{0,2,1:T(1,128)S(1)} async-done(((f32[2,32,1]{0,2,1:T(1,128)}), f32[2,32,1]{0,2,1:T(1,128)S(1)}, u32[]{:S(2)}, u32[]{:S(2)}) %all-to-all-start.1) | async-done | bytes 288 | tf_op jit(solution)/shard_map/all_to_all | solution.py:192
  76.9 0.1 copy.19
  77.0 0.1 reshape.276
  77.0 0.7 gather_fusion
  77.7 0.0 collective-permute-done.6
  77.8 1.3 %collective-permute-start.1 = (f32[136,128]{1,0:T(8,128)S(1)}, f32[136,128]{1,0:T(8,128)S(1)}, u32[]{:S(2)}, u32[]{:S(2)}) collective-permute-start(f32[136,128]{1,0:T(8,128)S(1)} %get-tuple-element.16), channel_id=1, source_target_pairs={{0,64},{32,96},{64,128},{96,160},{128,192},{160,224},{192,0},{224,... | collective-permute-start | bytes 208904 | tf_op jit(solution)/shard_map/ppermute | solution.py:203
  79.0 0.0 collective-permute-done.5
  79.0 0.6 collective-permute-start
  79.6 0.5 and_select_fusion
  80.1 0.0 collective-permute-done.4
  80.1 0.0 collective-permute-done.3
  80.1 2.0 %collective-permute-done.2 = f32[136,128]{1,0:T(8,128)S(1)} collective-permute-done((f32[136,128]{1,0:T(8,128)S(1)}, f32[136,128]{1,0:T(8,128)S(1)}, u32[]{:S(2)}, u32[]{:S(2)}) %collective-permute-start.2) | collective-permute-done | bytes 69664 | tf_op jit(solution)/shard_map/ppermute | solution.py:203
  82.1 4.9 %collective-permute-done.1 = f32[136,128]{1,0:T(8,128)S(1)} collective-permute-done((f32[136,128]{1,0:T(8,128)S(1)}, f32[136,128]{1,0:T(8,128)S(1)}, u32[]{:S(2)}, u32[]{:S(2)}) %collective-permute-start.1) | collective-permute-done | bytes 69664 | tf_op jit(solution)/shard_map/ppermute | solution.py:203
  87.0 1.7 %collective-permute-done = f32[136,128]{1,0:T(8,128)S(1)} collective-permute-done((f32[136,128]{1,0:T(8,128)S(1)}, f32[136,128]{1,0:T(8,128)S(1)}, u32[]{:S(2)}, u32[]{:S(2)}) %collective-permute-start) | collective-permute-done | bytes 69664 | tf_op jit(solution)/shard_map/ppermute | solution.py:203
  88.7 0.4 convolution_bitcast_fusion
  89.1 1.0 %fusion.3 = f32[32,8,256]{2,1,0:T(8,128)} fusion(f32[136,256,1]{1,0,2:T(8,128)S(1)} %convolution_bitcast_fusion, f32[8,136]{1,0:T(8,128)S(1)} %mul.47, f32[32,136]{1,0:T(8,128)S(1)} %mul.44), kind=kOutput, calls=%fused_computation.7 | convolution fusion | flops 53512192 | bytes 423168 | tf_op jit(solution)/shard_map/dot_general | solution.py:211
  (8 shorter events, 0.1 us)
Async XLA Ops:
  7.1 8.8 %copy-start = (bf16[1,48,16384]{2,1,0:T(8,128)(2,1)S(1)}, bf16[1,48,16384]{2,1,0:T(8,128)(2,1)}, u32[]{:S(2)}) copy-start(bf16[1,48,16384]{2,1,0:T(8,128)(2,1)} %param.10) | copy-start | bytes 4718596
  7.1 37.3 %all-to-all-start = ((bf16[2,32,16512]{2,0,1:T(2,128)(2,1)}), bf16[2,32,16512]{2,0,1:T(2,128)(2,1)}, u32[]{:S(2)}, u32[]{:S(2)}) async-start(bf16[2,32,16512]{2,0,1:T(2,128)(2,1)} %copy.15), calls=%async_computation | async-start | bytes 4227072 | tf_op jit(solution)/shard_map/all_to_all | solution.py:183
  16.9 29.4 %copy-start.1 = (f32[8,48]{1,0:T(8,128)S(1)}, f32[8,48]{1,0:T(8,128)}, u32[]{:S(2)}) copy-start(f32[8,48]{1,0:T(8,128)} %gain_ref.1) | copy-start | bytes 4612
  56.2 21.5 %collective-permute-start.6 = (f32[136,128]{1,0:T(8,128)S(1)}, f32[136,128]{1,0:T(8,128)S(1)}, u32[]{:S(2)}, u32[]{:S(2)}) collective-permute-start(f32[136,128]{1,0:T(8,128)S(1)} %get-tuple-element.11), channel_id=1, source_target_pairs={{0,224},{32,0},{64,32},{96,64},{128,96},{160,128},{192,160},{224,1... | collective-permute-start | bytes 208904 | tf_op jit(solution)/shard_map/ppermute | solution.py:203
  61.9 17.2 %collective-permute-start.5 = (f32[136,128]{1,0:T(8,128)S(1)}, f32[136,128]{1,0:T(8,128)S(1)}, u32[]{:S(2)}, u32[]{:S(2)}) collective-permute-start(f32[136,128]{1,0:T(8,128)S(1)} %get-tuple-element.12), channel_id=1, source_target_pairs={{0,192},{32,224},{64,0},{96,32},{128,64},{160,96},{192,128},{224,1... | collective-permute-start | bytes 208904 | tf_op jit(solution)/shard_map/ppermute | solution.py:203
  65.0 11.9 %all-to-all-start.1 = ((f32[2,32,1]{0,2,1:T(1,128)}), f32[2,32,1]{0,2,1:T(1,128)S(1)}, u32[]{:S(2)}, u32[]{:S(2)}) async-start(f32[2,32,1]{0,2,1:T(1,128)} %copy.18), calls=%async_computation.1 | async-start | bytes 32768 | tf_op jit(solution)/shard_map/all_to_all | solution.py:192
  69.9 10.2 %collective-permute-start.4 = (f32[136,128]{1,0:T(8,128)S(1)}, f32[136,128]{1,0:T(8,128)S(1)}, u32[]{:S(2)}, u32[]{:S(2)}) collective-permute-start(f32[136,128]{1,0:T(8,128)S(1)} %get-tuple-element.13), channel_id=1, source_target_pairs={{0,160},{32,192},{64,224},{96,0},{128,32},{160,64},{192,96},{224,1... | collective-permute-start | bytes 208904 | tf_op jit(solution)/shard_map/ppermute | solution.py:203
  70.3 9.8 %collective-permute-start.3 = (f32[136,128]{1,0:T(8,128)S(1)}, f32[136,128]{1,0:T(8,128)S(1)}, u32[]{:S(2)}, u32[]{:S(2)}) collective-permute-start(f32[136,128]{1,0:T(8,128)S(1)} %get-tuple-element.14), channel_id=1, source_target_pairs={{0,128},{32,160},{64,192},{96,224},{128,0},{160,32},{192,64},{224,... | collective-permute-start | bytes 208904 | tf_op jit(solution)/shard_map/ppermute | solution.py:203
  75.1 7.0 %collective-permute-start.2 = (f32[136,128]{1,0:T(8,128)S(1)}, f32[136,128]{1,0:T(8,128)S(1)}, u32[]{:S(2)}, u32[]{:S(2)}) collective-permute-start(f32[136,128]{1,0:T(8,128)S(1)} %get-tuple-element.15), channel_id=1, source_target_pairs={{0,96},{32,128},{64,160},{96,192},{128,224},{160,0},{192,32},{224,... | collective-permute-start | bytes 208904 | tf_op jit(solution)/shard_map/ppermute | solution.py:203
  77.8 9.2 %collective-permute-start.1 = (f32[136,128]{1,0:T(8,128)S(1)}, f32[136,128]{1,0:T(8,128)S(1)}, u32[]{:S(2)}, u32[]{:S(2)}) collective-permute-start(f32[136,128]{1,0:T(8,128)S(1)} %get-tuple-element.16), channel_id=1, source_target_pairs={{0,64},{32,96},{64,128},{96,160},{128,192},{160,224},{192,0},{224,... | collective-permute-start | bytes 208904 | tf_op jit(solution)/shard_map/ppermute | solution.py:203
  79.0 9.7 %collective-permute-start = (f32[136,128]{1,0:T(8,128)S(1)}, f32[136,128]{1,0:T(8,128)S(1)}, u32[]{:S(2)}, u32[]{:S(2)}) collective-permute-start(f32[136,128]{1,0:T(8,128)S(1)} %get-tuple-element.10), channel_id=1, source_target_pairs={{0,32},{32,64},{64,96},{96,128},{128,160},{160,192},{192,224},{224... | collective-permute-start | bytes 208904 | tf_op jit(solution)/shard_map/ppermute | solution.py:203
